TPU v7x, 512 devices: a whole 4x4x16 slice. The times are simulated.
512 devices in a mesh: mpo: 8 (over y, core), sec: 64 (over x, z).
Axes of the slice: x: 4, y: 4, z: 16, core: 2. Of those that a mesh axis runs over, the one named last changes fastest.
Arguments:
- theta: bfloat16 [16, 1024, 1024], P(None, 'sec'), may hold values from -6 to 6
- env_left: bfloat16 [24, 16384, 1024], P('mpo', 'sec'), may hold values from -0.1875 to 0.1875
- env_right: bfloat16 [24, 16384, 1024], P('mpo', 'sec'), may hold values from -0.0390625 to 0.0390625
- mpo_core: float32 [24, 24], replicated, may hold values from -1.25 to 1.25
- sector_sizes: int32 [16], replicated, may hold values from 1 to 1024, 12288 in all
Outputs:
- applied: bfloat16 [1024, 16384], P('mpo', 'sec')
Inputs may be any that keep to these rules, and one draw needn't show every extreme that they name: `sector_sizes`: one sector has exactly 1024 states in use; the sizes sum to 12288.
All inputs are finite; a program needn't handle non-finite values.
Results may differ from a plain program's by a relative error of at most 0.0058.
Values may be sent and summed in bfloat16 or wider, within the bound.
No kernel may reach another device: no remote copies, remote signals or barrier semaphores. Data moves between devices by JAX's collectives and lax.ppermute only.
A program may use at most 64 MiB of HBM per device.

v0:
```python
import jax
import jax.numpy as jnp
from jax import lax
from jax.sharding import PartitionSpec as P

G = 4


def swapped(array, axis, stride):
    return lax.ppermute(array, axis, [(i, i ^ 1 << stride) for i in range(lax.axis_size(axis))])


def on_device(theta, env_left, env_right, mpo_core, sector_sizes):
    sectors = theta.shape[0]
    rows_local = theta.shape[1]
    width = theta.shape[2]
    local_w = env_left.shape[0]
    slab = env_left.shape[1]
    sec_place = lax.axis_index("sec")
    sector = sec_place // G
    block_pos = sec_place % G
    live_size = jnp.sum(jnp.where(jnp.arange(sectors, dtype=jnp.int32) == sector, sector_sizes, 0))
    bit_count = G.bit_length() - 1
    spread = jnp.broadcast_to(theta[:, None], (sectors, G, rows_local, width))
    spread = spread.reshape(sectors * G, rows_local, width)
    sector_block = lax.all_to_all(spread, "sec", split_axis=0, concat_axis=1, tiled=True)[0]
    positions = jnp.arange(width, dtype=jnp.int32)
    keep_row = positions < live_size
    sector_block = jnp.where(
        keep_row[:, None] & keep_row[None, :], sector_block, jnp.zeros_like(sector_block)
    )
    product = jnp.einsum(
        "akm,mn->akn", env_left, sector_block, preferred_element_type=jnp.float32
    ).astype(jnp.bfloat16)
    own_start = lax.axis_index("mpo") * local_w
    core_cols = lax.dynamic_slice_in_dim(mpo_core, own_start, local_w, 1)
    mixed = jnp.einsum(
        "ab,akn->bkn",
        core_cols,
        lax.all_gather(product, "mpo", axis=0, tiled=True).astype(jnp.float32),
        precision=lax.Precision.HIGHEST,
    ).astype(jnp.bfloat16)
    for bit_index in range(bit_count):
        partner = swapped(mixed, "sec", bit_index)
        upper_half = sec_place >> bit_index & 1 == 1
        mixed = jnp.where(
            upper_half, jnp.concatenate([partner, mixed], 1), jnp.concatenate([mixed, partner], 1)
        )
    col_keep = block_pos * slab + jnp.arange(slab, dtype=jnp.int32) < live_size
    sector_term = jnp.einsum("bil,bjl->ij", mixed, env_right, preferred_element_type=jnp.float32)
    row_keep = (
        jnp.arange(lax.axis_size("mpo") * (width // lax.axis_size("mpo")), dtype=jnp.int32)
        < live_size
    )
    result = lax.psum_scatter(
        jnp.where(row_keep[:, None] & col_keep[None, :], sector_term, jnp.zeros_like(sector_term)),
        "mpo",
        scatter_dimension=0,
        tiled=True,
    )
    return result.astype(jnp.bfloat16)


def solution(mesh):
    return jax.shard_map(
        on_device,
        mesh=mesh,
        in_specs=(P(None, "sec", None), P("mpo", "sec", None), P("mpo", "sec", None), P(), P()),
        out_specs=P("mpo", "sec"),
        check_vma=False,
    )
```

profile of v0, /device:TPU:2, one launch (start us, length us, event | category | flops | bytes accessed | tf_op | source)
XLA Modules:
  0.0 477.4 jit_solution(1534336615428155424)
XLA Ops:
  6.5 2.8 broadcast_in_dim.11
  9.3 18.8 %all-to-all-start = ((bf16[64,16,1024]{2,1,0:T(8,128)(2,1)}), bf16[64,16,1024]{2,1,0:T(8,128)(2,1)}, u32[]{:S(2)}, u32[]{:S(2)}) async-start(bf16[64,16,1024]{2,1,0:T(8,128)(2,1)} %bitcast.21), calls=%async_computation | async-start | bytes 4194304 | tf_op jit(solution)/shard_map/all_to_all | solution.py:26
  28.2 0.6 fusion.27
  28.8 0.6 iota_compare_fusion
  29.5 95.7 %all-to-all-done = bf16[64,16,1024]{2,1,0:T(8,128)(2,1)} async-done(((bf16[64,16,1024]{2,1,0:T(8,128)(2,1)}), bf16[64,16,1024]{2,1,0:T(8,128)(2,1)}, u32[]{:S(2)}, u32[]{:S(2)}) %all-to-all-start) | async-done | bytes 2097184 | tf_op jit(solution)/shard_map/all_to_all | solution.py:26
  125.2 4.9 %fusion.15 = bf16[3,256,1024]{2,1,0:T(8,128)(2,1)} fusion(bf16[3,256,1024]{2,1,0:T(8,128)(2,1)S(1)} %copy-done, bf16[1024,1024]{1,0:T(8,128)(2,1)} %bitcast.2, pred[1024]{0:T(1024)(128)(4,1)S(1)} %iota_compare_fusion), kind=kOutput, calls=%fused_computation.13 | convolution fusion | flops 1613496320 | bytes 5243904 | tf_op jit(solution)/shard_map/akm,mn->akn/dot_general | solution.py:32
  130.2 69.3 %all-gather.2.cloned.1.call-done = bf16[24,256,1024]{2,1,0:T(8,128)(2,1)} async-done(((bf16[3,256,1024]{2,1,0:T(8,128)(2,1)}), bf16[24,256,1024]{2,1,0:T(8,128)(2,1)}) %all-gather.2.cloned.1.call-update) | async-done | bytes 12582928 | tf_op jit(solution)/shard_map/all_gather | solution.py:40
  199.5 17.3 %fusion.9 = bf16[3,256,1024]{2,0,1:T(4,128)(2,1)S(1)} fusion(bf16[24,256,1024]{2,1,0:T(8,128)(2,1)} %all-gather.2.cloned.1.call-done, f32[24,24]{1,0:T(8,128)S(1)} %copy-done.5, s32[]{:T(128)S(6)} %select_n.47), kind=kOutput, calls=%fused_computation.11 | convolution fusion | flops 227278848 | bytes 14158084 | tf_op jit(solution)/shard_map/ab,akn->bkn/dot_general | solution.py:37
  216.8 1.3 copy-done.3
  218.1 1.8 copy.10
  219.8 3.6 collective-permute-start
  223.5 35.0 %collective-permute-done = bf16[3,256,1024]{2,1,0:T(8,128)(2,1)S(1)} collective-permute-done((bf16[3,256,1024]{2,1,0:T(8,128)(2,1)}, bf16[3,256,1024]{2,1,0:T(8,128)(2,1)S(1)}, u32[]{:S(2)}, u32[]{:S(2)}) %collective-permute-start) | collective-permute-done | bytes 1572896 | tf_op jit(solution)/shard_map/ppermute | solution.py:10
  258.5 1.4 copy.11
  259.9 4.7 maximum_select_fusion.1
  264.5 1.9 copy-done.1
  266.5 2.9 copy.13
  269.4 4.4 collective-permute-start.1
  273.9 0.8 add_compare_fusion
  274.7 134.6 %collective-permute-done.1 = bf16[3,512,1024]{2,1,0:T(8,128)(2,1)} collective-permute-done((bf16[3,512,1024]{2,1,0:T(8,128)(2,1)}, bf16[3,512,1024]{2,1,0:T(8,128)(2,1)}, u32[]{:S(2)}, u32[]{:S(2)}) %collective-permute-start.1) | collective-permute-done | bytes 3145760 | tf_op jit(solution)/shard_map/ppermute | solution.py:10
  409.3 4.6 copy.14
  413.9 9.3 %maximum_select_fusion = bf16[3,1024,1024]{2,0,1:T(4,128)(2,1)S(1)} fusion(bf16[3,512,1024]{2,0,1:T(4,128)(2,1)S(1)} %copy-done.2, bf16[3,512,1024]{2,0,1:T(4,128)(2,1)S(1)} %copy.14, pred[]{:T(512)S(6)} %eq.16), kind=kLoop, calls=%fused_computation.2 | loop fusion | flops 9437184 | bytes 12582913 | tf_op jit(solution)/shard_map/jit(_where)/select_n | solution.py:46
  423.3 5.2 %fusion.21 = f32[1024,256]{1,0:T(8,128)} fusion(bf16[3,256,1024]{2,1,0:T(8,128)(2,1)S(1)} %copy-done.6, bf16[3,1024,1024]{2,0,1:T(4,128)(2,1)S(1)} %maximum_select_fusion, pred[256]{0:T(512)(128)(4,1)S(1)} %add_compare_fusion, pred[1024]{0:T(1024)(128)(4,1)S(1)} %iota_compare_fusion), kind=kOutput, calls=%fused_computation.15 | convolution fusion | flops 1611137024 | bytes 8914176 | tf_op jit(solution)/shard_map/bil,bjl->ij/dot_general | solution.py:50
  428.5 40.5 %reduce-scatter.2.cloned.1.call-done = f32[128,256]{1,0:T(8,128)} async-done(((f32[1024,256]{1,0:T(8,128)}), f32[128,256]{1,0:T(8,128)}) %reduce-scatter.2.cloned.1.call-update) | async-done | bytes 131088 | tf_op jit(solution)/shard_map/reduce_scatter | solution.py:55
  469.0 1.5 convert_element_type.16
  (18 shorter events, 0.1 us)
Async XLA Ops:
  6.5 118.7 %copy-start = (bf16[3,256,1024]{2,1,0:T(8,128)(2,1)S(1)}, bf16[3,256,1024]{2,1,0:T(8,128)(2,1)}, u32[]{:S(2)}) copy-start(bf16[3,256,1024]{2,1,0:T(8,128)(2,1)} %param.6) | copy-start | bytes 4718596
  6.5 21.7 %copy-start.7 = (s32[16]{0:T(128)S(1)}, s32[16]{0:T(128)}, u32[]{:S(2)}) copy-start(s32[16]{0:T(128)} %param.9) | copy-start | bytes 196
  9.3 115.9 %all-to-all-start = ((bf16[64,16,1024]{2,1,0:T(8,128)(2,1)}), bf16[64,16,1024]{2,1,0:T(8,128)(2,1)}, u32[]{:S(2)}, u32[]{:S(2)}) async-start(bf16[64,16,1024]{2,1,0:T(8,128)(2,1)} %bitcast.21), calls=%async_computation | async-start | bytes 4194304 | tf_op jit(solution)/shard_map/all_to_all | solution.py:26
  28.1 171.4 %all-gather.2.cloned.1.call-start = ((), (), s32[]{:S(2)}) async-start(), calls=%async_computation.2 | async-start | bytes 14155776 | tf_op jit(solution)/shard_map/all_gather | solution.py:40
  125.2 74.3 %copy-start.5 = (f32[24,24]{1,0:T(8,128)S(1)}, f32[24,24]{1,0:T(8,128)}, u32[]{:S(2)}) copy-start(f32[24,24]{1,0:T(8,128)} %param.8) | copy-start | bytes 6916
  130.1 338.9 %reduce-scatter.2.cloned.1.call-start = ((), (), s32[]{:S(2)}) async-start(), calls=%async_computation.3 | async-start | bytes 1179648 | tf_op jit(solution)/shard_map/reduce_scatter | solution.py:55
  216.8 1.3 copy-start.3
  219.8 38.6 %collective-permute-start = (bf16[3,256,1024]{2,1,0:T(8,128)(2,1)}, bf16[3,256,1024]{2,1,0:T(8,128)(2,1)S(1)}, u32[]{:S(2)}, u32[]{:S(2)}) collective-permute-start(bf16[3,256,1024]{2,1,0:T(8,128)(2,1)} %copy.10), channel_id=1, source_target_pairs={{0,1},{1,0},{2,3},{3,2},{4,5},{5,4},{6,7},{7,6},{8,9},{9,8},{10,11... | collective-permute-start | bytes 4718600 | tf_op jit(solution)/shard_map/ppermute | solution.py:10
  223.5 36.4 %copy-start.4 = (bf16[3,256,1024]{2,0,1:T(4,128)(2,1)S(1)}, bf16[3,256,1024]{2,0,1:T(4,128)(2,1)}, u32[]{:S(2)}) copy-start(bf16[3,256,1024]{2,0,1:T(4,128)(2,1)} %copy-done.3) | copy-start | bytes 4718596
  264.5 2.0 copy-start.1
  269.4 139.9 %collective-permute-start.1 = (bf16[3,512,1024]{2,1,0:T(8,128)(2,1)}, bf16[3,512,1024]{2,1,0:T(8,128)(2,1)}, u32[]{:S(2)}, u32[]{:S(2)}) collective-permute-start(bf16[3,512,1024]{2,1,0:T(8,128)(2,1)} %copy.13), channel_id=1, source_target_pairs={{0,2},{1,3},{2,0},{3,1},{4,6},{5,7},{6,4},{7,5},{8,10},{9,11},{10,... | collective-permute-start | bytes 9437192 | tf_op jit(solution)/shard_map/ppermute | solution.py:10
  273.9 140.0 %copy-start.2 = (bf16[3,512,1024]{2,0,1:T(4,128)(2,1)S(1)}, bf16[3,512,1024]{2,0,1:T(4,128)(2,1)}, u32[]{:S(2)}) copy-start(bf16[3,512,1024]{2,0,1:T(4,128)(2,1)} %copy-done.1) | copy-start | bytes 9437188
  413.9 9.3 %copy-start.6 = (bf16[3,256,1024]{2,1,0:T(8,128)(2,1)S(1)}, bf16[3,256,1024]{2,1,0:T(8,128)(2,1)}, u32[]{:S(2)}) copy-start(bf16[3,256,1024]{2,1,0:T(8,128)(2,1)} %param.7) | copy-start | bytes 4718596
Sparse Core Ops, SparseCore 0:
  130.3 69.1 all-gather.1
  428.7 40.3 reduce-scatter.1
where the time goes:
time: 478 us; the launch traced here: 477 us
  waiting for transfers between devices  375 us (78%)
  matrix products  27.4 us (6%)
  starting transfers between devices  27 us (6%)
  other arithmetic  17.6 us (4%)
  local copies, waits for them, and re-layouts  16.7 us (3%)
  between operations  13.6 us (3%)
    ppermute x2, waiting for transfers between devices, swapped(): lax.ppermute(array, axis, [(i, i ^ 1 << stride) for i in range(lax.axis_s...  170 us
    all_to_all x1, waiting for transfers between devices, on_device(): lax.all_to_all(spread, 'sec', split_axis=0, concat_axis=1, tiled=True)[0]  95.7 us
    all_gather x1, waiting for transfers between devices, on_device(): lax.all_gather(product, 'mpo', axis=0, tiled=True).astype(jnp.float32)  69.3 us
    reduce_scatter x1, waiting for transfers between devices, on_device(): lax.psum_scatter(jnp.where(row_keep[:, None] & col_keep[None, :], sector_...  40.5 us
    all_to_all x1, starting transfers between devices, on_device(): lax.all_to_all(spread, 'sec', split_axis=0, concat_axis=1, tiled=True)[0]  18.8 us
    dot_general x1, matrix products, on_device(): jnp.einsum('ab,akn->bkn', core_cols, lax.all_gather(product, 'mpo', axis=...  17.3 us
    select_n x2, other arithmetic, on_device(): jnp.where(upper_half, jnp.concatenate([partner, mixed], 1), jnp.concatena...  14 us
  transfers between devices with their start and end apart: 5, of which 5 were waited for; matrix products, arithmetic and copies ran while one was open for 0% of the time, Pallas kernels for 0%

commit v1 on v0

v1 whole, which is shorter than its diff:
```python
import jax
import jax.numpy as jnp
import numpy as np
from jax import lax
from jax.sharding import Mesh, PartitionSpec as P

G = 4


def on_device(theta, env_left, env_right, mpo_core, sector_sizes):
    sectors, rows_local, width = theta.shape
    local_w, slab, _ = env_left.shape
    n_mpo = lax.axis_size("mpo")
    n_sg = lax.axis_size("sg")
    mm = lax.axis_index("mpo")
    sector = lax.axis_index("sg")
    k = lax.axis_index("k")
    live_size = jnp.sum(jnp.where(jnp.arange(sectors, dtype=jnp.int32) == sector, sector_sizes, 0))

    right_all = lax.all_gather(env_right, "k", axis=1, tiled=True)

    per = rows_local // n_mpo
    sel = lax.dynamic_slice_in_dim(theta, mm * per, per, axis=1)
    spread = jnp.broadcast_to(sel[:, None], (sectors, G, per, width)).reshape(sectors * G, per, width)
    part = lax.all_to_all(spread, ("sg", "k"), 0, 0, tiled=True)
    everyone = jnp.broadcast_to(part[None], (n_mpo,) + part.shape)
    gathered = lax.all_to_all(everyone, "mpo", 0, 0, tiled=True)
    block = jnp.transpose(gathered, (1, 0, 2, 3)).reshape(width, width)
    positions = jnp.arange(width, dtype=jnp.int32)
    keep = positions < live_size
    block = jnp.where(keep[:, None] & keep[None, :], block, jnp.zeros_like(block))

    product = jnp.einsum(
        "akm,mn->akn", env_left, block, preferred_element_type=jnp.float32
    ).astype(jnp.bfloat16)
    sub = slab // n_mpo
    product = product.reshape(local_w, n_mpo, sub, width)
    all_a = lax.all_to_all(product, "mpo", 1, 0, tiled=True).reshape(local_w * n_mpo, sub, width)
    mixed = jnp.einsum(
        "ab,akn->bkn", mpo_core, all_a.astype(jnp.float32), precision=lax.Precision.HIGHEST
    ).astype(jnp.bfloat16)
    mixed = mixed.reshape(n_mpo, local_w, sub, width)
    own_b = lax.all_to_all(mixed, "mpo", 0, 0, tiled=False)

    term = jnp.einsum(
        "mbil,bjl->mij", own_b, right_all, preferred_element_type=jnp.float32
    ).reshape(slab, width)
    row_keep = k * slab + jnp.arange(slab, dtype=jnp.int32) < live_size
    term = jnp.where(row_keep[:, None] & keep[None, :], term, jnp.zeros_like(term))
    halves = n_mpo // G
    term = term.reshape(halves, slab // halves, G, slab)
    term = jnp.transpose(term, (2, 0, 1, 3)).reshape(n_mpo, slab // halves, slab)
    result = lax.psum_scatter(term, "mpo", scatter_dimension=0, tiled=True)
    result = result.reshape(slab // halves, slab).astype(jnp.bfloat16)

    pairs = []
    for src_m in range(n_mpo):
        for g in range(n_sg):
            for kk in range(G):
                dst_m = halves * kk + src_m % halves
                dst_k = src_m // halves
                pairs.append(((src_m * n_sg + g) * G + kk, (dst_m * n_sg + g) * G + dst_k))
    return lax.ppermute(result, ("mpo", "sg", "k"), pairs)


def solution(mesh):
    devices = np.asarray(mesh.devices)
    n_mpo, n_sec = devices.shape
    grid = Mesh(devices.reshape(n_mpo, n_sec // G, G), ("mpo", "sg", "k"))
    sec = ("sg", "k")
    return jax.shard_map(
        on_device,
        mesh=grid,
        in_specs=(P(None, sec, None), P("mpo", sec, None), P("mpo", sec, None), P(), P()),
        out_specs=P("mpo", sec),
        check_vma=False,
    )
```

time: 478 us -> 211 us (0.44)
  the two profiles are of different devices: /device:TPU:2 before, /device:TPU:96 now
where the time goes in v1:
time: 211 us
  waiting for transfers between devices  88 us (42%)
  blocking collectives  64.9 us (31%)
  local copies, waits for them, and re-layouts  18.7 us (9%)
  between operations  13.5 us (6%)
  matrix products  11.3 us (5%)
  starting transfers between devices  10.3 us (5%)
  other arithmetic  3.97 us (2%)
    all_to_all x1, blocking collectives, on_device(): part = lax.all_to_all(spread, ('sg', 'k'), 0, 0, tiled=True)  40.9 us
    reduce_scatter x1, waiting for transfers between devices, on_device(): result = lax.psum_scatter(term, 'mpo', scatter_dimension=0, tiled=True)  33.3 us
    all_to_all x1, waiting for transfers between devices, on_device(): gathered = lax.all_to_all(everyone, 'mpo', 0, 0, tiled=True)  26 us
    all_to_all x1, blocking collectives, on_device(): lax.all_to_all(product, 'mpo', 1, 0, tiled=True)  24 us
    all_to_all x1, waiting for transfers between devices, on_device(): own_b = lax.all_to_all(mixed, 'mpo', 0, 0, tiled=False)  19.9 us
    ppermute x1, waiting for transfers between devices, on_device(): return lax.ppermute(result, ('mpo', 'sg', 'k'), pairs)  8.14 us
    dot_general x1, matrix products, on_device(): jnp.einsum('mbil,bjl->mij', own_b, right_all, preferred_element_type=jnp....  5.6 us
    transpose x1, local copies, waits for them, and re-layouts, on_device(): block = jnp.transpose(gathered, (1, 0, 2, 3)).reshape(width, width)  5.26 us
  transfers between devices with their start and end apart: 5, of which 4 were waited for; matrix products, arithmetic and copies ran while one was open for 11% of the time, Pallas kernels for 0%

profile of v1, /device:TPU:96, one launch (start us, length us, event | category | flops | bytes accessed | tf_op | source)
XLA Modules:
  0.0 210.6 jit_solution(7886671997857918927)
XLA Ops:
  6.5 0.7 all-gather.2.cloned.1.call-update
  7.3 1.0 constant_dynamic-slice_fusion
  8.4 40.9 %all_to_all.30 = bf16[64,2,1024]{2,1,0:T(2,128)(2,1)S(1)} all-to-all(bf16[64,2,1024]{2,1,0:T(2,128)(2,1)S(1)} %bitcast.39), channel_id=1, replica_groups=mesh['mpo'=8,'sg'=16,'k'=4] {'sg','k'}, dimensions={0} | all-to-all | bytes 524288 | tf_op jit(solution)/shard_map/all_to_all | solution.py:25
  49.3 2.4 %broadcast_in_dim.14 = bf16[8,64,2,1024]{3,2,1,0:T(2,128)(2,1)} broadcast(bf16[64,2,1024]{2,1,0:T(2,128)(2,1)S(1)} %all_to_all.30), dimensions={1,2,3} | broadcast | bytes 2359296 | tf_op jit(solution)/shard_map/broadcast_in_dim | solution.py:26
  51.8 4.6 %all-to-all-start.1 = ((bf16[8,64,2,1024]{3,2,1,0:T(2,128)(2,1)}), bf16[8,64,2,1024]{3,2,1,0:T(2,128)(2,1)}, u32[]{:S(2)}, u32[]{:S(2)}) async-start(bf16[8,64,2,1024]{3,2,1,0:T(2,128)(2,1)} %broadcast_in_dim.14), calls=%async_computation.1 | async-start | bytes 4194304 | tf_op jit(solution)/shard_map/all_to_all | solution.py:27
  57.0 0.6 iota_compare_fusion
  57.6 26.0 %all-to-all-done.1 = bf16[8,64,2,1024]{3,2,1,0:T(2,128)(2,1)} async-done(((bf16[8,64,2,1024]{3,2,1,0:T(2,128)(2,1)}), bf16[8,64,2,1024]{3,2,1,0:T(2,128)(2,1)}, u32[]{:S(2)}, u32[]{:S(2)}) %all-to-all-start.1) | async-done | bytes 2097184 | tf_op jit(solution)/shard_map/all_to_all | solution.py:27
  83.6 5.3 %copy.20 = bf16[64,8,2,1024]{3,2,1,0:T(2,128)(2,1)} copy(bf16[64,8,2,1024]{3,2,0,1:T(2,128)(2,1)} %bitcast.1) | data formatting | bytes 4194304 | tf_op jit(solution)/shard_map/transpose | solution.py:28
  88.9 4.2 %reshape.53 = bf16[1024,1024]{1,0:T(8,128)(2,1)} reshape(bf16[64,8,2,1024]{3,2,1,0:T(2,128)(2,1)} %copy.20) | data formatting | bytes 4194304 | tf_op jit(solution)/shard_map/reshape | solution.py:28
  93.1 3.7 %fusion.7 = bf16[1024,3,256]{0,2,1:T(8,128)(2,1)S(1)} fusion(bf16[3,256,1024]{2,1,0:T(8,128)(2,1)S(1)} %copy-done, bf16[1024,1024]{1,0:T(8,128)(2,1)} %reshape.53, pred[1024]{0:T(1024)(128)(4,1)S(1)} %iota_compare_fusion), kind=kOutput, calls=%fused_computation.7 | convolution fusion | flops 1613496320 | bytes 5243904 | tf_op jit(solution)/shard_map/akm,mn->akn/dot_general | solution.py:33
  96.9 24.0 %all_to_all.31 = bf16[3,8,32,1024]{3,2,0,1:T(8,128)(2,1)S(1)} all-to-all(bf16[3,8,32,1024]{3,2,0,1:T(8,128)(2,1)S(1)} %copy.21), channel_id=1, replica_groups=mesh['mpo'=8,'sg'=16,'k'=4] {'mpo'}, dimensions={1} | all-to-all | bytes 3145728 | tf_op jit(solution)/shard_map/all_to_all | solution.py:38
  121.0 2.0 fusion.11
  122.9 2.0 copy.24
  124.9 3.6 %all-to-all-start.3 = ((bf16[8,3,32,1024]{3,2,1,0:T(8,128)(2,1)}), bf16[8,3,32,1024]{3,2,1,0:T(8,128)(2,1)S(1)}, u32[]{:S(2)}, u32[]{:S(2)}) async-start(bf16[8,3,32,1024]{3,2,1,0:T(8,128)(2,1)} %bitcast.10), calls=%async_computation.3 | async-start | bytes 3145728 | tf_op jit(solution)/shard_map/all_to_all | solution.py:43
  128.7 0.7 add_compare_fusion.1
  129.4 0.7 add_compare_fusion
  130.1 19.9 %all-to-all-done.3 = bf16[8,3,32,1024]{3,2,1,0:T(8,128)(2,1)S(1)} async-done(((bf16[8,3,32,1024]{3,2,1,0:T(8,128)(2,1)}), bf16[8,3,32,1024]{3,2,1,0:T(8,128)(2,1)S(1)}, u32[]{:S(2)}, u32[]{:S(2)}) %all-to-all-start.3) | async-done | bytes 1572896 | tf_op jit(solution)/shard_map/all_to_all | solution.py:43
  150.0 5.6 %fusion.14 = f32[8,32,1024]{2,1,0:T(8,128)} fusion(bf16[8,3,32,1024]{3,2,1,0:T(8,128)(2,1)S(1)} %all-to-all-done.3, bf16[3,1024,1024]{2,1,0:T(8,128)(2,1)} %all-gather.2.cloned.1.call-done), kind=kOutput, calls=%fused_computation.11 | convolution fusion | flops 1610612736 | bytes 8912896 | tf_op jit(solution)/shard_map/mbil,bjl->mij/dot_general | solution.py:45
  155.6 1.7 reshape.57
  157.8 1.2 copy.25
  158.9 33.3 %reduce-scatter.2.cloned.1.call-done = f32[1,128,256]{2,1,0:T(8,128)} async-done(((f32[8,128,256]{2,1,0:T(8,128)}), f32[1,128,256]{2,1,0:T(8,128)}) %reduce-scatter.2.cloned.1.call-update) | async-done | bytes 131088 | tf_op jit(solution)/shard_map/reduce_scatter | solution.py:53
  192.2 0.9 convert_bitcast_fusion
  193.1 1.9 collective-permute-start
  195.0 8.1 %collective-permute-done = bf16[128,256]{1,0:T(8,128)(2,1)S(1)} collective-permute-done((bf16[128,256]{1,0:T(8,128)(2,1)S(1)}, bf16[128,256]{1,0:T(8,128)(2,1)S(1)}, u32[]{:S(2)}, u32[]{:S(2)}) %collective-permute-start) | collective-permute-done | bytes 65568 | tf_op jit(solution)/shard_map/ppermute | solution.py:63
  (15 shorter events, 2.2 us)
Async XLA Ops:
  6.5 86.5 %copy-start = (bf16[3,256,1024]{2,1,0:T(8,128)(2,1)S(1)}, bf16[3,256,1024]{2,1,0:T(8,128)(2,1)}, u32[]{:S(2)}) copy-start(bf16[3,256,1024]{2,1,0:T(8,128)(2,1)} %param.6) | copy-start | bytes 4718596
  6.5 143.4 %all-gather.2.cloned.1.call-start = ((), (), s32[]{:S(2)}) async-start(), calls=%async_computation.5 | async-start | bytes 7864320 | tf_op jit(solution)/shard_map/all_gather | solution.py:20
  51.8 4.6 %copy-start.2 = (s32[16]{0:T(128)S(1)}, s32[16]{0:T(128)}, u32[]{:S(2)}) copy-start(s32[16]{0:T(128)} %param.9) | copy-start | bytes 196
  51.8 31.8 %all-to-all-start.1 = ((bf16[8,64,2,1024]{3,2,1,0:T(2,128)(2,1)}), bf16[8,64,2,1024]{3,2,1,0:T(2,128)(2,1)}, u32[]{:S(2)}, u32[]{:S(2)}) async-start(bf16[8,64,2,1024]{3,2,1,0:T(2,128)(2,1)} %broadcast_in_dim.14), calls=%async_computation.1 | async-start | bytes 4194304 | tf_op jit(solution)/shard_map/all_to_all | solution.py:27
  96.9 24.0 %copy-start.1 = (f32[24,24]{1,0:T(8,128)S(1)}, f32[24,24]{1,0:T(8,128)}, u32[]{:S(2)}) copy-start(f32[24,24]{1,0:T(8,128)} %param.8) | copy-start | bytes 6916
  124.9 25.1 %all-to-all-start.3 = ((bf16[8,3,32,1024]{3,2,1,0:T(8,128)(2,1)}), bf16[8,3,32,1024]{3,2,1,0:T(8,128)(2,1)S(1)}, u32[]{:S(2)}, u32[]{:S(2)}) async-start(bf16[8,3,32,1024]{3,2,1,0:T(8,128)(2,1)} %bitcast.10), calls=%async_computation.3 | async-start | bytes 3145728 | tf_op jit(solution)/shard_map/all_to_all | solution.py:43
  128.5 63.7 %reduce-scatter.2.cloned.1.call-start = ((), (), s32[]{:S(2)}) async-start(), calls=%async_computation.6 | async-start | bytes 1179648 | tf_op jit(solution)/shard_map/reduce_scatter | solution.py:53
  193.1 10.1 %collective-permute-start = (bf16[128,256]{1,0:T(8,128)(2,1)S(1)}, bf16[128,256]{1,0:T(8,128)(2,1)S(1)}, u32[]{:S(2)}, u32[]{:S(2)}) collective-permute-start(bf16[128,256]{1,0:T(8,128)(2,1)S(1)} %convert_bitcast_fusion), channel_id=1, source_target_pairs={{0,0},{1,128},{2,256},{3,384},{4,4},{5,132},{6,260},{7,388},{8,8},... | collective-permute-start | bytes 196616 | tf_op jit(solution)/shard_map/ppermute | solution.py:63
Sparse Core Ops, SparseCore 0:
  9.4 129.7 all-gather.1
  159.1 33.0 reduce-scatter.1

commit v2 on v1

--- a/solution.py
+++ b/solution.py
@@ -19,13 +19,12 @@
 
     right_all = lax.all_gather(env_right, "k", axis=1, tiled=True)
 
-    per = rows_local // n_mpo
-    sel = lax.dynamic_slice_in_dim(theta, mm * per, per, axis=1)
-    spread = jnp.broadcast_to(sel[:, None], (sectors, G, per, width)).reshape(sectors * G, per, width)
-    part = lax.all_to_all(spread, ("sg", "k"), 0, 0, tiled=True)
+    per = width // n_mpo
+    sel = lax.dynamic_slice_in_dim(theta, mm * per, per, axis=2)
+    spread = jnp.broadcast_to(sel[:, None], (sectors, G, rows_local, per)).reshape(sectors * G, rows_local, per)
+    part = lax.all_to_all(spread, ("sg", "k"), 0, 0, tiled=True).reshape(width, per)
     everyone = jnp.broadcast_to(part[None], (n_mpo,) + part.shape)
-    gathered = lax.all_to_all(everyone, "mpo", 0, 0, tiled=True)
-    block = jnp.transpose(gathered, (1, 0, 2, 3)).reshape(width, width)
+    block = lax.all_to_all(everyone, "mpo", 0, 2, tiled=True).reshape(width, width)
     positions = jnp.arange(width, dtype=jnp.int32)
     keep = positions < live_size
     block = jnp.where(keep[:, None] & keep[None, :], block, jnp.zeros_like(block))
@@ -50,8 +49,7 @@
     halves = n_mpo // G
     term = term.reshape(halves, slab // halves, G, slab)
     term = jnp.transpose(term, (2, 0, 1, 3)).reshape(n_mpo, slab // halves, slab)
-    result = lax.psum_scatter(term, "mpo", scatter_dimension=0, tiled=True)
-    result = result.reshape(slab // halves, slab).astype(jnp.bfloat16)
+    result = jnp.sum(lax.all_to_all(term, "mpo", 0, 0, tiled=False), axis=0).astype(jnp.bfloat16)
 
     pairs = []
     for src_m in range(n_mpo):

time: 211 us -> 189 us (0.90)
  the two profiles are of different devices: /device:TPU:96 before, /device:TPU:70 now
where the time goes in v2:
time: 189 us; the launch traced here: 188 us
  blocking collectives  85 us (45%)
  waiting for transfers between devices  54.4 us (29%)
  between operations  13.5 us (7%)
  matrix products  11 us (6%)
  local copies, waits for them, and re-layouts  10.9 us (6%)
  starting transfers between devices  10.1 us (5%)
  other arithmetic  2.97 us (2%)
    all_to_all x1, blocking collectives, on_device(): lax.all_to_all(spread, ('sg', 'k'), 0, 0, tiled=True).reshape(width, per)  42.6 us
    all_to_all x1, waiting for transfers between devices, on_device(): lax.all_to_all(everyone, 'mpo', 0, 2, tiled=True).reshape(width, width)  26 us
    all_to_all x1, blocking collectives, on_device(): lax.all_to_all(product, 'mpo', 1, 0, tiled=True)  24 us
    all_to_all x1, waiting for transfers between devices, on_device(): own_b = lax.all_to_all(mixed, 'mpo', 0, 0, tiled=False)  20.1 us
    all_to_all x1, blocking collectives, on_device(): lax.all_to_all(term, 'mpo', 0, 0, tiled=False)  18.4 us
    ppermute x1, waiting for transfers between devices, on_device(): return lax.ppermute(result, ('mpo', 'sg', 'k'), pairs)  7.53 us
    dot_general x1, matrix products, on_device(): jnp.einsum('mbil,bjl->mij', own_b, right_all, preferred_element_type=jnp....  5.6 us
    all_to_all x1, starting transfers between devices, on_device(): lax.all_to_all(everyone, 'mpo', 0, 2, tiled=True).reshape(width, width)  4.65 us
  transfers between devices with their start and end apart: 4, of which 3 were waited for; matrix products, arithmetic and copies ran while one was open for 9% of the time, Pallas kernels for 0%

profile of v2, /device:TPU:70, one launch (start us, length us, event | category | flops | bytes accessed | tf_op | source)
XLA Modules:
  0.0 188.0 jit_solution(10658091259161488896)
XLA Ops:
  6.5 0.7 all-gather.2.cloned.1.call-update
  7.3 0.8 constant_dynamic-slice_fusion
  8.2 42.6 %all_to_all.45 = bf16[64,16,128]{2,1,0:T(8,128)(2,1)S(1)} all-to-all(bf16[64,16,128]{2,1,0:T(8,128)(2,1)S(1)} %bitcast.44), channel_id=1, replica_groups=mesh['mpo'=8,'sg'=16,'k'=4] {'sg','k'}, dimensions={0} | all-to-all | bytes 524288 | tf_op jit(solution)/shard_map/all_to_all | solution.py:25
  50.8 1.6 broadcast_in_dim.30
  52.4 4.6 %all-to-all-start.1 = ((bf16[8,1024,128]{2,1,0:T(8,128)(2,1)}), bf16[8,1024,128]{2,1,0:T(8,128)(2,1)}, u32[]{:S(2)}, u32[]{:S(2)}) async-start(bf16[8,1024,128]{2,1,0:T(8,128)(2,1)} %broadcast_in_dim.30), calls=%async_computation.1 | async-start | bytes 4194304 | tf_op jit(solution)/shard_map/all_to_all | solution.py:27
  57.0 0.6 fusion.19
  57.7 0.6 iota_compare_fusion
  58.3 26.0 %all-to-all-done.1 = bf16[8,1024,128]{2,1,0:T(8,128)(2,1)} async-done(((bf16[8,1024,128]{2,1,0:T(8,128)(2,1)}), bf16[8,1024,128]{2,1,0:T(8,128)(2,1)}, u32[]{:S(2)}, u32[]{:S(2)}) %all-to-all-start.1) | async-done | bytes 2097184 | tf_op jit(solution)/shard_map/all_to_all | solution.py:27
  84.3 3.9 %copy.19 = bf16[8,1024,128]{1,2,0:T(8,128)(2,1)} copy(bf16[8,1024,128]{2,1,0:T(8,128)(2,1)} %all-to-all-done.1) | data formatting | bytes 4194304 | tf_op jit(solution)/shard_map/all_to_all | solution.py:27
  88.2 3.5 %fusion.7 = bf16[1024,3,256]{0,2,1:T(8,128)(2,1)S(1)} fusion(bf16[3,256,1024]{2,1,0:T(8,128)(2,1)S(1)} %copy-done, bf16[1024,1024]{0,1:T(8,128)(2,1)} %bitcast.41, pred[1024]{0:T(1024)(128)(4,1)S(1)} %iota_compare_fusion), kind=kOutput, calls=%fused_computation.7 | convolution fusion | flops 1613496320 | bytes 5243904 | tf_op jit(solution)/shard_map/akm,mn->akn/dot_general | solution.py:32
  91.9 24.0 %all_to_all.46 = bf16[3,8,32,1024]{3,2,0,1:T(8,128)(2,1)S(1)} all-to-all(bf16[3,8,32,1024]{3,2,0,1:T(8,128)(2,1)S(1)} %copy.21), channel_id=1, replica_groups=mesh['mpo'=8,'sg'=16,'k'=4] {'mpo'}, dimensions={1} | all-to-all | bytes 3145728 | tf_op jit(solution)/shard_map/all_to_all | solution.py:37
  115.9 2.0 %fusion.11 = bf16[24,32,1024]{2,0,1:T(8,128)(2,1)S(1)} fusion(bf16[24,32,1024]{2,1,0:T(8,128)(2,1)S(1)} %bitcast.39, f32[24,24]{1,0:T(8,128)S(1)} %copy-done.1), kind=kOutput, calls=%fused_computation.10 | convolution fusion | flops 227278848 | bytes 3148032 | tf_op jit(solution)/shard_map/ab,akn->bkn/dot_general | solution.py:38
  117.9 2.0 %copy.24 = bf16[24,32,1024]{2,1,0:T(8,128)(2,1)} copy(bf16[24,32,1024]{2,0,1:T(8,128)(2,1)S(1)} %fusion.11) | data formatting | bytes 3145728 | tf_op jit(solution)/shard_map/convert_element_type | solution.py:40
  119.9 3.6 %all-to-all-start.3 = ((bf16[8,3,32,1024]{3,2,1,0:T(8,128)(2,1)}), bf16[8,3,32,1024]{3,2,1,0:T(8,128)(2,1)S(1)}, u32[]{:S(2)}, u32[]{:S(2)}) async-start(bf16[8,3,32,1024]{3,2,1,0:T(8,128)(2,1)} %bitcast.13), calls=%async_computation.3 | async-start | bytes 3145728 | tf_op jit(solution)/shard_map/all_to_all | solution.py:42
  123.5 0.7 add_compare_fusion.1
  124.2 0.7 add_compare_fusion
  124.8 20.1 %all-to-all-done.3 = bf16[8,3,32,1024]{3,2,1,0:T(8,128)(2,1)S(1)} async-done(((bf16[8,3,32,1024]{3,2,1,0:T(8,128)(2,1)}), bf16[8,3,32,1024]{3,2,1,0:T(8,128)(2,1)S(1)}, u32[]{:S(2)}, u32[]{:S(2)}) %all-to-all-start.3) | async-done | bytes 1572896 | tf_op jit(solution)/shard_map/all_to_all | solution.py:42
  145.0 5.6 %fusion.14 = f32[8,32,1024]{2,1,0:T(8,128)} fusion(bf16[8,3,32,1024]{3,2,1,0:T(8,128)(2,1)S(1)} %all-to-all-done.3, bf16[3,1024,1024]{2,1,0:T(8,128)(2,1)} %all-gather.2.cloned.1.call-done), kind=kOutput, calls=%fused_computation.11 | convolution fusion | flops 1610612736 | bytes 8912896 | tf_op jit(solution)/shard_map/mbil,bjl->mij/dot_general | solution.py:44
  150.6 1.7 reshape.56
  152.3 0.3 copy_select_fusion
  152.6 18.4 %all_to_all.47 = f32[8,128,256]{2,1,0:T(8,128)S(1)} all-to-all(f32[8,128,256]{2,1,0:T(8,128)S(1)} %bitcast.40), channel_id=1, replica_groups=mesh['mpo'=8,'sg'=16,'k'=4] {'mpo'}, dimensions={0} | all-to-all | bytes 2097152 | tf_op jit(solution)/shard_map/all_to_all | solution.py:52
  171.1 1.9 %collective-permute-start = (bf16[128,256]{1,0:T(8,128)(2,1)S(1)}, bf16[128,256]{1,0:T(8,128)(2,1)S(1)}, u32[]{:S(2)}, u32[]{:S(2)}) collective-permute-start(bf16[128,256]{1,0:T(8,128)(2,1)S(1)} %reduce_sum.19), channel_id=1, source_target_pairs={{0,0},{1,128},{2,256},{3,384},{4,4},{5,132},{6,260},{7,388},{8,8},... | collective-permute-start | bytes 196616 | tf_op jit(solution)/shard_map/ppermute | solution.py:61
  173.0 7.5 %collective-permute-done = bf16[128,256]{1,0:T(8,128)(2,1)S(1)} collective-permute-done((bf16[128,256]{1,0:T(8,128)(2,1)S(1)}, bf16[128,256]{1,0:T(8,128)(2,1)S(1)}, u32[]{:S(2)}, u32[]{:S(2)}) %collective-permute-start) | collective-permute-done | bytes 65568 | tf_op jit(solution)/shard_map/ppermute | solution.py:61
  180.5 0.6 copy.37
  (11 shorter events, 0.3 us)
Async XLA Ops:
  6.5 81.7 %copy-start = (bf16[3,256,1024]{2,1,0:T(8,128)(2,1)S(1)}, bf16[3,256,1024]{2,1,0:T(8,128)(2,1)}, u32[]{:S(2)}) copy-start(bf16[3,256,1024]{2,1,0:T(8,128)(2,1)} %param.6) | copy-start | bytes 4718596
  6.5 138.4 %all-gather.2.cloned.1.call-start = ((), (), s32[]{:S(2)}) async-start(), calls=%async_computation.5 | async-start | bytes 7864320 | tf_op jit(solution)/shard_map/all_gather | solution.py:20
  52.4 4.7 %copy-start.2 = (s32[16]{0:T(128)S(1)}, s32[16]{0:T(128)}, u32[]{:S(2)}) copy-start(s32[16]{0:T(128)} %param.9) | copy-start | bytes 196
  52.4 31.9 %all-to-all-start.1 = ((bf16[8,1024,128]{2,1,0:T(8,128)(2,1)}), bf16[8,1024,128]{2,1,0:T(8,128)(2,1)}, u32[]{:S(2)}, u32[]{:S(2)}) async-start(bf16[8,1024,128]{2,1,0:T(8,128)(2,1)} %broadcast_in_dim.30), calls=%async_computation.1 | async-start | bytes 4194304 | tf_op jit(solution)/shard_map/all_to_all | solution.py:27
  91.9 24.0 %copy-start.1 = (f32[24,24]{1,0:T(8,128)S(1)}, f32[24,24]{1,0:T(8,128)}, u32[]{:S(2)}) copy-start(f32[24,24]{1,0:T(8,128)} %param.8) | copy-start | bytes 6916
  119.9 25.1 %all-to-all-start.3 = ((bf16[8,3,32,1024]{3,2,1,0:T(8,128)(2,1)}), bf16[8,3,32,1024]{3,2,1,0:T(8,128)(2,1)S(1)}, u32[]{:S(2)}, u32[]{:S(2)}) async-start(bf16[8,3,32,1024]{3,2,1,0:T(8,128)(2,1)} %bitcast.13), calls=%async_computation.3 | async-start | bytes 3145728 | tf_op jit(solution)/shard_map/all_to_all | solution.py:42
  171.1 9.5 %collective-permute-start = (bf16[128,256]{1,0:T(8,128)(2,1)S(1)}, bf16[128,256]{1,0:T(8,128)(2,1)S(1)}, u32[]{:S(2)}, u32[]{:S(2)}) collective-permute-start(bf16[128,256]{1,0:T(8,128)(2,1)S(1)} %reduce_sum.19), channel_id=1, source_target_pairs={{0,0},{1,128},{2,256},{3,384},{4,4},{5,132},{6,260},{7,388},{8,8},... | collective-permute-start | bytes 196616 | tf_op jit(solution)/shard_map/ppermute | solution.py:61
Sparse Core Ops, SparseCore 0:
  9.4 131.1 all-gather.1

commit v3 on v2

--- a/solution.py
+++ b/solution.py
@@ -5,6 +5,23 @@
 from jax.sharding import Mesh, PartitionSpec as P
 
 G = 4
+
+
+def shifted(array, pairs):
+    return lax.ppermute(array, "k", pairs)
+
+
+def line_gather(block, k):
+    ups, downs = [block], [block]
+    for step in range(1, G):
+        ups.append(shifted(ups[-1], [(i, i + 1) for i in range(step - 1, G - 1)]))
+        downs.append(shifted(downs[-1], [(i + 1, i) for i in range(0, G - step)]))
+
+    def placed(kk):
+        parts = [ups[kk - p] if p <= kk else downs[p - kk] for p in range(G)]
+        return lambda: jnp.concatenate(parts, axis=1)
+
+    return lax.switch(k, [placed(kk) for kk in range(G)])
 
 
 def on_device(theta, env_left, env_right, mpo_core, sector_sizes):
@@ -17,7 +34,7 @@
     k = lax.axis_index("k")
     live_size = jnp.sum(jnp.where(jnp.arange(sectors, dtype=jnp.int32) == sector, sector_sizes, 0))
 
-    right_all = lax.all_gather(env_right, "k", axis=1, tiled=True)
+    right_all = line_gather(env_right, k)
 
     per = width // n_mpo
     sel = lax.dynamic_slice_in_dim(theta, mm * per, per, axis=2)

time: 189 us -> 206 us (1.090)
  the two profiles are of different devices: /device:TPU:70 before, /device:TPU:102 now
where the time goes in v3:
time: 206 us; the launch traced here: 205 us
  waiting for transfers between devices  88.5 us (43%)
  blocking collectives  55.4 us (27%)
  starting transfers between devices  27.1 us (13%)
  matrix products  12.9 us (6%)
  local copies, waits for them, and re-layouts  12.2 us (6%)
  other arithmetic  8.62 us (4%)
    ppermute x6, waiting for transfers between devices, shifted(): return lax.ppermute(array, 'k', pairs)  80.3 us
    all_to_all x1, blocking collectives, on_device(): lax.all_to_all(spread, ('sg', 'k'), 0, 0, tiled=True).reshape(width, per)  36 us
    all_to_all x1, blocking collectives, on_device(): lax.all_to_all(term, 'mpo', 0, 0, tiled=False)  19.4 us
    ppermute x6, starting transfers between devices, shifted(): return lax.ppermute(array, 'k', pairs)  12 us
    ppermute x1, waiting for transfers between devices, on_device(): return lax.ppermute(result, ('mpo', 'sg', 'k'), pairs)  8.14 us
    dot_general x1, matrix products, on_device(): jnp.einsum('mbil,bjl->mij', own_b, right_all, preferred_element_type=jnp....  6.09 us
    concatenate x1, other arithmetic, placed(): return lambda: jnp.concatenate(parts, axis=1)  5.66 us
    all_to_all x1, starting transfers between devices, on_device(): lax.all_to_all(everyone, 'mpo', 0, 2, tiled=True).reshape(width, width)  4.47 us
  transfers between devices with their start and end apart: 10, of which 5 were waited for; matrix products, arithmetic and copies ran while one was open for 11% of the time, Pallas kernels for 0%

profile of v3, /device:TPU:102, one launch (start us, length us, event | category | flops | bytes accessed | tf_op | source)
XLA Modules:
  0.0 204.9 jit_solution(15706306322189141015)
XLA Ops:
  1.1 36.0 %all_to_all.45 = bf16[64,16,128]{2,1,0:T(8,128)(2,1)S(1)} all-to-all(bf16[64,16,128]{2,1,0:T(8,128)(2,1)S(1)} %bitcast.44), channel_id=1, replica_groups=mesh['mpo'=8,'sg'=16,'k'=4] {'sg','k'}, dimensions={0} | all-to-all | bytes 524288 | tf_op jit(solution)/shard_map/all_to_all | solution.py:42
  37.0 1.6 broadcast_in_dim.30
  38.6 4.5 %all-to-all-start.1 = ((bf16[8,1024,128]{2,1,0:T(8,128)(2,1)}), bf16[8,1024,128]{2,1,0:T(8,128)(2,1)}, u32[]{:S(2)}, u32[]{:S(2)}) async-start(bf16[8,1024,128]{2,1,0:T(8,128)(2,1)} %broadcast_in_dim.30), calls=%async_computation.1 | async-start | bytes 4194304 | tf_op jit(solution)/shard_map/all_to_all | solution.py:44
  43.1 4.5 %collective-permute-start = (bf16[3,256,1024]{2,1,0:T(8,128)(2,1)S(1)}, bf16[3,256,1024]{2,1,0:T(8,128)(2,1)}, u32[]{:S(2)}, u32[]{:S(2)}) collective-permute-start(bf16[3,256,1024]{2,1,0:T(8,128)(2,1)S(1)} %copy-done.1), channel_id=1, source_target_pairs={{1,0},{2,1},{3,2},{5,4},{6,5},{7,6},{9,8},{10,9},{11,10},{13,12},{... | collective-permute-start | bytes 4718600 | tf_op jit(solution)/shard_map/ppermute | solution.py:11
  50.2 30.6 %collective-permute-done = bf16[3,256,1024]{2,1,0:T(8,128)(2,1)} collective-permute-done((bf16[3,256,1024]{2,1,0:T(8,128)(2,1)S(1)}, bf16[3,256,1024]{2,1,0:T(8,128)(2,1)}, u32[]{:S(2)}, u32[]{:S(2)}) %collective-permute-start) | collective-permute-done | bytes 1572896 | tf_op jit(solution)/shard_map/ppermute | solution.py:11
  80.7 1.9 collective-permute-start.1
  82.6 3.5 %collective-permute-done.3 = bf16[3,256,1024]{2,1,0:T(8,128)(2,1)} collective-permute-done((bf16[3,256,1024]{2,1,0:T(8,128)(2,1)S(1)}, bf16[3,256,1024]{2,1,0:T(8,128)(2,1)}, u32[]{:S(2)}, u32[]{:S(2)}) %collective-permute-start.3) | collective-permute-done | bytes 1572896 | tf_op jit(solution)/shard_map/ppermute | solution.py:11
  86.1 1.3 collective-permute-start.4
  87.4 3.9 %copy.19 = bf16[8,1024,128]{1,2,0:T(8,128)(2,1)} copy(bf16[8,1024,128]{2,1,0:T(8,128)(2,1)} %all-to-all-done.1) | data formatting | bytes 4194304 | tf_op jit(solution)/shard_map/all_to_all | solution.py:44
  91.3 3.5 %fusion.7 = bf16[1024,3,256]{0,2,1:T(8,128)(2,1)S(1)} fusion(bf16[3,256,1024]{2,1,0:T(8,128)(2,1)S(1)} %copy-done, bf16[1024,1024]{0,1:T(8,128)(2,1)} %bitcast.41, pred[1024]{0:T(1024)(128)(4,1)S(1)} %iota_compare_fusion), kind=kOutput, calls=%fused_computation.11 | convolution fusion | flops 1613496320 | bytes 5243904 | tf_op jit(solution)/shard_map/akm,mn->akn/dot_general | solution.py:49
  96.1 4.4 %all-to-all-start.2 = ((bf16[3,8,32,1024]{3,2,0,1:T(8,128)(2,1)}), bf16[3,8,32,1024]{3,2,0,1:T(8,128)(2,1)}, u32[]{:S(2)}, u32[]{:S(2)}) async-start(bf16[3,8,32,1024]{3,2,0,1:T(8,128)(2,1)} %copy.21), calls=%async_computation.2 | async-start | bytes 3145728 | tf_op jit(solution)/shard_map/all_to_all | solution.py:54
  100.5 1.8 collective-permute-start.2
  102.3 21.6 %collective-permute-done.4 = bf16[3,256,1024]{2,1,0:T(8,128)(2,1)} collective-permute-done((bf16[3,256,1024]{2,1,0:T(8,128)(2,1)}, bf16[3,256,1024]{2,1,0:T(8,128)(2,1)}, u32[]{:S(2)}, u32[]{:S(2)}) %collective-permute-start.4) | collective-permute-done | bytes 1572896 | tf_op jit(solution)/shard_map/ppermute | solution.py:11
  125.2 3.3 %fusion.11 = bf16[24,32,1024]{2,0,1:T(8,128)(2,1)S(1)} fusion(bf16[24,32,1024]{2,1,0:T(8,128)(2,1)} %bitcast.10, f32[24,24]{1,0:T(8,128)S(1)} %copy-done.2), kind=kOutput, calls=%fused_computation.14 | convolution fusion | flops 227278848 | bytes 3148032 | tf_op jit(solution)/shard_map/ab,akn->bkn/dot_general | solution.py:55
  128.6 2.0 copy.24
  130.6 4.3 %all-to-all-start.3 = ((bf16[8,3,32,1024]{3,2,1,0:T(8,128)(2,1)}), bf16[8,3,32,1024]{3,2,1,0:T(8,128)(2,1)}, u32[]{:S(2)}, u32[]{:S(2)}) async-start(bf16[8,3,32,1024]{3,2,1,0:T(8,128)(2,1)} %bitcast.39), calls=%async_computation.3 | async-start | bytes 3145728 | tf_op jit(solution)/shard_map/all_to_all | solution.py:59
  136.2 24.7 %collective-permute-done.5 = bf16[3,256,1024]{2,1,0:T(8,128)(2,1)} collective-permute-done((bf16[3,256,1024]{2,1,0:T(8,128)(2,1)}, bf16[3,256,1024]{2,1,0:T(8,128)(2,1)}, u32[]{:S(2)}, u32[]{:S(2)}) %collective-permute-start.5) | collective-permute-done | bytes 1572896 | tf_op jit(solution)/shard_map/ppermute | solution.py:11
  160.9 5.7 %conditional.1 = (bf16[3,1024,1024]{2,1,0:T(8,128)(2,1)}) conditional(s32[]{:T(128)} %clamp.3, (bf16[3,256,1024]{2,1,0:T(8,128)(2,1)S(1)}, bf16[3,256,1024]{2,1,0:T(8,128)(2,1)}, bf16[3,256,1024]{2,1,0:T(8,128)(2,1)}, bf16[3,256,1024]{2,1,0:T(8,128)(2,1)}) %tuple.25, (bf16[3,256,1024]{2,1,0:T(8,128)(2,1)}, ...), branch_computations={%region_1.2_spmd, %region_2.3_spmd, %region_3.4_spmd, %region_4.5_... | conditional | flops 25165824 | bytes 12582920 | solution.py:24
  160.9 5.7 %pad_maximum_fusion.3 = bf16[3,1024,1024]{2,1,0:T(8,128)(2,1)} fusion(bf16[3,256,1024]{2,1,0:T(8,128)(2,1)S(1)} %get-tuple-element.57, bf16[3,256,1024]{2,1,0:T(8,128)(2,1)} %get-tuple-element.56, bf16[3,256,1024]{2,1,0:T(8,128)(2,1)} %get-tuple-element.55, bf16[3,256,1024]{2,1,0:T(8,128)(2,1)} %get-tuple-element.54), kind=kLoop, calls=%fused_computation.3 | loop fusion | flops 25165824 | bytes 12582912 | tf_op jit(solution)/shard_map/cond/branch_3_fun/concatenate | solution.py:22
  166.6 6.1 %fusion.14 = f32[8,32,1024]{2,1,0:T(8,128)} fusion(bf16[8,3,32,1024]{3,2,1,0:T(8,128)(2,1)} %all-to-all-done.3, bf16[3,1024,1024]{2,1,0:T(8,128)(2,1)} %get-tuple-element.58), kind=kOutput, calls=%fused_computation.15 | convolution fusion | flops 1610612736 | bytes 8912896 | tf_op jit(solution)/shard_map/mbil,bjl->mij/dot_general | solution.py:61
  172.7 1.7 reshape.56
  174.7 19.4 %all_to_all.46 = f32[8,128,256]{2,1,0:T(8,128)S(1)} all-to-all(f32[8,128,256]{2,1,0:T(8,128)S(1)} %bitcast.40), channel_id=1, replica_groups=mesh['mpo'=8,'sg'=16,'k'=4] {'mpo'}, dimensions={0} | all-to-all | bytes 2097152 | tf_op jit(solution)/shard_map/all_to_all | solution.py:69
  194.2 1.9 collective-permute-start.6
  196.1 8.1 %collective-permute-done.6 = bf16[128,256]{1,0:T(8,128)(2,1)S(1)} collective-permute-done((bf16[128,256]{1,0:T(8,128)(2,1)S(1)}, bf16[128,256]{1,0:T(8,128)(2,1)S(1)}, u32[]{:S(2)}, u32[]{:S(2)}) %collective-permute-start.6) | collective-permute-done | bytes 65568 | tf_op jit(solution)/shard_map/ppermute | solution.py:78
  (25 shorter events, 8.5 us)
Async XLA Ops:
  0.0 91.3 %copy-start = (bf16[3,256,1024]{2,1,0:T(8,128)(2,1)S(1)}, bf16[3,256,1024]{2,1,0:T(8,128)(2,1)}, u32[]{:S(2)}) copy-start(bf16[3,256,1024]{2,1,0:T(8,128)(2,1)} %param.10) | copy-start | bytes 4718596
  0.0 43.1 %copy-start.1 = (bf16[3,256,1024]{2,1,0:T(8,128)(2,1)S(1)}, bf16[3,256,1024]{2,1,0:T(8,128)(2,1)}, u32[]{:S(2)}) copy-start(bf16[3,256,1024]{2,1,0:T(8,128)(2,1)} %param.11) | copy-start | bytes 4718596
  0.0 48.9 %copy-start.3 = (s32[16]{0:T(128)S(1)}, s32[16]{0:T(128)}, u32[]{:S(2)}) copy-start(s32[16]{0:T(128)} %param.13) | copy-start | bytes 196
  38.6 48.7 %all-to-all-start.1 = ((bf16[8,1024,128]{2,1,0:T(8,128)(2,1)}), bf16[8,1024,128]{2,1,0:T(8,128)(2,1)}, u32[]{:S(2)}, u32[]{:S(2)}) async-start(bf16[8,1024,128]{2,1,0:T(8,128)(2,1)} %broadcast_in_dim.30), calls=%async_computation.1 | async-start | bytes 4194304 | tf_op jit(solution)/shard_map/all_to_all | solution.py:44
  43.1 37.6 %collective-permute-start = (bf16[3,256,1024]{2,1,0:T(8,128)(2,1)S(1)}, bf16[3,256,1024]{2,1,0:T(8,128)(2,1)}, u32[]{:S(2)}, u32[]{:S(2)}) collective-permute-start(bf16[3,256,1024]{2,1,0:T(8,128)(2,1)S(1)} %copy-done.1), channel_id=1, source_target_pairs={{1,0},{2,1},{3,2},{5,4},{6,5},{7,6},{9,8},{10,9},{11,10},{13,12},{... | collective-permute-start | bytes 4718600 | tf_op jit(solution)/shard_map/ppermute | solution.py:11
  47.6 38.5 %collective-permute-start.3 = (bf16[3,256,1024]{2,1,0:T(8,128)(2,1)S(1)}, bf16[3,256,1024]{2,1,0:T(8,128)(2,1)}, u32[]{:S(2)}, u32[]{:S(2)}) collective-permute-start(bf16[3,256,1024]{2,1,0:T(8,128)(2,1)S(1)} %copy-done.1), channel_id=1, source_target_pairs={{0,1},{1,2},{2,3},{4,5},{5,6},{6,7},{8,9},{9,10},{10,11},{12,13},{... | collective-permute-start | bytes 4718600 | tf_op jit(solution)/shard_map/ppermute | solution.py:11
  80.7 19.8 %collective-permute-start.1 = (bf16[3,256,1024]{2,1,0:T(8,128)(2,1)}, bf16[3,256,1024]{2,1,0:T(8,128)(2,1)}, u32[]{:S(2)}, u32[]{:S(2)}) collective-permute-start(bf16[3,256,1024]{2,1,0:T(8,128)(2,1)} %collective-permute-done), channel_id=1, source_target_pairs={{1,0},{2,1},{5,4},{6,5},{9,8},{10,9},{13,12},{14,13},{17,16},{18,1... | collective-permute-start | bytes 4718600 | tf_op jit(solution)/shard_map/ppermute | solution.py:11
  86.1 37.9 %collective-permute-start.4 = (bf16[3,256,1024]{2,1,0:T(8,128)(2,1)}, bf16[3,256,1024]{2,1,0:T(8,128)(2,1)}, u32[]{:S(2)}, u32[]{:S(2)}) collective-permute-start(bf16[3,256,1024]{2,1,0:T(8,128)(2,1)} %collective-permute-done.3), channel_id=1, source_target_pairs={{1,2},{2,3},{5,6},{6,7},{9,10},{10,11},{13,14},{14,15},{17,18},{18... | collective-permute-start | bytes 4718600 | tf_op jit(solution)/shard_map/ppermute | solution.py:11
  91.3 33.9 %copy-start.2 = (f32[24,24]{1,0:T(8,128)S(1)}, f32[24,24]{1,0:T(8,128)}, u32[]{:S(2)}) copy-start(f32[24,24]{1,0:T(8,128)} %param.12) | copy-start | bytes 6916
  96.1 29.1 %all-to-all-start.2 = ((bf16[3,8,32,1024]{3,2,0,1:T(8,128)(2,1)}), bf16[3,8,32,1024]{3,2,0,1:T(8,128)(2,1)}, u32[]{:S(2)}, u32[]{:S(2)}) async-start(bf16[3,8,32,1024]{3,2,0,1:T(8,128)(2,1)} %copy.21), calls=%async_computation.2 | async-start | bytes 3145728 | tf_op jit(solution)/shard_map/all_to_all | solution.py:54
  100.5 35.7 %collective-permute-start.2 = (bf16[3,256,1024]{2,1,0:T(8,128)(2,1)}, bf16[3,256,1024]{2,1,0:T(8,128)(2,1)}, u32[]{:S(2)}, u32[]{:S(2)}) collective-permute-start(bf16[3,256,1024]{2,1,0:T(8,128)(2,1)} %collective-permute-done.1), channel_id=1, source_target_pairs={{1,0},{5,4},{9,8},{13,12},{17,16},{21,20},{25,24},{29,28},{33,32},... | collective-permute-start | bytes 4718600 | tf_op jit(solution)/shard_map/ppermute | solution.py:11
  123.9 37.0 %collective-permute-start.5 = (bf16[3,256,1024]{2,1,0:T(8,128)(2,1)}, bf16[3,256,1024]{2,1,0:T(8,128)(2,1)}, u32[]{:S(2)}, u32[]{:S(2)}) collective-permute-start(bf16[3,256,1024]{2,1,0:T(8,128)(2,1)} %collective-permute-done.4), channel_id=1, source_target_pairs={{2,3},{6,7},{10,11},{14,15},{18,19},{22,23},{26,27},{30,31},{34,35... | collective-permute-start | bytes 4718600 | tf_op jit(solution)/shard_map/ppermute | solution.py:11
  130.6 36.0 %all-to-all-start.3 = ((bf16[8,3,32,1024]{3,2,1,0:T(8,128)(2,1)}), bf16[8,3,32,1024]{3,2,1,0:T(8,128)(2,1)}, u32[]{:S(2)}, u32[]{:S(2)}) async-start(bf16[8,3,32,1024]{3,2,1,0:T(8,128)(2,1)} %bitcast.39), calls=%async_computation.3 | async-start | bytes 3145728 | tf_op jit(solution)/shard_map/all_to_all | solution.py:59
  194.2 10.1 %collective-permute-start.6 = (bf16[128,256]{1,0:T(8,128)(2,1)S(1)}, bf16[128,256]{1,0:T(8,128)(2,1)S(1)}, u32[]{:S(2)}, u32[]{:S(2)}) collective-permute-start(bf16[128,256]{1,0:T(8,128)(2,1)S(1)} %reduce_sum.19), channel_id=1, source_target_pairs={{0,0},{1,128},{2,256},{3,384},{4,4},{5,132},{6,260},{7,388},{8,8},... | collective-permute-start | bytes 196616 | tf_op jit(solution)/shard_map/ppermute | solution.py:78

commit v4 on v3

--- a/solution.py
+++ b/solution.py
@@ -11,20 +11,15 @@
     return lax.ppermute(array, "k", pairs)
 
 
-def line_gather(block, k):
+def line_blocks(block):
     ups, downs = [block], [block]
     for step in range(1, G):
         ups.append(shifted(ups[-1], [(i, i + 1) for i in range(step - 1, G - 1)]))
         downs.append(shifted(downs[-1], [(i + 1, i) for i in range(0, G - step)]))
-
-    def placed(kk):
-        parts = [ups[kk - p] if p <= kk else downs[p - kk] for p in range(G)]
-        return lambda: jnp.concatenate(parts, axis=1)
-
-    return lax.switch(k, [placed(kk) for kk in range(G)])
+    return ups, downs
 
 
-def on_device(theta, env_left, env_right, mpo_core, sector_sizes):
+def body(theta, env_left, env_right, mpo_core, sector_sizes):
     sectors, rows_local, width = theta.shape
     local_w, slab, _ = env_left.shape
     n_mpo = lax.axis_size("mpo")
@@ -33,8 +28,18 @@
     sector = lax.axis_index("sg")
     k = lax.axis_index("k")
     live_size = jnp.sum(jnp.where(jnp.arange(sectors, dtype=jnp.int32) == sector, sector_sizes, 0))
+    sub = slab // n_mpo
 
-    right_all = line_gather(env_right, k)
+    ups, downs = line_blocks(env_right)
+
+    pieces = env_left.reshape(local_w, n_mpo, sub, width)
+    got = [lax.dynamic_index_in_dim(pieces, mm, 1, keepdims=False)]
+    for t in range(1, n_mpo):
+        piece = lax.dynamic_index_in_dim(pieces, (mm + t) % n_mpo, 1, keepdims=False)
+        got.append(lax.ppermute(piece, "mpo", [(i, (i + t) % n_mpo) for i in range(n_mpo)]))
+    left_rows = jnp.stack(got).reshape(local_w * n_mpo, sub, width)
+    a_order = (3 * ((mm - jnp.arange(n_mpo, dtype=jnp.int32)) % n_mpo))[:, None] + jnp.arange(local_w, dtype=jnp.int32)
+    core_rows = jnp.take(mpo_core, a_order.reshape(-1), axis=0)
 
     per = width // n_mpo
     sel = lax.dynamic_slice_in_dim(theta, mm * per, per, axis=2)
@@ -47,20 +52,22 @@
     block = jnp.where(keep[:, None] & keep[None, :], block, jnp.zeros_like(block))
 
     product = jnp.einsum(
-        "akm,mn->akn", env_left, block, preferred_element_type=jnp.float32
+        "akm,mn->akn", left_rows, block, preferred_element_type=jnp.float32
     ).astype(jnp.bfloat16)
-    sub = slab // n_mpo
-    product = product.reshape(local_w, n_mpo, sub, width)
-    all_a = lax.all_to_all(product, "mpo", 1, 0, tiled=True).reshape(local_w * n_mpo, sub, width)
     mixed = jnp.einsum(
-        "ab,akn->bkn", mpo_core, all_a.astype(jnp.float32), precision=lax.Precision.HIGHEST
+        "ab,akn->bkn", core_rows, product.astype(jnp.float32), precision=lax.Precision.HIGHEST
     ).astype(jnp.bfloat16)
     mixed = mixed.reshape(n_mpo, local_w, sub, width)
     own_b = lax.all_to_all(mixed, "mpo", 0, 0, tiled=False)
 
-    term = jnp.einsum(
-        "mbil,bjl->mij", own_b, right_all, preferred_element_type=jnp.float32
-    ).reshape(slab, width)
+    def placed(kk):
+        parts = [ups[kk - p] if p <= kk else downs[p - kk] for p in range(G)]
+        return lambda: jnp.concatenate(
+            [jnp.einsum("mbil,bjl->mij", own_b, f, preferred_element_type=jnp.float32) for f in parts],
+            axis=2,
+        )
+
+    term = lax.switch(k, [placed(kk) for kk in range(G)]).reshape(slab, width)
     row_keep = k * slab + jnp.arange(slab, dtype=jnp.int32) < live_size
     term = jnp.where(row_keep[:, None] & keep[None, :], term, jnp.zeros_like(term))
     halves = n_mpo // G
@@ -84,7 +91,7 @@
     grid = Mesh(devices.reshape(n_mpo, n_sec // G, G), ("mpo", "sg", "k"))
     sec = ("sg", "k")
     return jax.shard_map(
-        on_device,
+        body,
         mesh=grid,
         in_specs=(P(None, sec, None), P("mpo", sec, None), P("mpo", sec, None), P(), P()),
         out_specs=P("mpo", sec),

time: 206 us -> 223 us (1.083)
  the two profiles are of different devices: /device:TPU:102 before, /device:TPU:8 now
where the time goes in v4:
time: 223 us; the launch traced here: 222 us
  waiting for transfers between devices  105 us (47%)
  starting transfers between devices  58.5 us (26%)
  local copies, waits for them, and re-layouts  21.6 us (10%)
  blocking collectives  18.3 us (8%)
  matrix products  10.5 us (5%)
  other arithmetic  7.57 us (3%)
    ppermute x6, waiting for transfers between devices, shifted(): return lax.ppermute(array, 'k', pairs)  37.5 us
    all_to_all x1, waiting for transfers between devices, body(): lax.all_to_all(spread, ('sg', 'k'), 0, 0, tiled=True).reshape(width, per)  22.6 us
    all_to_all x1, waiting for transfers between devices, body(): own_b = lax.all_to_all(mixed, 'mpo', 0, 0, tiled=False)  18.7 us
    ppermute x7, waiting for transfers between devices, body(): lax.ppermute(piece, 'mpo', [(i, (i + t) % n_mpo) for i in range(n_mpo)])  18.5 us
    ppermute x7, starting transfers between devices, body(): lax.ppermute(piece, 'mpo', [(i, (i + t) % n_mpo) for i in range(n_mpo)])  18.4 us
    all_to_all x1, blocking collectives, body(): lax.all_to_all(term, 'mpo', 0, 0, tiled=False)  18.3 us
    all_to_all x1, starting transfers between devices, body(): lax.all_to_all(spread, ('sg', 'k'), 0, 0, tiled=True).reshape(width, per)  16.1 us
    ppermute x6, starting transfers between devices, shifted(): return lax.ppermute(array, 'k', pairs)  12.7 us
  transfers between devices with their start and end apart: 17, of which 9 were waited for; matrix products, arithmetic and copies ran while one was open for 13% of the time, Pallas kernels for 0%

profile of v4, /device:TPU:8, one launch (start us, length us, event | category | flops | bytes accessed | tf_op | source)
XLA Modules:
  0.0 222.3 jit_solution(6662746368020372042)
XLA Ops:
  0.0 5.1 %collective-permute-start.10 = (bf16[3,256,1024]{2,1,0:T(8,128)(2,1)}, bf16[3,256,1024]{2,1,0:T(8,128)(2,1)}, u32[]{:S(2)}, u32[]{:S(2)}) collective-permute-start(bf16[3,256,1024]{2,1,0:T(8,128)(2,1)} %param.11), channel_id=1, source_target_pairs={{0,1},{1,2},{2,3},{4,5},{5,6},{6,7},{8,9},{9,10},{10,11},{12,13},{... | collective-permute-start | bytes 4718600 | tf_op jit(solution)/shard_map/ppermute | solution.py:11
  6.5 2.3 %dynamic-slice_bitcast_fusion = (bf16[3,32,1024]{2,1,0:T(8,128)(2,1)S(1)}, bf16[3,32,1024]{2,1,0:T(8,128)(2,1)S(1)}, bf16[3,32,1024]{2,1,0:T(8,128)(2,1)S(1)}, b...) fusion(bf16[3,8,32,1024]{3,2,1,0:T(8,128)(2,1)} %bitcast.214, ...), kind=kLoop, calls=%fused_computation.66 | loop fusion | bytes 2752540 | tf_op jit(solution)/shard_map/jit(dynamic_index_in_dim)/squeeze | solution.py:38
  8.8 3.5 %collective-permute-start.1 = (bf16[3,32,1024]{2,1,0:T(8,128)(2,1)}, bf16[3,32,1024]{2,1,0:T(8,128)(2,1)}, u32[]{:S(2)}, u32[]{:S(2)}) collective-permute-start(bf16[3,32,1024]{2,1,0:T(8,128)(2,1)} %get-tuple-element.77), channel_id=1, source_target_pairs={{0,128},{64,192},{128,256},{192,320},{256,384},{320,448},{384,0},{... | collective-permute-start | bytes 589832 | tf_op jit(solution)/shard_map/ppermute | solution.py:39
  12.3 5.7 %collective-permute-start.2 = (bf16[3,32,1024]{2,1,0:T(8,128)(2,1)}, bf16[3,32,1024]{2,1,0:T(8,128)(2,1)}, u32[]{:S(2)}, u32[]{:S(2)}) collective-permute-start(bf16[3,32,1024]{2,1,0:T(8,128)(2,1)} %get-tuple-element.76), channel_id=1, source_target_pairs={{0,192},{64,256},{128,320},{192,384},{256,448},{320,0},{384,64},{4... | collective-permute-start | bytes 589832 | tf_op jit(solution)/shard_map/ppermute | solution.py:39
  18.8 16.1 %all-to-all-start = ((bf16[64,16,128]{2,1,0:T(8,128)(2,1)}), bf16[64,16,128]{2,1,0:T(8,128)(2,1)S(1)}, u32[]{:S(2)}, u32[]{:S(2)}) async-start(bf16[64,16,128]{2,1,0:T(8,128)(2,1)} %bitcast.67), calls=%async_computation | async-start | bytes 524288 | tf_op jit(solution)/shard_map/all_to_all | solution.py:47
  39.5 22.6 %all-to-all-done = bf16[64,16,128]{2,1,0:T(8,128)(2,1)S(1)} async-done(((bf16[64,16,128]{2,1,0:T(8,128)(2,1)}), bf16[64,16,128]{2,1,0:T(8,128)(2,1)S(1)}, u32[]{:S(2)}, u32[]{:S(2)}) %all-to-all-start) | async-done | bytes 262176 | tf_op jit(solution)/shard_map/all_to_all | solution.py:47
  63.7 4.9 %all-to-all-start.1 = ((bf16[8,1024,128]{2,1,0:T(8,128)(2,1)}), bf16[8,1024,128]{2,1,0:T(8,128)(2,1)S(1)}, u32[]{:S(2)}, u32[]{:S(2)}) async-start(bf16[8,1024,128]{2,1,0:T(8,128)(2,1)} %broadcast_in_dim.44), calls=%async_computation.1 | async-start | bytes 4194304 | tf_op jit(solution)/shard_map/all_to_all | solution.py:49
  68.7 4.0 %collective-permute-start.3 = (bf16[3,32,1024]{2,1,0:T(8,128)(2,1)S(1)}, bf16[3,32,1024]{2,1,0:T(8,128)(2,1)S(1)}, u32[]{:S(2)}, u32[]{:S(2)}) collective-permute-start(bf16[3,32,1024]{2,1,0:T(8,128)(2,1)S(1)} %get-tuple-element.75), channel_id=1, source_target_pairs={{0,256},{64,320},{128,384},{192,448},{256,0},{320,64},{384,128},{4... | collective-permute-start | bytes 589832 | tf_op jit(solution)/shard_map/ppermute | solution.py:39
  74.3 2.8 %collective-permute-start.4 = (bf16[3,32,1024]{2,1,0:T(8,128)(2,1)S(1)}, bf16[3,32,1024]{2,1,0:T(8,128)(2,1)S(1)}, u32[]{:S(2)}, u32[]{:S(2)}) collective-permute-start(bf16[3,32,1024]{2,1,0:T(8,128)(2,1)S(1)} %get-tuple-element.74), channel_id=1, source_target_pairs={{0,320},{64,384},{128,448},{192,0},{256,64},{320,128},{384,192},{4... | collective-permute-start | bytes 589832 | tf_op jit(solution)/shard_map/ppermute | solution.py:39
  78.7 2.5 %collective-permute-start.5 = (bf16[3,32,1024]{2,1,0:T(8,128)(2,1)S(1)}, bf16[3,32,1024]{2,1,0:T(8,128)(2,1)S(1)}, u32[]{:S(2)}, u32[]{:S(2)}) collective-permute-start(bf16[3,32,1024]{2,1,0:T(8,128)(2,1)S(1)} %get-tuple-element.73), channel_id=1, source_target_pairs={{0,384},{64,448},{128,0},{192,64},{256,128},{320,192},{384,256},{4... | collective-permute-start | bytes 589832 | tf_op jit(solution)/shard_map/ppermute | solution.py:39
  82.8 16.4 %collective-permute-done.3 = bf16[3,32,1024]{2,1,0:T(8,128)(2,1)S(1)} collective-permute-done((bf16[3,32,1024]{2,1,0:T(8,128)(2,1)S(1)}, bf16[3,32,1024]{2,1,0:T(8,128)(2,1)S(1)}, u32[]{:S(2)}, u32[]{:S(2)}) %collective-permute-start.3) | collective-permute-done | bytes 196640 | tf_op jit(solution)/shard_map/ppermute | solution.py:39
  107.3 2.6 %copy.30 = bf16[8,1024,128]{1,2,0:T(8,128)(2,1)} copy(bf16[8,1024,128]{2,1,0:T(8,128)(2,1)S(1)} %all-to-all-done.1) | data formatting | bytes 4194304 | tf_op jit(solution)/shard_map/all_to_all | solution.py:49
  109.9 2.4 %and_select_fusion = bf16[1,1024,8,128]{1,3,2,0:T(8,128)(2,1)S(1)} fusion(bf16[8,1024,128]{1,2,0:T(8,128)(2,1)} %copy.30, pred[8,128]{1,0:T(8,128)(4,1)S(1)} %add_compare_fusion, pred[1024]{0:T(1024)(128)(4,1)S(1)} %iota_compare_fusion), kind=kLoop, calls=%fused_computation.53 | loop fusion | flops 2097152 | bytes 4196352 | tf_op jit(solution)/shard_map/jit(_where)/select_n | solution.py:52
  112.3 2.2 %convolution_convert_fusion.1 = bf16[24,32,1024]{2,0,1:T(8,128)(2,1)S(1)} fusion(bf16[1024,1024,1]{0,1,2:T(8,128)(2,1)S(1)} %bitcast.213, bf16[24,32,1024]{2,1,0:T(8,128)(2,1)S(1)} %bitcast.217), kind=kOutput, calls=%fused_computation.55 | convolution fusion | flops 1611399168 | bytes 5242880 | tf_op jit(solution)/shard_map/akm,mn->akn/dot_general | solution.py:54
  116.4 28.7 %collective-permute-done.8 = bf16[3,256,1024]{2,1,0:T(8,128)(2,1)} collective-permute-done((bf16[3,256,1024]{2,1,0:T(8,128)(2,1)}, bf16[3,256,1024]{2,1,0:T(8,128)(2,1)}, u32[]{:S(2)}, u32[]{:S(2)}) %collective-permute-start.8) | collective-permute-done | bytes 1572896 | tf_op jit(solution)/shard_map/ppermute | solution.py:11
  149.9 4.3 %all-to-all-start.2 = ((bf16[8,3,32,1024]{3,2,1,0:T(8,128)(2,1)}), bf16[8,3,32,1024]{3,2,1,0:T(8,128)(2,1)S(1)}, u32[]{:S(2)}, u32[]{:S(2)}) async-start(bf16[8,3,32,1024]{3,2,1,0:T(8,128)(2,1)} %bitcast.73), calls=%async_computation.2 | async-start | bytes 3145728 | tf_op jit(solution)/shard_map/all_to_all | solution.py:61
  155.7 18.7 %all-to-all-done.2 = bf16[8,3,32,1024]{3,2,1,0:T(8,128)(2,1)S(1)} async-done(((bf16[8,3,32,1024]{3,2,1,0:T(8,128)(2,1)}), bf16[8,3,32,1024]{3,2,1,0:T(8,128)(2,1)S(1)}, u32[]{:S(2)}, u32[]{:S(2)}) %all-to-all-start.2) | async-done | bytes 1572896 | tf_op jit(solution)/shard_map/all_to_all | solution.py:61
  174.4 8.9 %collective-permute-done.9 = bf16[3,256,1024]{2,1,0:T(8,128)(2,1)} collective-permute-done((bf16[3,256,1024]{2,1,0:T(8,128)(2,1)}, bf16[3,256,1024]{2,1,0:T(8,128)(2,1)}, u32[]{:S(2)}, u32[]{:S(2)}) %collective-permute-start.9) | collective-permute-done | bytes 1572896 | tf_op jit(solution)/shard_map/ppermute | solution.py:11
  183.3 8.1 %conditional.1 = (f32[2,128,4,256]{3,1,0,2:T(8,128)S(1)}) conditional(s32[]{:T(128)} %clamp.3, (bf16[8,3,32,1024]{3,2,1,0:T(8,128)(2,1)S(1)}, bf16[3,256,1024]{2,1,0:T(8,128)(2,1)}, bf16[3,256,1024]{2,1,0:T(8,128)(2,1)}, bf16[3,256,1024]{2,1,0:T(8,128)(2,1)}, bf16[3,256,1024]{2,1,0:T(8,128)(2,1)}) %tuple.21, ...), branch_computations={%region_1.2_spmd, %region_2.3_spmd, %region_3.4_spmd, %region_4.5_... | conditional | flops 1611399168 | bytes 26214436 | solution.py:70
  185.3 2.0 fusion.14
  187.3 2.1 fusion.17
  193.7 18.3 %all_to_all.30 = f32[8,128,256]{2,1,0:T(8,128)S(1)} all-to-all(f32[8,128,256]{2,1,0:T(8,128)S(1)} %bitcast.212), channel_id=1, replica_groups=mesh['mpo'=8,'sg'=16,'k'=4] {'mpo'}, dimensions={0} | all-to-all | bytes 2097152 | tf_op jit(solution)/shard_map/all_to_all | solution.py:76
  212.1 2.1 collective-permute-start.13
  214.2 7.5 %collective-permute-done.13 = bf16[128,256]{1,0:T(8,128)(2,1)S(1)} collective-permute-done((bf16[128,256]{1,0:T(8,128)(2,1)S(1)}, bf16[128,256]{1,0:T(8,128)(2,1)S(1)}, u32[]{:S(2)}, u32[]{:S(2)}) %collective-permute-start.13) | collective-permute-done | bytes 65568 | tf_op jit(solution)/shard_map/ppermute | solution.py:85
  (64 shorter events, 35.8 us)
Async XLA Ops:
  0.0 18.0 %copy-start = (bf16[16,16,1024]{2,1,0:T(8,128)(2,1)S(1)}, bf16[16,16,1024]{2,1,0:T(8,128)(2,1)}, u32[]{:S(2)}) copy-start(bf16[16,16,1024]{2,1,0:T(8,128)(2,1)} %param.9) | copy-start | bytes 1572868
  0.0 99.2 %collective-permute-start.10 = (bf16[3,256,1024]{2,1,0:T(8,128)(2,1)}, bf16[3,256,1024]{2,1,0:T(8,128)(2,1)}, u32[]{:S(2)}, u32[]{:S(2)}) collective-permute-start(bf16[3,256,1024]{2,1,0:T(8,128)(2,1)} %param.11), channel_id=1, source_target_pairs={{0,1},{1,2},{2,3},{4,5},{5,6},{6,7},{8,9},{9,10},{10,11},{12,13},{... | collective-permute-start | bytes 4718600 | tf_op jit(solution)/shard_map/ppermute | solution.py:11
  5.1 96.0 %collective-permute-start.7 = (bf16[3,256,1024]{2,1,0:T(8,128)(2,1)}, bf16[3,256,1024]{2,1,0:T(8,128)(2,1)}, u32[]{:S(2)}, u32[]{:S(2)}) collective-permute-start(bf16[3,256,1024]{2,1,0:T(8,128)(2,1)} %param.11), channel_id=1, source_target_pairs={{1,0},{2,1},{3,2},{5,4},{6,5},{7,6},{9,8},{10,9},{11,10},{13,12},{... | collective-permute-start | bytes 4718600 | tf_op jit(solution)/shard_map/ppermute | solution.py:11
  6.5 28.6 %copy-start.2 = (f32[24,24]{1,0:T(8,128)S(1)}, f32[24,24]{1,0:T(8,128)}, u32[]{:S(2)}) copy-start(f32[24,24]{1,0:T(8,128)} %param.12) | copy-start | bytes 6916
  6.5 29.2 %copy-start.8 = (s32[16]{0:T(128)S(1)}, s32[16]{0:T(128)}, u32[]{:S(2)}) copy-start(s32[16]{0:T(128)} %param.13) | copy-start | bytes 196
  8.8 59.8 %collective-permute-start = (bf16[3,32,1024]{2,1,0:T(8,128)(2,1)}, bf16[3,32,1024]{2,1,0:T(8,128)(2,1)}, u32[]{:S(2)}, u32[]{:S(2)}) collective-permute-start(bf16[3,32,1024]{2,1,0:T(8,128)(2,1)} %get-tuple-element.78), channel_id=1, source_target_pairs={{0,64},{64,128},{128,192},{192,256},{256,320},{320,384},{384,448},... | collective-permute-start | bytes 589832 | tf_op jit(solution)/shard_map/ppermute | solution.py:39
  8.8 65.4 %collective-permute-start.1 = (bf16[3,32,1024]{2,1,0:T(8,128)(2,1)}, bf16[3,32,1024]{2,1,0:T(8,128)(2,1)}, u32[]{:S(2)}, u32[]{:S(2)}) collective-permute-start(bf16[3,32,1024]{2,1,0:T(8,128)(2,1)} %get-tuple-element.77), channel_id=1, source_target_pairs={{0,128},{64,192},{128,256},{192,320},{256,384},{320,448},{384,0},{... | collective-permute-start | bytes 589832 | tf_op jit(solution)/shard_map/ppermute | solution.py:39
  12.3 66.4 %collective-permute-start.2 = (bf16[3,32,1024]{2,1,0:T(8,128)(2,1)}, bf16[3,32,1024]{2,1,0:T(8,128)(2,1)}, u32[]{:S(2)}, u32[]{:S(2)}) collective-permute-start(bf16[3,32,1024]{2,1,0:T(8,128)(2,1)} %get-tuple-element.76), channel_id=1, source_target_pairs={{0,192},{64,256},{128,320},{192,384},{256,448},{320,0},{384,64},{4... | collective-permute-start | bytes 589832 | tf_op jit(solution)/shard_map/ppermute | solution.py:39
  18.8 43.3 %all-to-all-start = ((bf16[64,16,128]{2,1,0:T(8,128)(2,1)}), bf16[64,16,128]{2,1,0:T(8,128)(2,1)S(1)}, u32[]{:S(2)}, u32[]{:S(2)}) async-start(bf16[64,16,128]{2,1,0:T(8,128)(2,1)} %bitcast.67), calls=%async_computation | async-start | bytes 524288 | tf_op jit(solution)/shard_map/all_to_all | solution.py:47
  63.7 43.6 %all-to-all-start.1 = ((bf16[8,1024,128]{2,1,0:T(8,128)(2,1)}), bf16[8,1024,128]{2,1,0:T(8,128)(2,1)S(1)}, u32[]{:S(2)}, u32[]{:S(2)}) async-start(bf16[8,1024,128]{2,1,0:T(8,128)(2,1)} %broadcast_in_dim.44), calls=%async_computation.1 | async-start | bytes 4194304 | tf_op jit(solution)/shard_map/all_to_all | solution.py:49
  68.7 30.5 %collective-permute-start.3 = (bf16[3,32,1024]{2,1,0:T(8,128)(2,1)S(1)}, bf16[3,32,1024]{2,1,0:T(8,128)(2,1)S(1)}, u32[]{:S(2)}, u32[]{:S(2)}) collective-permute-start(bf16[3,32,1024]{2,1,0:T(8,128)(2,1)S(1)} %get-tuple-element.75), channel_id=1, source_target_pairs={{0,256},{64,320},{128,384},{192,448},{256,0},{320,64},{384,128},{4... | collective-permute-start | bytes 589832 | tf_op jit(solution)/shard_map/ppermute | solution.py:39
  74.3 29.4 %collective-permute-start.4 = (bf16[3,32,1024]{2,1,0:T(8,128)(2,1)S(1)}, bf16[3,32,1024]{2,1,0:T(8,128)(2,1)S(1)}, u32[]{:S(2)}, u32[]{:S(2)}) collective-permute-start(bf16[3,32,1024]{2,1,0:T(8,128)(2,1)S(1)} %get-tuple-element.74), channel_id=1, source_target_pairs={{0,320},{64,384},{128,448},{192,0},{256,64},{320,128},{384,192},{4... | collective-permute-start | bytes 589832 | tf_op jit(solution)/shard_map/ppermute | solution.py:39
  78.7 26.1 %collective-permute-start.5 = (bf16[3,32,1024]{2,1,0:T(8,128)(2,1)S(1)}, bf16[3,32,1024]{2,1,0:T(8,128)(2,1)S(1)}, u32[]{:S(2)}, u32[]{:S(2)}) collective-permute-start(bf16[3,32,1024]{2,1,0:T(8,128)(2,1)S(1)} %get-tuple-element.73), channel_id=1, source_target_pairs={{0,384},{64,448},{128,0},{192,64},{256,128},{320,192},{384,256},{4... | collective-permute-start | bytes 589832 | tf_op jit(solution)/shard_map/ppermute | solution.py:39
  99.2 7.4 %collective-permute-start.6 = (bf16[3,32,1024]{2,1,0:T(8,128)(2,1)S(1)}, bf16[3,32,1024]{2,1,0:T(8,128)(2,1)S(1)}, u32[]{:S(2)}, u32[]{:S(2)}) collective-permute-start(bf16[3,32,1024]{2,1,0:T(8,128)(2,1)S(1)} %get-tuple-element.72), channel_id=1, source_target_pairs={{0,448},{64,0},{128,64},{192,128},{256,192},{320,256},{384,320},{4... | collective-permute-start | bytes 589832 | tf_op jit(solution)/shard_map/ppermute | solution.py:39
  99.2 15.4 %collective-permute-start.11 = (bf16[3,256,1024]{2,1,0:T(8,128)(2,1)}, bf16[3,256,1024]{2,1,0:T(8,128)(2,1)}, u32[]{:S(2)}, u32[]{:S(2)}) collective-permute-start(bf16[3,256,1024]{2,1,0:T(8,128)(2,1)} %collective-permute-done.10), channel_id=1, source_target_pairs={{1,2},{2,3},{5,6},{6,7},{9,10},{10,11},{13,14},{14,15},{17,18},{18... | collective-permute-start | bytes 4718600 | tf_op jit(solution)/shard_map/ppermute | solution.py:11
  101.1 44.0 %collective-permute-start.8 = (bf16[3,256,1024]{2,1,0:T(8,128)(2,1)}, bf16[3,256,1024]{2,1,0:T(8,128)(2,1)}, u32[]{:S(2)}, u32[]{:S(2)}) collective-permute-start(bf16[3,256,1024]{2,1,0:T(8,128)(2,1)} %collective-permute-done.7), channel_id=1, source_target_pairs={{1,0},{2,1},{5,4},{6,5},{9,8},{10,9},{13,12},{14,13},{17,16},{18,1... | collective-permute-start | bytes 4718600 | tf_op jit(solution)/shard_map/ppermute | solution.py:11
  109.9 2.4 %copy-start.3 = (bf16[8,3,32,1024]{3,2,1,0:T(8,128)(2,1)S(1)}, bf16[8,3,32,1024]{3,2,1,0:T(8,128)(2,1)}, u32[]{:S(2)}) copy-start(bf16[8,3,32,1024]{3,2,1,0:T(8,128)(2,1)} %bitcast_dynamic-update-slice_fusion.1) | copy-start | bytes 4718596
  114.6 59.8 %collective-permute-start.12 = (bf16[3,256,1024]{2,1,0:T(8,128)(2,1)}, bf16[3,256,1024]{2,1,0:T(8,128)(2,1)}, u32[]{:S(2)}, u32[]{:S(2)}) collective-permute-start(bf16[3,256,1024]{2,1,0:T(8,128)(2,1)} %collective-permute-done.11), channel_id=1, source_target_pairs={{2,3},{6,7},{10,11},{14,15},{18,19},{22,23},{26,27},{30,31},{34,35... | collective-permute-start | bytes 4718600 | tf_op jit(solution)/shard_map/ppermute | solution.py:11
  145.1 38.1 %collective-permute-start.9 = (bf16[3,256,1024]{2,1,0:T(8,128)(2,1)}, bf16[3,256,1024]{2,1,0:T(8,128)(2,1)}, u32[]{:S(2)}, u32[]{:S(2)}) collective-permute-start(bf16[3,256,1024]{2,1,0:T(8,128)(2,1)} %collective-permute-done.8), channel_id=1, source_target_pairs={{1,0},{5,4},{9,8},{13,12},{17,16},{21,20},{25,24},{29,28},{33,32},... | collective-permute-start | bytes 4718600 | tf_op jit(solution)/shard_map/ppermute | solution.py:11
  149.9 24.5 %all-to-all-start.2 = ((bf16[8,3,32,1024]{3,2,1,0:T(8,128)(2,1)}), bf16[8,3,32,1024]{3,2,1,0:T(8,128)(2,1)S(1)}, u32[]{:S(2)}, u32[]{:S(2)}) async-start(bf16[8,3,32,1024]{3,2,1,0:T(8,128)(2,1)} %bitcast.73), calls=%async_computation.2 | async-start | bytes 3145728 | tf_op jit(solution)/shard_map/all_to_all | solution.py:61
  187.3 2.2 copy-start.4
  191.3 1.0 copy-start.1
  212.1 9.6 %collective-permute-start.13 = (bf16[128,256]{1,0:T(8,128)(2,1)S(1)}, bf16[128,256]{1,0:T(8,128)(2,1)S(1)}, u32[]{:S(2)}, u32[]{:S(2)}) collective-permute-start(bf16[128,256]{1,0:T(8,128)(2,1)S(1)} %reduce_sum.19), channel_id=1, source_target_pairs={{0,0},{1,128},{2,256},{3,384},{4,4},{5,132},{6,260},{7,388},{8,8},... | collective-permute-start | bytes 196616 | tf_op jit(solution)/shard_map/ppermute | solution.py:85

commit v5 on v4

--- a/solution.py
+++ b/solution.py
@@ -32,15 +32,6 @@
 
     ups, downs = line_blocks(env_right)
 
-    pieces = env_left.reshape(local_w, n_mpo, sub, width)
-    got = [lax.dynamic_index_in_dim(pieces, mm, 1, keepdims=False)]
-    for t in range(1, n_mpo):
-        piece = lax.dynamic_index_in_dim(pieces, (mm + t) % n_mpo, 1, keepdims=False)
-        got.append(lax.ppermute(piece, "mpo", [(i, (i + t) % n_mpo) for i in range(n_mpo)]))
-    left_rows = jnp.stack(got).reshape(local_w * n_mpo, sub, width)
-    a_order = (3 * ((mm - jnp.arange(n_mpo, dtype=jnp.int32)) % n_mpo))[:, None] + jnp.arange(local_w, dtype=jnp.int32)
-    core_rows = jnp.take(mpo_core, a_order.reshape(-1), axis=0)
-
     per = width // n_mpo
     sel = lax.dynamic_slice_in_dim(theta, mm * per, per, axis=2)
     spread = jnp.broadcast_to(sel[:, None], (sectors, G, rows_local, per)).reshape(sectors * G, rows_local, per)
@@ -52,10 +43,12 @@
     block = jnp.where(keep[:, None] & keep[None, :], block, jnp.zeros_like(block))
 
     product = jnp.einsum(
-        "akm,mn->akn", left_rows, block, preferred_element_type=jnp.float32
+        "akm,mn->akn", env_left, block, preferred_element_type=jnp.float32
     ).astype(jnp.bfloat16)
+    product = product.reshape(local_w, n_mpo, sub, width)
+    all_a = lax.all_to_all(product, "mpo", 1, 0, tiled=True).reshape(local_w * n_mpo, sub, width)
     mixed = jnp.einsum(
-        "ab,akn->bkn", core_rows, product.astype(jnp.float32), precision=lax.Precision.HIGHEST
+        "ab,akn->bkn", mpo_core, all_a.astype(jnp.float32), precision=lax.Precision.HIGHEST
     ).astype(jnp.bfloat16)
     mixed = mixed.reshape(n_mpo, local_w, sub, width)
     own_b = lax.all_to_all(mixed, "mpo", 0, 0, tiled=False)

time: 223 us -> 206 us (0.924)
  the two profiles are of different devices: /device:TPU:8 before, /device:TPU:14 now
where the time goes in v5:
time: 206 us; the launch traced here: 205 us
  waiting for transfers between devices  87.1 us (42%)
  blocking collectives  58.6 us (28%)
  starting transfers between devices  28.5 us (14%)
  local copies, waits for them, and re-layouts  14.3 us (7%)
  matrix products  12.2 us (6%)
  other arithmetic  4.09 us (2%)
    ppermute x6, waiting for transfers between devices, shifted(): return lax.ppermute(array, 'k', pairs)  60.8 us
    all_to_all x1, blocking collectives, body(): lax.all_to_all(spread, ('sg', 'k'), 0, 0, tiled=True).reshape(width, per)  39.4 us
    all_to_all x1, blocking collectives, body(): lax.all_to_all(term, 'mpo', 0, 0, tiled=False)  19.2 us
    all_to_all x1, waiting for transfers between devices, body(): own_b = lax.all_to_all(mixed, 'mpo', 0, 0, tiled=False)  18.9 us
    ppermute x6, starting transfers between devices, shifted(): return lax.ppermute(array, 'k', pairs)  11.7 us
    ppermute x1, waiting for transfers between devices, body(): return lax.ppermute(result, ('mpo', 'sg', 'k'), pairs)  7.47 us
    dot_general x4, matrix products, placed(): jnp.einsum('mbil,bjl->mij', own_b, f, preferred_element_type=jnp.float32)  6.77 us
    all_to_all x1, starting transfers between devices, body(): lax.all_to_all(everyone, 'mpo', 0, 2, tiled=True).reshape(width, width)  5.05 us
  transfers between devices with their start and end apart: 10, of which 6 were waited for; matrix products, arithmetic and copies ran while one was open for 7% of the time, Pallas kernels for 0%

profile of v5, /device:TPU:14, one launch (start us, length us, event | category | flops | bytes accessed | tf_op | source)
XLA Modules:
  0.0 205.4 jit_solution(10635860712672119094)
XLA Ops:
  1.0 39.4 %all_to_all.45 = bf16[64,16,128]{2,1,0:T(8,128)(2,1)S(1)} all-to-all(bf16[64,16,128]{2,1,0:T(8,128)(2,1)S(1)} %bitcast.179), channel_id=1, replica_groups=mesh['mpo'=8,'sg'=16,'k'=4] {'sg','k'}, dimensions={0} | all-to-all | bytes 524288 | tf_op jit(solution)/shard_map/all_to_all | solution.py:38
  40.4 1.6 broadcast_in_dim.30
  42.0 5.0 %all-to-all-start.1 = ((bf16[8,1024,128]{2,1,0:T(8,128)(2,1)}), bf16[8,1024,128]{2,1,0:T(8,128)(2,1)}, u32[]{:S(2)}, u32[]{:S(2)}) async-start(bf16[8,1024,128]{2,1,0:T(8,128)(2,1)} %broadcast_in_dim.30), calls=%async_computation.1 | async-start | bytes 4194304 | tf_op jit(solution)/shard_map/all_to_all | solution.py:40
  47.0 4.1 %collective-permute-start.3 = (bf16[3,256,1024]{2,1,0:T(8,128)(2,1)S(1)}, bf16[3,256,1024]{2,1,0:T(8,128)(2,1)}, u32[]{:S(2)}, u32[]{:S(2)}) collective-permute-start(bf16[3,256,1024]{2,1,0:T(8,128)(2,1)S(1)} %copy-done.3), channel_id=1, source_target_pairs={{0,1},{1,2},{2,3},{4,5},{5,6},{6,7},{8,9},{9,10},{10,11},{12,13},{... | collective-permute-start | bytes 4718600 | tf_op jit(solution)/shard_map/ppermute | solution.py:11
  53.7 30.2 %collective-permute-done.3 = bf16[3,256,1024]{2,1,0:T(8,128)(2,1)} collective-permute-done((bf16[3,256,1024]{2,1,0:T(8,128)(2,1)S(1)}, bf16[3,256,1024]{2,1,0:T(8,128)(2,1)}, u32[]{:S(2)}, u32[]{:S(2)}) %collective-permute-start.3) | collective-permute-done | bytes 1572896 | tf_op jit(solution)/shard_map/ppermute | solution.py:11
  83.9 1.9 collective-permute-start.4
  85.7 3.5 %collective-permute-done = bf16[3,256,1024]{2,1,0:T(8,128)(2,1)} collective-permute-done((bf16[3,256,1024]{2,1,0:T(8,128)(2,1)S(1)}, bf16[3,256,1024]{2,1,0:T(8,128)(2,1)}, u32[]{:S(2)}, u32[]{:S(2)}) %collective-permute-start) | collective-permute-done | bytes 1572896 | tf_op jit(solution)/shard_map/ppermute | solution.py:11
  90.5 3.9 %copy.19 = bf16[8,1024,128]{1,2,0:T(8,128)(2,1)} copy(bf16[8,1024,128]{2,1,0:T(8,128)(2,1)} %all-to-all-done.1) | data formatting | bytes 4194304 | tf_op jit(solution)/shard_map/all_to_all | solution.py:40
  94.4 3.5 %fusion.85 = bf16[1024,3,256]{0,2,1:T(8,128)(2,1)S(1)} fusion(bf16[3,256,1024]{2,1,0:T(8,128)(2,1)S(1)} %copy-done, bf16[1024,1024]{0,1:T(8,128)(2,1)} %bitcast.176, pred[1024]{0:T(1024)(128)(4,1)S(1)} %iota_compare_fusion), kind=kOutput, calls=%fused_computation.57 | convolution fusion | flops 1613496320 | bytes 5243904 | tf_op jit(solution)/shard_map/akm,mn->akn/dot_general | solution.py:45
  99.2 4.9 %all-to-all-start.2 = ((bf16[3,8,32,1024]{3,2,0,1:T(8,128)(2,1)}), bf16[3,8,32,1024]{3,2,0,1:T(8,128)(2,1)S(1)}, u32[]{:S(2)}, u32[]{:S(2)}) async-start(bf16[3,8,32,1024]{3,2,0,1:T(8,128)(2,1)} %copy.21), calls=%async_computation.2 | async-start | bytes 3145728 | tf_op jit(solution)/shard_map/all_to_all | solution.py:49
  104.1 1.9 collective-permute-start.5
  106.0 20.6 %collective-permute-done.1 = bf16[3,256,1024]{2,1,0:T(8,128)(2,1)} collective-permute-done((bf16[3,256,1024]{2,1,0:T(8,128)(2,1)}, bf16[3,256,1024]{2,1,0:T(8,128)(2,1)}, u32[]{:S(2)}, u32[]{:S(2)}) %collective-permute-start.1) | collective-permute-done | bytes 1572896 | tf_op jit(solution)/shard_map/ppermute | solution.py:11
  128.0 2.0 fusion.89
  129.9 2.0 copy.24
  132.0 4.8 %all-to-all-start.3 = ((bf16[8,3,32,1024]{3,2,1,0:T(8,128)(2,1)}), bf16[8,3,32,1024]{3,2,1,0:T(8,128)(2,1)S(1)}, u32[]{:S(2)}, u32[]{:S(2)}) async-start(bf16[8,3,32,1024]{3,2,1,0:T(8,128)(2,1)} %bitcast.61), calls=%async_computation.3 | async-start | bytes 3145728 | tf_op jit(solution)/shard_map/all_to_all | solution.py:54
  138.0 18.9 %all-to-all-done.3 = bf16[8,3,32,1024]{3,2,1,0:T(8,128)(2,1)S(1)} async-done(((bf16[8,3,32,1024]{3,2,1,0:T(8,128)(2,1)}), bf16[8,3,32,1024]{3,2,1,0:T(8,128)(2,1)S(1)}, u32[]{:S(2)}, u32[]{:S(2)}) %all-to-all-start.3) | async-done | bytes 1572896 | tf_op jit(solution)/shard_map/all_to_all | solution.py:54
  156.9 6.4 %collective-permute-done.2 = bf16[3,256,1024]{2,1,0:T(8,128)(2,1)} collective-permute-done((bf16[3,256,1024]{2,1,0:T(8,128)(2,1)}, bf16[3,256,1024]{2,1,0:T(8,128)(2,1)}, u32[]{:S(2)}, u32[]{:S(2)}) %collective-permute-start.2) | collective-permute-done | bytes 1572896 | tf_op jit(solution)/shard_map/ppermute | solution.py:11
  163.3 10.3 %conditional.1 = (f32[2,128,4,256]{3,1,0,2:T(8,128)S(1)}) conditional(s32[]{:T(128)} %clamp.3, (bf16[8,3,32,1024]{3,2,1,0:T(8,128)(2,1)S(1)}, bf16[3,256,1024]{2,1,0:T(8,128)(2,1)}, bf16[3,256,1024]{2,1,0:T(8,128)(2,1)}, bf16[3,256,1024]{2,1,0:T(8,128)(2,1)}, bf16[3,256,1024]{2,1,0:T(8,128)(2,1)}) %tuple.21, ...), branch_computations={%region_1.2_spmd, %region_2.3_spmd, %region_3.4_spmd, %region_4.5_... | conditional | flops 1611399168 | bytes 26214436 | solution.py:63
  163.3 2.0 fusion.11
  165.3 2.0 fusion.14
  167.4 2.1 %fusion.17 = f32[8,32,256]{2,1,0:T(8,128)S(1)} fusion(bf16[8,3,32,1024]{3,2,1,0:T(8,128)(2,1)S(1)} %get-tuple-element.50, bf16[3,256,1024]{2,1,0:T(8,128)(2,1)} %get-tuple-element.55), kind=kOutput, calls=%fused_computation.11 | convolution fusion | flops 402653184 | bytes 3407872 | tf_op jit(solution)/shard_map/cond/branch_0_fun/mbil,bjl->mij/dot_general | solution.py:59
  176.0 19.2 %all_to_all.46 = f32[8,128,256]{2,1,0:T(8,128)S(1)} all-to-all(f32[8,128,256]{2,1,0:T(8,128)S(1)} %bitcast.175), channel_id=1, replica_groups=mesh['mpo'=8,'sg'=16,'k'=4] {'mpo'}, dimensions={0} | all-to-all | bytes 2097152 | tf_op jit(solution)/shard_map/all_to_all | solution.py:69
  195.2 2.1 %collective-permute-start.6 = (bf16[128,256]{1,0:T(8,128)(2,1)S(1)}, bf16[128,256]{1,0:T(8,128)(2,1)S(1)}, u32[]{:S(2)}, u32[]{:S(2)}) collective-permute-start(bf16[128,256]{1,0:T(8,128)(2,1)S(1)} %reduce_sum.19), channel_id=1, source_target_pairs={{0,0},{1,128},{2,256},{3,384},{4,4},{5,132},{6,260},{7,388},{8,8},... | collective-permute-start | bytes 196616 | tf_op jit(solution)/shard_map/ppermute | solution.py:78
  197.3 7.5 %collective-permute-done.6 = bf16[128,256]{1,0:T(8,128)(2,1)S(1)} collective-permute-done((bf16[128,256]{1,0:T(8,128)(2,1)S(1)}, bf16[128,256]{1,0:T(8,128)(2,1)S(1)}, u32[]{:S(2)}, u32[]{:S(2)}) %collective-permute-start.6) | collective-permute-done | bytes 65568 | tf_op jit(solution)/shard_map/ppermute | solution.py:78
  (33 shorter events, 15.3 us)
Async XLA Ops:
  0.0 94.4 %copy-start = (bf16[3,256,1024]{2,1,0:T(8,128)(2,1)S(1)}, bf16[3,256,1024]{2,1,0:T(8,128)(2,1)}, u32[]{:S(2)}) copy-start(bf16[3,256,1024]{2,1,0:T(8,128)(2,1)} %param.10) | copy-start | bytes 4718596
  42.0 5.1 %copy-start.3 = (bf16[3,256,1024]{2,1,0:T(8,128)(2,1)S(1)}, bf16[3,256,1024]{2,1,0:T(8,128)(2,1)}, u32[]{:S(2)}) copy-start(bf16[3,256,1024]{2,1,0:T(8,128)(2,1)} %param.11) | copy-start | bytes 4718596
  42.0 10.4 %copy-start.8 = (s32[16]{0:T(128)S(1)}, s32[16]{0:T(128)}, u32[]{:S(2)}) copy-start(s32[16]{0:T(128)} %param.13) | copy-start | bytes 196
  42.0 48.5 %all-to-all-start.1 = ((bf16[8,1024,128]{2,1,0:T(8,128)(2,1)}), bf16[8,1024,128]{2,1,0:T(8,128)(2,1)}, u32[]{:S(2)}, u32[]{:S(2)}) async-start(bf16[8,1024,128]{2,1,0:T(8,128)(2,1)} %broadcast_in_dim.30), calls=%async_computation.1 | async-start | bytes 4194304 | tf_op jit(solution)/shard_map/all_to_all | solution.py:40
  47.0 36.8 %collective-permute-start.3 = (bf16[3,256,1024]{2,1,0:T(8,128)(2,1)S(1)}, bf16[3,256,1024]{2,1,0:T(8,128)(2,1)}, u32[]{:S(2)}, u32[]{:S(2)}) collective-permute-start(bf16[3,256,1024]{2,1,0:T(8,128)(2,1)S(1)} %copy-done.3), channel_id=1, source_target_pairs={{0,1},{1,2},{2,3},{4,5},{5,6},{6,7},{8,9},{9,10},{10,11},{12,13},{... | collective-permute-start | bytes 4718600 | tf_op jit(solution)/shard_map/ppermute | solution.py:11
  51.1 38.1 %collective-permute-start = (bf16[3,256,1024]{2,1,0:T(8,128)(2,1)S(1)}, bf16[3,256,1024]{2,1,0:T(8,128)(2,1)}, u32[]{:S(2)}, u32[]{:S(2)}) collective-permute-start(bf16[3,256,1024]{2,1,0:T(8,128)(2,1)S(1)} %copy-done.3), channel_id=1, source_target_pairs={{1,0},{2,1},{3,2},{5,4},{6,5},{7,6},{9,8},{10,9},{11,10},{13,12},{... | collective-permute-start | bytes 4718600 | tf_op jit(solution)/shard_map/ppermute | solution.py:11
  83.9 20.3 %collective-permute-start.4 = (bf16[3,256,1024]{2,1,0:T(8,128)(2,1)}, bf16[3,256,1024]{2,1,0:T(8,128)(2,1)}, u32[]{:S(2)}, u32[]{:S(2)}) collective-permute-start(bf16[3,256,1024]{2,1,0:T(8,128)(2,1)} %collective-permute-done.3), channel_id=1, source_target_pairs={{1,2},{2,3},{5,6},{6,7},{9,10},{10,11},{13,14},{14,15},{17,18},{18... | collective-permute-start | bytes 4718600 | tf_op jit(solution)/shard_map/ppermute | solution.py:11
  89.2 37.5 %collective-permute-start.1 = (bf16[3,256,1024]{2,1,0:T(8,128)(2,1)}, bf16[3,256,1024]{2,1,0:T(8,128)(2,1)}, u32[]{:S(2)}, u32[]{:S(2)}) collective-permute-start(bf16[3,256,1024]{2,1,0:T(8,128)(2,1)} %collective-permute-done), channel_id=1, source_target_pairs={{1,0},{2,1},{5,4},{6,5},{9,8},{10,9},{13,12},{14,13},{17,16},{18,1... | collective-permute-start | bytes 4718600 | tf_op jit(solution)/shard_map/ppermute | solution.py:11
  99.2 28.8 %copy-start.2 = (f32[24,24]{1,0:T(8,128)S(1)}, f32[24,24]{1,0:T(8,128)}, u32[]{:S(2)}) copy-start(f32[24,24]{1,0:T(8,128)} %param.12) | copy-start | bytes 6916
  99.2 28.8 %all-to-all-start.2 = ((bf16[3,8,32,1024]{3,2,0,1:T(8,128)(2,1)}), bf16[3,8,32,1024]{3,2,0,1:T(8,128)(2,1)S(1)}, u32[]{:S(2)}, u32[]{:S(2)}) async-start(bf16[3,8,32,1024]{3,2,0,1:T(8,128)(2,1)} %copy.21), calls=%async_computation.2 | async-start | bytes 3145728 | tf_op jit(solution)/shard_map/all_to_all | solution.py:49
  104.1 52.7 %collective-permute-start.5 = (bf16[3,256,1024]{2,1,0:T(8,128)(2,1)}, bf16[3,256,1024]{2,1,0:T(8,128)(2,1)}, u32[]{:S(2)}, u32[]{:S(2)}) collective-permute-start(bf16[3,256,1024]{2,1,0:T(8,128)(2,1)} %collective-permute-done.4), channel_id=1, source_target_pairs={{2,3},{6,7},{10,11},{14,15},{18,19},{22,23},{26,27},{30,31},{34,35... | collective-permute-start | bytes 4718600 | tf_op jit(solution)/shard_map/ppermute | solution.py:11
  126.7 36.6 %collective-permute-start.2 = (bf16[3,256,1024]{2,1,0:T(8,128)(2,1)}, bf16[3,256,1024]{2,1,0:T(8,128)(2,1)}, u32[]{:S(2)}, u32[]{:S(2)}) collective-permute-start(bf16[3,256,1024]{2,1,0:T(8,128)(2,1)} %collective-permute-done.1), channel_id=1, source_target_pairs={{1,0},{5,4},{9,8},{13,12},{17,16},{21,20},{25,24},{29,28},{33,32},... | collective-permute-start | bytes 4718600 | tf_op jit(solution)/shard_map/ppermute | solution.py:11
  132.0 24.9 %all-to-all-start.3 = ((bf16[8,3,32,1024]{3,2,1,0:T(8,128)(2,1)}), bf16[8,3,32,1024]{3,2,1,0:T(8,128)(2,1)S(1)}, u32[]{:S(2)}, u32[]{:S(2)}) async-start(bf16[8,3,32,1024]{3,2,1,0:T(8,128)(2,1)} %bitcast.61), calls=%async_computation.3 | async-start | bytes 3145728 | tf_op jit(solution)/shard_map/all_to_all | solution.py:54
  167.3 2.2 %copy-start.4 = (bf16[3,256,1024]{2,1,0:T(8,128)(2,1)S(1)}, bf16[3,256,1024]{2,1,0:T(8,128)(2,1)}, u32[]{:S(2)}) copy-start(bf16[3,256,1024]{2,1,0:T(8,128)(2,1)} %get-tuple-element.52) | copy-start | bytes 4718596 | tf_op jit(solution)/shard_map/cond
  173.6 1.0 copy-start.1
  195.2 9.6 %collective-permute-start.6 = (bf16[128,256]{1,0:T(8,128)(2,1)S(1)}, bf16[128,256]{1,0:T(8,128)(2,1)S(1)}, u32[]{:S(2)}, u32[]{:S(2)}) collective-permute-start(bf16[128,256]{1,0:T(8,128)(2,1)S(1)} %reduce_sum.19), channel_id=1, source_target_pairs={{0,0},{1,128},{2,256},{3,384},{4,4},{5,132},{6,260},{7,388},{8,8},... | collective-permute-start | bytes 196616 | tf_op jit(solution)/shard_map/ppermute | solution.py:78

commit v6 on v2

--- a/solution.py
+++ b/solution.py
@@ -49,7 +49,8 @@
     halves = n_mpo // G
     term = term.reshape(halves, slab // halves, G, slab)
     term = jnp.transpose(term, (2, 0, 1, 3)).reshape(n_mpo, slab // halves, slab)
-    result = jnp.sum(lax.all_to_all(term, "mpo", 0, 0, tiled=False), axis=0).astype(jnp.bfloat16)
+    partials = lax.all_to_all(term.astype(jnp.bfloat16), "mpo", 0, 0, tiled=False)
+    result = jnp.sum(partials.astype(jnp.float32), axis=0).astype(jnp.bfloat16)
 
     pairs = []
     for src_m in range(n_mpo):

time: 189 us -> 182 us (0.963)
  blocking collectives: 85 us -> 79.4 us
    all_to_all x1, blocking collectives: 18.4 us -> 12.8 us  [on_device(): lax.all_to_all(term.astype(jnp.bfloat16), 'mpo', 0, 0, tiled=False)]
where the time goes in v6:
time: 182 us
  blocking collectives  79.4 us (44%)
  waiting for transfers between devices  54.4 us (30%)
  between operations  13.5 us (7%)
  matrix products  10.9 us (6%)
  local copies, waits for them, and re-layouts  10.7 us (6%)
  starting transfers between devices  10.1 us (6%)
  other arithmetic  2.89 us (2%)
    all_to_all x1, blocking collectives, on_device(): lax.all_to_all(spread, ('sg', 'k'), 0, 0, tiled=True).reshape(width, per)  42.6 us
    all_to_all x1, waiting for transfers between devices, on_device(): lax.all_to_all(everyone, 'mpo', 0, 2, tiled=True).reshape(width, width)  26 us
    all_to_all x1, blocking collectives, on_device(): lax.all_to_all(product, 'mpo', 1, 0, tiled=True)  24 us
    all_to_all x1, waiting for transfers between devices, on_device(): own_b = lax.all_to_all(mixed, 'mpo', 0, 0, tiled=False)  20.1 us
    all_to_all x1, blocking collectives, on_device(): lax.all_to_all(term.astype(jnp.bfloat16), 'mpo', 0, 0, tiled=False)  12.8 us
    ppermute x1, waiting for transfers between devices, on_device(): return lax.ppermute(result, ('mpo', 'sg', 'k'), pairs)  7.53 us
    dot_general x1, matrix products, on_device(): jnp.einsum('mbil,bjl->mij', own_b, right_all, preferred_element_type=jnp....  5.41 us
    all_to_all x1, starting transfers between devices, on_device(): lax.all_to_all(everyone, 'mpo', 0, 2, tiled=True).reshape(width, width)  4.65 us
  transfers between devices with their start and end apart: 4, of which 3 were waited for; matrix products, arithmetic and copies ran while one was open for 9% of the time, Pallas kernels for 0%

profile of v6, /device:TPU:70, one launch (start us, length us, event | category | flops | bytes accessed | tf_op | source)
XLA Modules:
  0.0 181.8 jit_solution(10082707445298096907)
XLA Ops:
  6.5 0.7 all-gather.2.cloned.1.call-update
  7.3 0.8 constant_dynamic-slice_fusion
  8.2 42.6 %all_to_all.45 = bf16[64,16,128]{2,1,0:T(8,128)(2,1)S(1)} all-to-all(bf16[64,16,128]{2,1,0:T(8,128)(2,1)S(1)} %bitcast.44), channel_id=1, replica_groups=mesh['mpo'=8,'sg'=16,'k'=4] {'sg','k'}, dimensions={0} | all-to-all | bytes 524288 | tf_op jit(solution)/shard_map/all_to_all | solution.py:25
  50.8 1.6 broadcast_in_dim.30
  52.4 4.6 %all-to-all-start.1 = ((bf16[8,1024,128]{2,1,0:T(8,128)(2,1)}), bf16[8,1024,128]{2,1,0:T(8,128)(2,1)}, u32[]{:S(2)}, u32[]{:S(2)}) async-start(bf16[8,1024,128]{2,1,0:T(8,128)(2,1)} %broadcast_in_dim.30), calls=%async_computation.1 | async-start | bytes 4194304 | tf_op jit(solution)/shard_map/all_to_all | solution.py:27
  57.0 0.6 fusion.20
  57.7 0.6 iota_compare_fusion
  58.3 26.0 %all-to-all-done.1 = bf16[8,1024,128]{2,1,0:T(8,128)(2,1)} async-done(((bf16[8,1024,128]{2,1,0:T(8,128)(2,1)}), bf16[8,1024,128]{2,1,0:T(8,128)(2,1)}, u32[]{:S(2)}, u32[]{:S(2)}) %all-to-all-start.1) | async-done | bytes 2097184 | tf_op jit(solution)/shard_map/all_to_all | solution.py:27
  84.3 3.9 %copy.19 = bf16[8,1024,128]{1,2,0:T(8,128)(2,1)} copy(bf16[8,1024,128]{2,1,0:T(8,128)(2,1)} %all-to-all-done.1) | data formatting | bytes 4194304 | tf_op jit(solution)/shard_map/all_to_all | solution.py:27
  88.2 3.5 %fusion.7 = bf16[1024,3,256]{0,2,1:T(8,128)(2,1)S(1)} fusion(bf16[3,256,1024]{2,1,0:T(8,128)(2,1)S(1)} %copy-done, bf16[1024,1024]{0,1:T(8,128)(2,1)} %bitcast.40, pred[1024]{0:T(1024)(128)(4,1)S(1)} %iota_compare_fusion), kind=kOutput, calls=%fused_computation.7 | convolution fusion | flops 1613496320 | bytes 5243904 | tf_op jit(solution)/shard_map/akm,mn->akn/dot_general | solution.py:32
  91.9 24.0 %all_to_all.46 = bf16[3,8,32,1024]{3,2,0,1:T(8,128)(2,1)S(1)} all-to-all(bf16[3,8,32,1024]{3,2,0,1:T(8,128)(2,1)S(1)} %copy.21), channel_id=1, replica_groups=mesh['mpo'=8,'sg'=16,'k'=4] {'mpo'}, dimensions={1} | all-to-all | bytes 3145728 | tf_op jit(solution)/shard_map/all_to_all | solution.py:37
  115.9 2.0 %fusion.11 = bf16[24,32,1024]{2,0,1:T(8,128)(2,1)S(1)} fusion(bf16[24,32,1024]{2,1,0:T(8,128)(2,1)S(1)} %bitcast.39, f32[24,24]{1,0:T(8,128)S(1)} %copy-done.1), kind=kOutput, calls=%fused_computation.10 | convolution fusion | flops 227278848 | bytes 3148032 | tf_op jit(solution)/shard_map/ab,akn->bkn/dot_general | solution.py:38
  117.9 2.0 %copy.24 = bf16[24,32,1024]{2,1,0:T(8,128)(2,1)} copy(bf16[24,32,1024]{2,0,1:T(8,128)(2,1)S(1)} %fusion.11) | data formatting | bytes 3145728 | tf_op jit(solution)/shard_map/convert_element_type | solution.py:40
  119.9 3.6 %all-to-all-start.3 = ((bf16[8,3,32,1024]{3,2,1,0:T(8,128)(2,1)}), bf16[8,3,32,1024]{3,2,1,0:T(8,128)(2,1)S(1)}, u32[]{:S(2)}, u32[]{:S(2)}) async-start(bf16[8,3,32,1024]{3,2,1,0:T(8,128)(2,1)} %bitcast.13), calls=%async_computation.3 | async-start | bytes 3145728 | tf_op jit(solution)/shard_map/all_to_all | solution.py:42
  123.5 0.7 add_compare_fusion.1
  124.2 0.7 add_compare_fusion
  124.8 20.1 %all-to-all-done.3 = bf16[8,3,32,1024]{3,2,1,0:T(8,128)(2,1)S(1)} async-done(((bf16[8,3,32,1024]{3,2,1,0:T(8,128)(2,1)}), bf16[8,3,32,1024]{3,2,1,0:T(8,128)(2,1)S(1)}, u32[]{:S(2)}, u32[]{:S(2)}) %all-to-all-start.3) | async-done | bytes 1572896 | tf_op jit(solution)/shard_map/all_to_all | solution.py:42
  145.0 5.4 %fusion.14 = bf16[8,32,1024]{2,1,0:T(8,128)(2,1)} fusion(bf16[8,3,32,1024]{3,2,1,0:T(8,128)(2,1)S(1)} %all-to-all-done.3, bf16[3,1024,1024]{2,1,0:T(8,128)(2,1)} %all-gather.2.cloned.1.call-done), kind=kOutput, calls=%fused_computation.11 | convolution fusion | flops 1610612736 | bytes 8388608 | tf_op jit(solution)/shard_map/mbil,bjl->mij/dot_general | solution.py:44
  150.4 1.4 reshape.55
  151.8 0.2 fusion.17
  152.1 12.8 %all_to_all.47 = bf16[8,128,256]{2,1,0:T(8,128)(2,1)S(1)} all-to-all(bf16[8,128,256]{2,1,0:T(8,128)(2,1)S(1)} %bitcast.41), channel_id=1, replica_groups=mesh['mpo'=8,'sg'=16,'k'=4] {'mpo'}, dimensions={0} | all-to-all | bytes 1048576 | tf_op jit(solution)/shard_map/all_to_all | solution.py:52
  164.9 1.9 %collective-permute-start = (bf16[128,256]{1,0:T(8,128)(2,1)S(1)}, bf16[128,256]{1,0:T(8,128)(2,1)S(1)}, u32[]{:S(2)}, u32[]{:S(2)}) collective-permute-start(bf16[128,256]{1,0:T(8,128)(2,1)S(1)} %reduce_sum.22), channel_id=1, source_target_pairs={{0,0},{1,128},{2,256},{3,384},{4,4},{5,132},{6,260},{7,388},{8,8},... | collective-permute-start | bytes 196616 | tf_op jit(solution)/shard_map/ppermute | solution.py:62
  166.8 7.5 %collective-permute-done = bf16[128,256]{1,0:T(8,128)(2,1)S(1)} collective-permute-done((bf16[128,256]{1,0:T(8,128)(2,1)S(1)}, bf16[128,256]{1,0:T(8,128)(2,1)S(1)}, u32[]{:S(2)}, u32[]{:S(2)}) %collective-permute-start) | collective-permute-done | bytes 65568 | tf_op jit(solution)/shard_map/ppermute | solution.py:62
  174.4 0.6 copy.39
  (11 shorter events, 0.3 us)
Async XLA Ops:
  6.5 81.7 %copy-start = (bf16[3,256,1024]{2,1,0:T(8,128)(2,1)S(1)}, bf16[3,256,1024]{2,1,0:T(8,128)(2,1)}, u32[]{:S(2)}) copy-start(bf16[3,256,1024]{2,1,0:T(8,128)(2,1)} %param.6) | copy-start | bytes 4718596
  6.5 138.4 %all-gather.2.cloned.1.call-start = ((), (), s32[]{:S(2)}) async-start(), calls=%async_computation.5 | async-start | bytes 7864320 | tf_op jit(solution)/shard_map/all_gather | solution.py:20
  52.4 4.7 %copy-start.2 = (s32[16]{0:T(128)S(1)}, s32[16]{0:T(128)}, u32[]{:S(2)}) copy-start(s32[16]{0:T(128)} %param.9) | copy-start | bytes 196
  52.4 31.9 %all-to-all-start.1 = ((bf16[8,1024,128]{2,1,0:T(8,128)(2,1)}), bf16[8,1024,128]{2,1,0:T(8,128)(2,1)}, u32[]{:S(2)}, u32[]{:S(2)}) async-start(bf16[8,1024,128]{2,1,0:T(8,128)(2,1)} %broadcast_in_dim.30), calls=%async_computation.1 | async-start | bytes 4194304 | tf_op jit(solution)/shard_map/all_to_all | solution.py:27
  91.9 24.0 %copy-start.1 = (f32[24,24]{1,0:T(8,128)S(1)}, f32[24,24]{1,0:T(8,128)}, u32[]{:S(2)}) copy-start(f32[24,24]{1,0:T(8,128)} %param.8) | copy-start | bytes 6916
  119.9 25.1 %all-to-all-start.3 = ((bf16[8,3,32,1024]{3,2,1,0:T(8,128)(2,1)}), bf16[8,3,32,1024]{3,2,1,0:T(8,128)(2,1)S(1)}, u32[]{:S(2)}, u32[]{:S(2)}) async-start(bf16[8,3,32,1024]{3,2,1,0:T(8,128)(2,1)} %bitcast.13), calls=%async_computation.3 | async-start | bytes 3145728 | tf_op jit(solution)/shard_map/all_to_all | solution.py:42
  164.9 9.5 %collective-permute-start = (bf16[128,256]{1,0:T(8,128)(2,1)S(1)}, bf16[128,256]{1,0:T(8,128)(2,1)S(1)}, u32[]{:S(2)}, u32[]{:S(2)}) collective-permute-start(bf16[128,256]{1,0:T(8,128)(2,1)S(1)} %reduce_sum.22), channel_id=1, source_target_pairs={{0,0},{1,128},{2,256},{3,384},{4,4},{5,132},{6,260},{7,388},{8,8},... | collective-permute-start | bytes 196616 | tf_op jit(solution)/shard_map/ppermute | solution.py:62
Sparse Core Ops, SparseCore 0:
  9.4 131.1 all-gather.1

commit v7 on v2

v7 whole, which is shorter than its diff:
```python
import jax
import jax.numpy as jnp
import numpy as np
from jax import lax
from jax.sharding import Mesh, PartitionSpec as P

G = 4
MPO = ("y", "c")


def on_device(theta, env_left, env_right, mpo_core, sector_sizes):
    sectors, rows_local, width = theta.shape
    local_w, slab, _ = env_left.shape
    n_mpo = lax.axis_size(MPO)
    n_sg = lax.axis_size("sg")
    mm = lax.axis_index(MPO)
    sector = lax.axis_index("sg")
    k = lax.axis_index("k")
    live_size = jnp.sum(jnp.where(jnp.arange(sectors, dtype=jnp.int32) == sector, sector_sizes, 0))

    right_all = lax.all_gather(env_right, "k", axis=1, tiled=True)

    per = width // n_mpo
    sel = lax.dynamic_slice_in_dim(theta, mm * per, per, axis=2)
    spread = jnp.broadcast_to(sel[:, None], (sectors, G, rows_local, per)).reshape(sectors * G, rows_local, per)
    part = lax.all_to_all(spread, ("sg", "k"), 0, 0, tiled=True).reshape(width, per)
    everyone = jnp.broadcast_to(part[None], (n_mpo,) + part.shape)
    block = lax.all_to_all(everyone, MPO, 0, 2, tiled=True).reshape(width, width)
    positions = jnp.arange(width, dtype=jnp.int32)
    keep = positions < live_size
    block = jnp.where(keep[:, None] & keep[None, :], block, jnp.zeros_like(block))

    product = jnp.einsum(
        "akm,mn->akn", env_left, block, preferred_element_type=jnp.float32
    ).astype(jnp.bfloat16)
    sub = slab // n_mpo
    product = product.reshape(local_w, n_mpo, sub, width)
    all_a = lax.all_to_all(product, MPO, 1, 0, tiled=True).reshape(local_w * n_mpo, sub, width)
    mixed = jnp.einsum(
        "ab,akn->bkn", mpo_core, all_a.astype(jnp.float32), precision=lax.Precision.HIGHEST
    ).astype(jnp.bfloat16)
    mixed = mixed.reshape(n_mpo, local_w, sub, width)
    own_b = lax.all_to_all(mixed, MPO, 0, 0, tiled=False)

    term = jnp.einsum(
        "mbil,bjl->mij", own_b, right_all, preferred_element_type=jnp.float32
    ).reshape(slab, width)
    row_keep = k * slab + jnp.arange(slab, dtype=jnp.int32) < live_size
    term = jnp.where(row_keep[:, None] & keep[None, :], term, jnp.zeros_like(term))
    halves = n_mpo // G
    term = term.reshape(halves, slab // halves, G, slab)
    term = jnp.transpose(term, (2, 0, 1, 3)).reshape(n_mpo, slab // halves, slab)
    n_c = lax.axis_size("c")
    c = lax.axis_index("c")
    term = term.reshape(n_mpo // n_c, n_c, slab // halves, slab)
    mine = lax.dynamic_index_in_dim(term, c, 1, keepdims=False)
    other = lax.dynamic_index_in_dim(term, 1 - c, 1, keepdims=False)
    pair = mine + lax.ppermute(other, "c", [(0, 1), (1, 0)])
    result = jnp.sum(lax.all_to_all(pair, "y", 0, 0, tiled=False), axis=0).astype(jnp.bfloat16)

    pairs = []
    for src_m in range(n_mpo):
        for g in range(n_sg):
            for kk in range(G):
                dst_m = halves * kk + src_m % halves
                dst_k = src_m // halves
                pairs.append(((src_m * n_sg + g) * G + kk, (dst_m * n_sg + g) * G + dst_k))
    return lax.ppermute(result, MPO + ("sg", "k"), pairs)


def solution(mesh):
    devices = np.asarray(mesh.devices)
    n_mpo, n_sec = devices.shape
    grid = Mesh(devices.reshape(n_mpo // 2, 2, n_sec // G, G), ("y", "c", "sg", "k"))
    sec = ("sg", "k")
    mpo = ("y", "c")
    return jax.shard_map(
        on_device,
        mesh=grid,
        in_specs=(P(None, sec, None), P(mpo, sec, None), P(mpo, sec, None), P(), P()),
        out_specs=P(mpo, sec),
        check_vma=False,
    )
```

time: 189 us -> 190 us (level)
  blocking collectives: 85 us -> 79.1 us
  waiting for transfers between devices: 54.4 us -> 56.5 us
  starting transfers between devices: 10.1 us -> 12.1 us
    all_to_all x2, blocking collectives: 42.4 us -> 36.5 us  [the longest x1 24 us: on_device(): lax.all_to_all(product, MPO, 1, 0, tiled=True)]
    ppermute x1 -> x2, waiting for transfers between devices: 7.53 us -> 9.62 us  [the longest x1 7.53 us: on_device(): return lax.ppermute(result, MPO + ('sg', 'k'), pairs)]
    ppermute x1 -> x2, starting transfers between devices: 1.92 us -> 3.83 us  [the longest x1 1.92 us: on_device(): return lax.ppermute(result, MPO + ('sg', 'k'), pairs)]
  transfers between devices with their start and end apart: 4 -> 5, of which waited for: 3 -> 4; matrix products, arithmetic and copies ran while one was open for 9% -> 9% of each run, Pallas kernels for 0% -> 0%
where the time goes in v7:
time: 190 us; the launch traced here: 189 us
  blocking collectives  79.1 us (42%)
  waiting for transfers between devices  56.5 us (30%)
  between operations  13.5 us (7%)
  local copies, waits for them, and re-layouts  12.7 us (7%)
  starting transfers between devices  12.1 us (6%)
  matrix products  11 us (6%)
  other arithmetic  4.22 us (2%)
    all_to_all x1, blocking collectives, on_device(): lax.all_to_all(spread, ('sg', 'k'), 0, 0, tiled=True).reshape(width, per)  42.6 us
    all_to_all x1, waiting for transfers between devices, on_device(): lax.all_to_all(everyone, MPO, 0, 2, tiled=True).reshape(width, width)  26 us
    all_to_all x1, blocking collectives, on_device(): lax.all_to_all(product, MPO, 1, 0, tiled=True)  24 us
    all_to_all x1, waiting for transfers between devices, on_device(): own_b = lax.all_to_all(mixed, MPO, 0, 0, tiled=False)  20.1 us
    all_to_all x1, blocking collectives, on_device(): lax.all_to_all(pair, 'y', 0, 0, tiled=False)  12.5 us
    ppermute x1, waiting for transfers between devices, on_device(): return lax.ppermute(result, MPO + ('sg', 'k'), pairs)  7.53 us
    dot_general x1, matrix products, on_device(): jnp.einsum('mbil,bjl->mij', own_b, right_all, preferred_element_type=jnp....  5.61 us
    all_to_all x1, starting transfers between devices, on_device(): lax.all_to_all(everyone, MPO, 0, 2, tiled=True).reshape(width, width)  4.65 us
  transfers between devices with their start and end apart: 5, of which 4 were waited for; matrix products, arithmetic and copies ran while one was open for 9% of the time, Pallas kernels for 0%

profile of v7, /device:TPU:70, one launch (start us, length us, event | category | flops | bytes accessed | tf_op | source)
XLA Modules:
  0.0 189.1 jit_solution(9324012906809128591)
XLA Ops:
  6.5 0.7 all-gather.2.cloned.1.call-update
  7.3 0.8 constant_dynamic-slice_fusion
  8.2 42.6 %all_to_all.45 = bf16[64,16,128]{2,1,0:T(8,128)(2,1)S(1)} all-to-all(bf16[64,16,128]{2,1,0:T(8,128)(2,1)S(1)} %bitcast.48), channel_id=1, replica_groups=mesh['y'=4,'c'=2,'sg'=16,'k'=4] {'sg','k'}, dimensions={0} | all-to-all | bytes 524288 | tf_op jit(solution)/shard_map/all_to_all | solution.py:26
  50.8 1.6 broadcast_in_dim.30
  52.4 4.6 %all-to-all-start.1 = ((bf16[8,1024,128]{2,1,0:T(8,128)(2,1)}), bf16[8,1024,128]{2,1,0:T(8,128)(2,1)}, u32[]{:S(2)}, u32[]{:S(2)}) async-start(bf16[8,1024,128]{2,1,0:T(8,128)(2,1)} %broadcast_in_dim.30), calls=%async_computation.1 | async-start | bytes 4194304 | tf_op jit(solution)/shard_map/all_to_all | solution.py:28
  58.3 26.0 %all-to-all-done.1 = bf16[8,1024,128]{2,1,0:T(8,128)(2,1)} async-done(((bf16[8,1024,128]{2,1,0:T(8,128)(2,1)}), bf16[8,1024,128]{2,1,0:T(8,128)(2,1)}, u32[]{:S(2)}, u32[]{:S(2)}) %all-to-all-start.1) | async-done | bytes 2097184 | tf_op jit(solution)/shard_map/all_to_all | solution.py:28
  84.3 3.9 %copy.18 = bf16[8,1024,128]{1,2,0:T(8,128)(2,1)} copy(bf16[8,1024,128]{2,1,0:T(8,128)(2,1)} %all-to-all-done.1) | data formatting | bytes 4194304 | tf_op jit(solution)/shard_map/all_to_all | solution.py:28
  88.2 3.5 %fusion.7 = bf16[1024,3,256]{0,2,1:T(8,128)(2,1)S(1)} fusion(bf16[3,256,1024]{2,1,0:T(8,128)(2,1)S(1)} %copy-done, bf16[1024,1024]{0,1:T(8,128)(2,1)} %bitcast.45, pred[1024]{0:T(1024)(128)(4,1)S(1)} %iota_compare_fusion), kind=kOutput, calls=%fused_computation.7 | convolution fusion | flops 1613496320 | bytes 5243904 | tf_op jit(solution)/shard_map/akm,mn->akn/dot_general | solution.py:33
  91.9 24.0 %all_to_all.46 = bf16[3,8,32,1024]{3,2,0,1:T(8,128)(2,1)S(1)} all-to-all(bf16[3,8,32,1024]{3,2,0,1:T(8,128)(2,1)S(1)} %copy.20), channel_id=1, replica_groups=mesh['y'=4,'c'=2,'sg'=16,'k'=4] {'y','c'}, dimensions={1} | all-to-all | bytes 3145728 | tf_op jit(solution)/shard_map/all_to_all | solution.py:38
  115.9 2.0 %fusion.11 = bf16[24,32,1024]{2,0,1:T(8,128)(2,1)S(1)} fusion(bf16[24,32,1024]{2,1,0:T(8,128)(2,1)S(1)} %bitcast.44, f32[24,24]{1,0:T(8,128)S(1)} %copy-done.1), kind=kOutput, calls=%fused_computation.10 | convolution fusion | flops 227278848 | bytes 3148032 | tf_op jit(solution)/shard_map/ab,akn->bkn/dot_general | solution.py:39
  117.9 2.0 %copy.23 = bf16[24,32,1024]{2,1,0:T(8,128)(2,1)} copy(bf16[24,32,1024]{2,0,1:T(8,128)(2,1)S(1)} %fusion.11) | data formatting | bytes 3145728 | tf_op jit(solution)/shard_map/convert_element_type | solution.py:41
  119.9 3.6 %all-to-all-start.3 = ((bf16[8,3,32,1024]{3,2,1,0:T(8,128)(2,1)}), bf16[8,3,32,1024]{3,2,1,0:T(8,128)(2,1)S(1)}, u32[]{:S(2)}, u32[]{:S(2)}) async-start(bf16[8,3,32,1024]{3,2,1,0:T(8,128)(2,1)} %bitcast.13), calls=%async_computation.3 | async-start | bytes 3145728 | tf_op jit(solution)/shard_map/all_to_all | solution.py:43
  123.5 0.7 add_compare_fusion.1
  124.1 0.7 add_compare_fusion
  124.8 20.1 %all-to-all-done.3 = bf16[8,3,32,1024]{3,2,1,0:T(8,128)(2,1)S(1)} async-done(((bf16[8,3,32,1024]{3,2,1,0:T(8,128)(2,1)}), bf16[8,3,32,1024]{3,2,1,0:T(8,128)(2,1)S(1)}, u32[]{:S(2)}, u32[]{:S(2)}) %all-to-all-start.3) | async-done | bytes 1572896 | tf_op jit(solution)/shard_map/all_to_all | solution.py:43
  144.9 5.6 %fusion.14 = f32[8,32,1024]{2,1,0:T(8,128)} fusion(bf16[8,3,32,1024]{3,2,1,0:T(8,128)(2,1)S(1)} %all-to-all-done.3, bf16[3,1024,1024]{2,1,0:T(8,128)(2,1)} %all-gather.2.cloned.1.call-done), kind=kOutput, calls=%fused_computation.11 | convolution fusion | flops 1610612736 | bytes 8912896 | tf_op jit(solution)/shard_map/mbil,bjl->mij/dot_general | solution.py:45
  150.6 2.7 %reshape.53 = f32[2,128,4,256]{3,2,1,0:T(4,128)} reshape(f32[8,32,1024]{2,1,0:T(8,128)} %fusion.14) | data formatting | bytes 2097152 | tf_op jit(solution)/shard_map/reshape | solution.py:47
  153.2 1.5 copy_select_fusion
  154.7 0.8 dynamic-slice_bitcast_fusion
  155.6 1.9 %collective-permute-start = (f32[4,128,256]{2,1,0:T(8,128)}, f32[4,128,256]{2,1,0:T(8,128)S(1)}, u32[]{:S(2)}, u32[]{:S(2)}) collective-permute-start(f32[4,128,256]{2,1,0:T(8,128)} %dynamic-slice_bitcast_fusion), channel_id=1, source_target_pairs={{0,64},{64,0},{1,65},{65,1},{2,66},{66,2},{3,67},{67,3},{4,68},{68... | collective-permute-start | bytes 1572872 | tf_op jit(solution)/shard_map/ppermute | solution.py:58
  157.5 2.1 %collective-permute-done = f32[4,128,256]{2,1,0:T(8,128)S(1)} collective-permute-done((f32[4,128,256]{2,1,0:T(8,128)}, f32[4,128,256]{2,1,0:T(8,128)S(1)}, u32[]{:S(2)}, u32[]{:S(2)}) %collective-permute-start) | collective-permute-done | bytes 524320 | tf_op jit(solution)/shard_map/ppermute | solution.py:58
  159.7 12.5 %all_to_all.47 = f32[4,128,256]{2,1,0:T(8,128)S(1)} all-to-all(f32[4,128,256]{2,1,0:T(8,128)S(1)} %bitcast_add_fusion), channel_id=1, replica_groups=mesh['y'=4,'c'=2,'sg'=16,'k'=4] {'y'}, dimensions={0} | all-to-all | bytes 1048576 | tf_op jit(solution)/shard_map/all_to_all | solution.py:59
  172.1 1.9 %collective-permute-start.1 = (bf16[128,256]{1,0:T(8,128)(2,1)S(1)}, bf16[128,256]{1,0:T(8,128)(2,1)S(1)}, u32[]{:S(2)}, u32[]{:S(2)}) collective-permute-start(bf16[128,256]{1,0:T(8,128)(2,1)S(1)} %reduce_sum.19), channel_id=1, source_target_pairs={{0,0},{1,128},{2,256},{3,384},{4,4},{5,132},{6,260},{7,388},{8,8},... | collective-permute-start | bytes 196616 | tf_op jit(solution)/shard_map/ppermute | solution.py:68
  174.1 7.5 %collective-permute-done.1 = bf16[128,256]{1,0:T(8,128)(2,1)S(1)} collective-permute-done((bf16[128,256]{1,0:T(8,128)(2,1)S(1)}, bf16[128,256]{1,0:T(8,128)(2,1)S(1)}, u32[]{:S(2)}, u32[]{:S(2)}) %collective-permute-start.1) | collective-permute-done | bytes 65568 | tf_op jit(solution)/shard_map/ppermute | solution.py:68
  (15 shorter events, 2.2 us)
Async XLA Ops:
  6.5 81.7 %copy-start = (bf16[3,256,1024]{2,1,0:T(8,128)(2,1)S(1)}, bf16[3,256,1024]{2,1,0:T(8,128)(2,1)}, u32[]{:S(2)}) copy-start(bf16[3,256,1024]{2,1,0:T(8,128)(2,1)} %param.6) | copy-start | bytes 4718596
  6.5 138.4 %all-gather.2.cloned.1.call-start = ((), (), s32[]{:S(2)}) async-start(), calls=%async_computation.5 | async-start | bytes 7864320 | tf_op jit(solution)/shard_map/all_gather | solution.py:21
  52.4 4.7 %copy-start.2 = (s32[16]{0:T(128)S(1)}, s32[16]{0:T(128)}, u32[]{:S(2)}) copy-start(s32[16]{0:T(128)} %param.9) | copy-start | bytes 196
  52.4 31.9 %all-to-all-start.1 = ((bf16[8,1024,128]{2,1,0:T(8,128)(2,1)}), bf16[8,1024,128]{2,1,0:T(8,128)(2,1)}, u32[]{:S(2)}, u32[]{:S(2)}) async-start(bf16[8,1024,128]{2,1,0:T(8,128)(2,1)} %broadcast_in_dim.30), calls=%async_computation.1 | async-start | bytes 4194304 | tf_op jit(solution)/shard_map/all_to_all | solution.py:28
  91.9 24.0 %copy-start.1 = (f32[24,24]{1,0:T(8,128)S(1)}, f32[24,24]{1,0:T(8,128)}, u32[]{:S(2)}) copy-start(f32[24,24]{1,0:T(8,128)} %param.8) | copy-start | bytes 6916
  119.9 25.1 %all-to-all-start.3 = ((bf16[8,3,32,1024]{3,2,1,0:T(8,128)(2,1)}), bf16[8,3,32,1024]{3,2,1,0:T(8,128)(2,1)S(1)}, u32[]{:S(2)}, u32[]{:S(2)}) async-start(bf16[8,3,32,1024]{3,2,1,0:T(8,128)(2,1)} %bitcast.13), calls=%async_computation.3 | async-start | bytes 3145728 | tf_op jit(solution)/shard_map/all_to_all | solution.py:43
  155.6 4.0 %collective-permute-start = (f32[4,128,256]{2,1,0:T(8,128)}, f32[4,128,256]{2,1,0:T(8,128)S(1)}, u32[]{:S(2)}, u32[]{:S(2)}) collective-permute-start(f32[4,128,256]{2,1,0:T(8,128)} %dynamic-slice_bitcast_fusion), channel_id=1, source_target_pairs={{0,64},{64,0},{1,65},{65,1},{2,66},{66,2},{3,67},{67,3},{4,68},{68... | collective-permute-start | bytes 1572872 | tf_op jit(solution)/shard_map/ppermute | solution.py:58
  172.1 9.5 %collective-permute-start.1 = (bf16[128,256]{1,0:T(8,128)(2,1)S(1)}, bf16[128,256]{1,0:T(8,128)(2,1)S(1)}, u32[]{:S(2)}, u32[]{:S(2)}) collective-permute-start(bf16[128,256]{1,0:T(8,128)(2,1)S(1)} %reduce_sum.19), channel_id=1, source_target_pairs={{0,0},{1,128},{2,256},{3,384},{4,4},{5,132},{6,260},{7,388},{8,8},... | collective-permute-start | bytes 196616 | tf_op jit(solution)/shard_map/ppermute | solution.py:68
Sparse Core Ops, SparseCore 0:
  9.4 131.1 all-gather.1

commit v8 on v2

--- a/solution.py
+++ b/solution.py
@@ -17,7 +17,7 @@
     k = lax.axis_index("k")
     live_size = jnp.sum(jnp.where(jnp.arange(sectors, dtype=jnp.int32) == sector, sector_sizes, 0))
 
-    right_all = lax.all_gather(env_right, "k", axis=1, tiled=True)
+    right_all = lax.all_gather(env_right, "k", axis=0, tiled=False)
 
     per = width // n_mpo
     sel = lax.dynamic_slice_in_dim(theta, mm * per, per, axis=2)
@@ -42,7 +42,7 @@
     own_b = lax.all_to_all(mixed, "mpo", 0, 0, tiled=False)
 
     term = jnp.einsum(
-        "mbil,bjl->mij", own_b, right_all, preferred_element_type=jnp.float32
+        "mbil,qbjl->miqj", own_b, right_all, preferred_element_type=jnp.float32
     ).reshape(slab, width)
     row_keep = k * slab + jnp.arange(slab, dtype=jnp.int32) < live_size
     term = jnp.where(row_keep[:, None] & keep[None, :], term, jnp.zeros_like(term))

time: 189 us -> 186 us (0.984)
  no operation moved by 1% of the time
where the time goes in v8:
time: 186 us; the launch traced here: 185 us
  blocking collectives  85 us (46%)
  waiting for transfers between devices  54.4 us (29%)
  between operations  13.5 us (7%)
  starting transfers between devices  10.1 us (5%)
  matrix products  10 us (5%)
  local copies, waits for them, and re-layouts  9.25 us (5%)
  other arithmetic  2.84 us (2%)
    all_to_all x1, blocking collectives, on_device(): lax.all_to_all(spread, ('sg', 'k'), 0, 0, tiled=True).reshape(width, per)  42.6 us
    all_to_all x1, waiting for transfers between devices, on_device(): lax.all_to_all(everyone, 'mpo', 0, 2, tiled=True).reshape(width, width)  26 us
    all_to_all x1, blocking collectives, on_device(): lax.all_to_all(product, 'mpo', 1, 0, tiled=True)  24 us
    all_to_all x1, waiting for transfers between devices, on_device(): own_b = lax.all_to_all(mixed, 'mpo', 0, 0, tiled=False)  20.1 us
    all_to_all x1, blocking collectives, on_device(): lax.all_to_all(term, 'mpo', 0, 0, tiled=False)  18.4 us
    ppermute x1, waiting for transfers between devices, on_device(): return lax.ppermute(result, ('mpo', 'sg', 'k'), pairs)  7.53 us
    all_to_all x1, starting transfers between devices, on_device(): lax.all_to_all(everyone, 'mpo', 0, 2, tiled=True).reshape(width, width)  4.64 us
    dot_general x1, matrix products, on_device(): jnp.einsum('mbil,qbjl->miqj', own_b, right_all, preferred_element_type=jn...  4.6 us
  transfers between devices with their start and end apart: 4, of which 3 were waited for; matrix products, arithmetic and copies ran while one was open for 9% of the time, Pallas kernels for 0%

profile of v8, /device:TPU:70, one launch (start us, length us, event | category | flops | bytes accessed | tf_op | source)
XLA Modules:
  0.0 185.2 jit_solution(16475044044723621790)
XLA Ops:
  6.5 0.7 all-gather.3.cloned.1.call-update
  7.3 0.8 constant_dynamic-slice_fusion
  8.2 42.6 %all_to_all.45 = bf16[64,16,128]{2,1,0:T(8,128)(2,1)S(1)} all-to-all(bf16[64,16,128]{2,1,0:T(8,128)(2,1)S(1)} %bitcast.47), channel_id=1, replica_groups=mesh['mpo'=8,'sg'=16,'k'=4] {'sg','k'}, dimensions={0} | all-to-all | bytes 524288 | tf_op jit(solution)/shard_map/all_to_all | solution.py:25
  50.8 1.6 broadcast_in_dim.30
  52.4 4.6 %all-to-all-start.1 = ((bf16[8,1024,128]{2,1,0:T(8,128)(2,1)}), bf16[8,1024,128]{2,1,0:T(8,128)(2,1)}, u32[]{:S(2)}, u32[]{:S(2)}) async-start(bf16[8,1024,128]{2,1,0:T(8,128)(2,1)} %broadcast_in_dim.30), calls=%async_computation.1 | async-start | bytes 4194304 | tf_op jit(solution)/shard_map/all_to_all | solution.py:27
  57.0 0.6 fusion.16
  57.7 0.6 iota_compare_fusion
  58.3 26.0 %all-to-all-done.1 = bf16[8,1024,128]{2,1,0:T(8,128)(2,1)} async-done(((bf16[8,1024,128]{2,1,0:T(8,128)(2,1)}), bf16[8,1024,128]{2,1,0:T(8,128)(2,1)}, u32[]{:S(2)}, u32[]{:S(2)}) %all-to-all-start.1) | async-done | bytes 2097184 | tf_op jit(solution)/shard_map/all_to_all | solution.py:27
  84.3 3.9 %copy.19 = bf16[8,1024,128]{1,2,0:T(8,128)(2,1)} copy(bf16[8,1024,128]{2,1,0:T(8,128)(2,1)} %all-to-all-done.1) | data formatting | bytes 4194304 | tf_op jit(solution)/shard_map/all_to_all | solution.py:27
  88.2 3.5 %fusion.5 = bf16[1024,3,256]{0,2,1:T(8,128)(2,1)S(1)} fusion(bf16[3,256,1024]{2,1,0:T(8,128)(2,1)S(1)} %copy-done, bf16[1024,1024]{0,1:T(8,128)(2,1)} %bitcast.44, pred[1024]{0:T(1024)(128)(4,1)S(1)} %iota_compare_fusion), kind=kOutput, calls=%fused_computation.5 | convolution fusion | flops 1613496320 | bytes 5243904 | tf_op jit(solution)/shard_map/akm,mn->akn/dot_general | solution.py:32
  91.7 0.2 copy.21
  91.9 24.0 %all_to_all.46 = bf16[3,8,32,1024]{3,2,0,1:T(8,128)(2,1)S(1)} all-to-all(bf16[3,8,32,1024]{3,2,0,1:T(8,128)(2,1)S(1)} %copy.21), channel_id=1, replica_groups=mesh['mpo'=8,'sg'=16,'k'=4] {'mpo'}, dimensions={1} | all-to-all | bytes 3145728 | tf_op jit(solution)/shard_map/all_to_all | solution.py:37
  115.9 2.0 %fusion.11 = bf16[24,32,1024]{2,0,1:T(8,128)(2,1)S(1)} fusion(bf16[24,32,1024]{2,1,0:T(8,128)(2,1)S(1)} %bitcast.42, f32[24,24]{1,0:T(8,128)S(1)} %copy-done.1), kind=kOutput, calls=%fused_computation.10 | convolution fusion | flops 227278848 | bytes 3148032 | tf_op jit(solution)/shard_map/ab,akn->bkn/dot_general | solution.py:38
  117.9 2.0 %copy.24 = bf16[24,32,1024]{2,1,0:T(8,128)(2,1)} copy(bf16[24,32,1024]{2,0,1:T(8,128)(2,1)S(1)} %fusion.11) | data formatting | bytes 3145728 | tf_op jit(solution)/shard_map/convert_element_type | solution.py:40
  119.9 3.6 %all-to-all-start.3 = ((bf16[8,3,32,1024]{3,2,1,0:T(8,128)(2,1)}), bf16[8,3,32,1024]{3,2,1,0:T(8,128)(2,1)S(1)}, u32[]{:S(2)}, u32[]{:S(2)}) async-start(bf16[8,3,32,1024]{3,2,1,0:T(8,128)(2,1)} %bitcast.13), calls=%async_computation.3 | async-start | bytes 3145728 | tf_op jit(solution)/shard_map/all_to_all | solution.py:42
  123.5 0.7 add_compare_fusion.1
  124.2 0.7 add_compare_fusion
  124.8 20.1 %all-to-all-done.3 = bf16[8,3,32,1024]{3,2,1,0:T(8,128)(2,1)S(1)} async-done(((bf16[8,3,32,1024]{3,2,1,0:T(8,128)(2,1)}), bf16[8,3,32,1024]{3,2,1,0:T(8,128)(2,1)S(1)}, u32[]{:S(2)}, u32[]{:S(2)}) %all-to-all-start.3) | async-done | bytes 1572896 | tf_op jit(solution)/shard_map/all_to_all | solution.py:42
  145.0 4.6 %fusion.8 = f32[8,32,4,256,1]{3,1,4,0,2:T(8,128)S(1)} fusion(bf16[4,3,256,1024,1]{3,2,1,4,0:T(8,128)(2,1)} %bitcast.49, bf16[8,3,32,1024]{3,2,1,0:T(8,128)(2,1)S(1)} %all-to-all-done.3), kind=kOutput, calls=%fused_computation.7 | convolution fusion | flops 1610612736 | bytes 8912896 | tf_op jit(solution)/shard_map/mbil,qbjl->miqj/dot_general | solution.py:44
  149.6 0.2 and_select_fusion.1
  149.8 18.4 %all_to_all.47 = f32[8,128,256]{2,1,0:T(8,128)S(1)} all-to-all(f32[8,128,256]{2,1,0:T(8,128)S(1)} %bitcast.43), channel_id=1, replica_groups=mesh['mpo'=8,'sg'=16,'k'=4] {'mpo'}, dimensions={0} | all-to-all | bytes 2097152 | tf_op jit(solution)/shard_map/all_to_all | solution.py:52
  168.2 1.9 %collective-permute-start = (bf16[128,256]{1,0:T(8,128)(2,1)S(1)}, bf16[128,256]{1,0:T(8,128)(2,1)S(1)}, u32[]{:S(2)}, u32[]{:S(2)}) collective-permute-start(bf16[128,256]{1,0:T(8,128)(2,1)S(1)} %reduce_sum.19), channel_id=1, source_target_pairs={{0,0},{1,128},{2,256},{3,384},{4,4},{5,132},{6,260},{7,388},{8,8},... | collective-permute-start | bytes 196616 | tf_op jit(solution)/shard_map/ppermute | solution.py:61
  170.2 7.5 %collective-permute-done = bf16[128,256]{1,0:T(8,128)(2,1)S(1)} collective-permute-done((bf16[128,256]{1,0:T(8,128)(2,1)S(1)}, bf16[128,256]{1,0:T(8,128)(2,1)S(1)}, u32[]{:S(2)}, u32[]{:S(2)}) %collective-permute-start) | collective-permute-done | bytes 65568 | tf_op jit(solution)/shard_map/ppermute | solution.py:61
  177.7 0.6 copy.38
  (10 shorter events, 0.1 us)
Async XLA Ops:
  6.5 81.7 %copy-start = (bf16[3,256,1024]{2,1,0:T(8,128)(2,1)S(1)}, bf16[3,256,1024]{2,1,0:T(8,128)(2,1)}, u32[]{:S(2)}) copy-start(bf16[3,256,1024]{2,1,0:T(8,128)(2,1)} %param.6) | copy-start | bytes 4718596
  6.5 138.4 %all-gather.3.cloned.1.call-start = ((), (), s32[]{:S(2)}) async-start(), calls=%async_computation.5 | async-start | bytes 7864320 | tf_op jit(solution)/shard_map/all_gather | solution.py:20
  52.4 4.6 %copy-start.2 = (s32[16]{0:T(128)S(1)}, s32[16]{0:T(128)}, u32[]{:S(2)}) copy-start(s32[16]{0:T(128)} %param.9) | copy-start | bytes 196
  52.4 31.9 %all-to-all-start.1 = ((bf16[8,1024,128]{2,1,0:T(8,128)(2,1)}), bf16[8,1024,128]{2,1,0:T(8,128)(2,1)}, u32[]{:S(2)}, u32[]{:S(2)}) async-start(bf16[8,1024,128]{2,1,0:T(8,128)(2,1)} %broadcast_in_dim.30), calls=%async_computation.1 | async-start | bytes 4194304 | tf_op jit(solution)/shard_map/all_to_all | solution.py:27
  91.9 24.0 %copy-start.1 = (f32[24,24]{1,0:T(8,128)S(1)}, f32[24,24]{1,0:T(8,128)}, u32[]{:S(2)}) copy-start(f32[24,24]{1,0:T(8,128)} %param.8) | copy-start | bytes 6916
  119.9 25.1 %all-to-all-start.3 = ((bf16[8,3,32,1024]{3,2,1,0:T(8,128)(2,1)}), bf16[8,3,32,1024]{3,2,1,0:T(8,128)(2,1)S(1)}, u32[]{:S(2)}, u32[]{:S(2)}) async-start(bf16[8,3,32,1024]{3,2,1,0:T(8,128)(2,1)} %bitcast.13), calls=%async_computation.3 | async-start | bytes 3145728 | tf_op jit(solution)/shard_map/all_to_all | solution.py:42
  168.2 9.5 %collective-permute-start = (bf16[128,256]{1,0:T(8,128)(2,1)S(1)}, bf16[128,256]{1,0:T(8,128)(2,1)S(1)}, u32[]{:S(2)}, u32[]{:S(2)}) collective-permute-start(bf16[128,256]{1,0:T(8,128)(2,1)S(1)} %reduce_sum.19), channel_id=1, source_target_pairs={{0,0},{1,128},{2,256},{3,384},{4,4},{5,132},{6,260},{7,388},{8,8},... | collective-permute-start | bytes 196616 | tf_op jit(solution)/shard_map/ppermute | solution.py:61
Sparse Core Ops, SparseCore 0:
  9.4 131.1 all-gather.2

commit v9 on v8

--- a/solution.py
+++ b/solution.py
@@ -35,10 +35,10 @@
     sub = slab // n_mpo
     product = product.reshape(local_w, n_mpo, sub, width)
     all_a = lax.all_to_all(product, "mpo", 1, 0, tiled=True).reshape(local_w * n_mpo, sub, width)
-    mixed = jnp.einsum(
-        "ab,akn->bkn", mpo_core, all_a.astype(jnp.float32), precision=lax.Precision.HIGHEST
+    core_g = mpo_core.reshape(local_w * n_mpo, n_mpo, local_w)
+    mixed = jnp.sum(
+        core_g[:, :, :, None, None] * all_a.astype(jnp.float32)[:, None, None], axis=0
     ).astype(jnp.bfloat16)
-    mixed = mixed.reshape(n_mpo, local_w, sub, width)
     own_b = lax.all_to_all(mixed, "mpo", 0, 0, tiled=False)
 
     term = jnp.einsum(

time: 186 us -> 193 us (1.038)
  blocking collectives: 85 us -> 61 us
  waiting for transfers between devices: 54.4 us -> 75.7 us
  other arithmetic: 2.84 us -> 12.3 us
  starting transfers between devices: 10.1 us -> 13.9 us
    all_to_all x1 -> x0, blocking collectives: 24 us -> none  [on_device(): lax.all_to_all(product, 'mpo', 1, 0, tiled=True)]
    all_to_all x0 -> x1, waiting for transfers between devices: none -> 21.4 us  [on_device(): lax.all_to_all(product, 'mpo', 1, 0, tiled=True)]
    reduce_sum x0 -> x1, other arithmetic: none -> 9.06 us  [on_device(): jnp.sum(core_g[:, :, :, None, None] * all_a.astype(jnp.float32)[:, None,...]
    all_to_all x0 -> x1, starting transfers between devices: none -> 3.71 us  [on_device(): lax.all_to_all(product, 'mpo', 1, 0, tiled=True)]
    convert_element_type x1 -> x0, local copies, waits for them, and re-layouts: 2.02 us -> none  [on_device(): mixed = jnp.einsum('ab,akn->bkn', mpo_core, all_a.astype(jnp.float32), pr...]
    dot_general x1 -> x0, matrix products: 1.95 us -> none  [on_device(): jnp.einsum('ab,akn->bkn', mpo_core, all_a.astype(jnp.float32), precision=...]
  transfers between devices with their start and end apart: 4 -> 5, of which waited for: 3 -> 4; matrix products, arithmetic and copies ran while one was open for 9% -> 12% of each run, Pallas kernels for 0% -> 0%
where the time goes in v9:
time: 193 us
  waiting for transfers between devices  75.7 us (39%)
  blocking collectives  61 us (32%)
  starting transfers between devices  13.9 us (7%)
  between operations  13.5 us (7%)
  other arithmetic  12.3 us (6%)
  local copies, waits for them, and re-layouts  8.4 us (4%)
  matrix products  8.09 us (4%)
    all_to_all x1, blocking collectives, on_device(): lax.all_to_all(spread, ('sg', 'k'), 0, 0, tiled=True).reshape(width, per)  42.6 us
    all_to_all x1, waiting for transfers between devices, on_device(): lax.all_to_all(everyone, 'mpo', 0, 2, tiled=True).reshape(width, width)  26 us
    all_to_all x1, waiting for transfers between devices, on_device(): lax.all_to_all(product, 'mpo', 1, 0, tiled=True)  21.4 us
    all_to_all x1, waiting for transfers between devices, on_device(): own_b = lax.all_to_all(mixed, 'mpo', 0, 0, tiled=False)  20.1 us
    all_to_all x1, blocking collectives, on_device(): lax.all_to_all(term, 'mpo', 0, 0, tiled=False)  18.4 us
    reduce_sum x1, other arithmetic, on_device(): jnp.sum(core_g[:, :, :, None, None] * all_a.astype(jnp.float32)[:, None,...  9.06 us
    ppermute x1, waiting for transfers between devices, on_device(): return lax.ppermute(result, ('mpo', 'sg', 'k'), pairs)  7.53 us
    all_to_all x1, starting transfers between devices, on_device(): lax.all_to_all(everyone, 'mpo', 0, 2, tiled=True).reshape(width, width)  4.64 us
  transfers between devices with their start and end apart: 5, of which 4 were waited for; matrix products, arithmetic and copies ran while one was open for 12% of the time, Pallas kernels for 0%

profile of v9, /device:TPU:70, one launch (start us, length us, event | category | flops | bytes accessed | tf_op | source)
XLA Modules:
  0.0 192.9 jit_solution(4214644442632814499)
XLA Ops:
  6.5 0.7 all-gather.3.cloned.1.call-update
  7.3 0.8 constant_dynamic-slice_fusion
  8.2 42.6 %all_to_all.39 = bf16[64,16,128]{2,1,0:T(8,128)(2,1)S(1)} all-to-all(bf16[64,16,128]{2,1,0:T(8,128)(2,1)S(1)} %bitcast.42), channel_id=1, replica_groups=mesh['mpo'=8,'sg'=16,'k'=4] {'sg','k'}, dimensions={0} | all-to-all | bytes 524288 | tf_op jit(solution)/shard_map/all_to_all | solution.py:25
  50.8 1.6 broadcast_in_dim.31
  52.4 4.6 %all-to-all-start.1 = ((bf16[8,1024,128]{2,1,0:T(8,128)(2,1)}), bf16[8,1024,128]{2,1,0:T(8,128)(2,1)}, u32[]{:S(2)}, u32[]{:S(2)}) async-start(bf16[8,1024,128]{2,1,0:T(8,128)(2,1)} %broadcast_in_dim.31), calls=%async_computation.1 | async-start | bytes 4194304 | tf_op jit(solution)/shard_map/all_to_all | solution.py:27
  57.0 0.6 fusion.11
  57.7 0.6 iota_compare_fusion
  58.3 26.0 %all-to-all-done.1 = bf16[8,1024,128]{2,1,0:T(8,128)(2,1)} async-done(((bf16[8,1024,128]{2,1,0:T(8,128)(2,1)}), bf16[8,1024,128]{2,1,0:T(8,128)(2,1)}, u32[]{:S(2)}, u32[]{:S(2)}) %all-to-all-start.1) | async-done | bytes 2097184 | tf_op jit(solution)/shard_map/all_to_all | solution.py:27
  84.3 3.9 %copy.22 = bf16[8,1024,128]{1,2,0:T(8,128)(2,1)} copy(bf16[8,1024,128]{2,1,0:T(8,128)(2,1)} %all-to-all-done.1) | data formatting | bytes 4194304 | tf_op jit(solution)/shard_map/all_to_all | solution.py:27
  88.2 3.5 %fusion.5 = bf16[1024,3,256]{0,2,1:T(8,128)(2,1)S(1)} fusion(bf16[3,256,1024]{2,1,0:T(8,128)(2,1)S(1)} %copy-done, bf16[1024,1024]{0,1:T(8,128)(2,1)} %bitcast.39, pred[1024]{0:T(1024)(128)(4,1)S(1)} %iota_compare_fusion), kind=kOutput, calls=%fused_computation.6 | convolution fusion | flops 1613496320 | bytes 5243904 | tf_op jit(solution)/shard_map/akm,mn->akn/dot_general | solution.py:32
  91.7 1.3 copy.24
  93.0 3.7 %all-to-all-start.2 = ((bf16[3,8,32,1024]{3,2,0,1:T(8,128)(2,1)}), bf16[3,8,32,1024]{3,2,0,1:T(8,128)(2,1)S(1)}, u32[]{:S(2)}, u32[]{:S(2)}) async-start(bf16[3,8,32,1024]{3,2,0,1:T(8,128)(2,1)} %copy.24), calls=%async_computation.2 | async-start | bytes 3145728 | tf_op jit(solution)/shard_map/all_to_all | solution.py:37
  96.8 21.4 %all-to-all-done.2 = bf16[3,8,32,1024]{3,2,0,1:T(8,128)(2,1)S(1)} async-done(((bf16[3,8,32,1024]{3,2,0,1:T(8,128)(2,1)}), bf16[3,8,32,1024]{3,2,0,1:T(8,128)(2,1)S(1)}, u32[]{:S(2)}, u32[]{:S(2)}) %all-to-all-start.2) | async-done | bytes 1572896 | tf_op jit(solution)/shard_map/all_to_all | solution.py:37
  118.2 0.4 bitcast_convert_fusion
  118.6 9.1 %multiply_reduce_fusion = bf16[8,3,32,1024]{3,2,1,0:T(8,128)(2,1)} fusion(f32[24,32,1024]{2,1,0:T(8,128)S(1)} %bitcast.37, f32[24,8,3]{2,1,0:T(8,128)S(1)} %reshape.68), kind=kLoop, calls=%fused_computation | loop fusion | flops 36962304 | bytes 4720896 | tf_op jit(solution)/shard_map/reduce_sum | solution.py:39
  127.6 3.6 %all-to-all-start.3 = ((bf16[8,3,32,1024]{3,2,1,0:T(8,128)(2,1)}), bf16[8,3,32,1024]{3,2,1,0:T(8,128)(2,1)S(1)}, u32[]{:S(2)}, u32[]{:S(2)}) async-start(bf16[8,3,32,1024]{3,2,1,0:T(8,128)(2,1)} %multiply_reduce_fusion), calls=%async_computation.3 | async-start | bytes 3145728 | tf_op jit(solution)/shard_map/all_to_all | solution.py:42
  131.2 0.7 add_compare_fusion.1
  131.9 0.7 add_compare_fusion
  132.5 20.1 %all-to-all-done.3 = bf16[8,3,32,1024]{3,2,1,0:T(8,128)(2,1)S(1)} async-done(((bf16[8,3,32,1024]{3,2,1,0:T(8,128)(2,1)}), bf16[8,3,32,1024]{3,2,1,0:T(8,128)(2,1)S(1)}, u32[]{:S(2)}, u32[]{:S(2)}) %all-to-all-start.3) | async-done | bytes 1572896 | tf_op jit(solution)/shard_map/all_to_all | solution.py:42
  152.7 4.6 %fusion.8 = f32[8,32,4,256,1]{3,1,4,0,2:T(8,128)S(1)} fusion(bf16[4,3,256,1024,1]{3,2,1,4,0:T(8,128)(2,1)} %bitcast.44, bf16[8,3,32,1024]{3,2,1,0:T(8,128)(2,1)S(1)} %all-to-all-done.3), kind=kOutput, calls=%fused_computation.8 | convolution fusion | flops 1610612736 | bytes 8912896 | tf_op jit(solution)/shard_map/mbil,qbjl->miqj/dot_general | solution.py:44
  157.5 18.4 %all_to_all.40 = f32[8,128,256]{2,1,0:T(8,128)S(1)} all-to-all(f32[8,128,256]{2,1,0:T(8,128)S(1)} %bitcast.38), channel_id=1, replica_groups=mesh['mpo'=8,'sg'=16,'k'=4] {'mpo'}, dimensions={0} | all-to-all | bytes 2097152 | tf_op jit(solution)/shard_map/all_to_all | solution.py:52
  176.0 1.9 collective-permute-start
  177.9 7.5 %collective-permute-done = bf16[128,256]{1,0:T(8,128)(2,1)S(1)} collective-permute-done((bf16[128,256]{1,0:T(8,128)(2,1)S(1)}, bf16[128,256]{1,0:T(8,128)(2,1)S(1)}, u32[]{:S(2)}, u32[]{:S(2)}) %collective-permute-start) | collective-permute-done | bytes 65568 | tf_op jit(solution)/shard_map/ppermute | solution.py:61
  185.4 0.6 copy.32
  (12 shorter events, 0.4 us)
Async XLA Ops:
  6.5 81.7 %copy-start = (bf16[3,256,1024]{2,1,0:T(8,128)(2,1)S(1)}, bf16[3,256,1024]{2,1,0:T(8,128)(2,1)}, u32[]{:S(2)}) copy-start(bf16[3,256,1024]{2,1,0:T(8,128)(2,1)} %param.6) | copy-start | bytes 4718596
  6.5 146.2 %all-gather.3.cloned.1.call-start = ((), (), s32[]{:S(2)}) async-start(), calls=%async_computation.5 | async-start | bytes 7864320 | tf_op jit(solution)/shard_map/all_gather | solution.py:20
  52.4 4.6 %copy-start.2 = (s32[16]{0:T(128)S(1)}, s32[16]{0:T(128)}, u32[]{:S(2)}) copy-start(s32[16]{0:T(128)} %param.9) | copy-start | bytes 196
  52.4 31.9 %all-to-all-start.1 = ((bf16[8,1024,128]{2,1,0:T(8,128)(2,1)}), bf16[8,1024,128]{2,1,0:T(8,128)(2,1)}, u32[]{:S(2)}, u32[]{:S(2)}) async-start(bf16[8,1024,128]{2,1,0:T(8,128)(2,1)} %broadcast_in_dim.31), calls=%async_computation.1 | async-start | bytes 4194304 | tf_op jit(solution)/shard_map/all_to_all | solution.py:27
  93.0 3.7 %copy-start.1 = (f32[24,24]{1,0:T(8,128)S(1)}, f32[24,24]{1,0:T(8,128)}, u32[]{:S(2)}) copy-start(f32[24,24]{1,0:T(8,128)} %param.8) | copy-start | bytes 6916
  93.0 25.2 %all-to-all-start.2 = ((bf16[3,8,32,1024]{3,2,0,1:T(8,128)(2,1)}), bf16[3,8,32,1024]{3,2,0,1:T(8,128)(2,1)S(1)}, u32[]{:S(2)}, u32[]{:S(2)}) async-start(bf16[3,8,32,1024]{3,2,0,1:T(8,128)(2,1)} %copy.24), calls=%async_computation.2 | async-start | bytes 3145728 | tf_op jit(solution)/shard_map/all_to_all | solution.py:37
  127.6 25.1 %all-to-all-start.3 = ((bf16[8,3,32,1024]{3,2,1,0:T(8,128)(2,1)}), bf16[8,3,32,1024]{3,2,1,0:T(8,128)(2,1)S(1)}, u32[]{:S(2)}, u32[]{:S(2)}) async-start(bf16[8,3,32,1024]{3,2,1,0:T(8,128)(2,1)} %multiply_reduce_fusion), calls=%async_computation.3 | async-start | bytes 3145728 | tf_op jit(solution)/shard_map/all_to_all | solution.py:42
  176.0 9.5 %collective-permute-start = (bf16[128,256]{1,0:T(8,128)(2,1)S(1)}, bf16[128,256]{1,0:T(8,128)(2,1)S(1)}, u32[]{:S(2)}, u32[]{:S(2)}) collective-permute-start(bf16[128,256]{1,0:T(8,128)(2,1)S(1)} %reduce_sum.29), channel_id=1, source_target_pairs={{0,0},{1,128},{2,256},{3,384},{4,4},{5,132},{6,260},{7,388},{8,8},... | collective-permute-start | bytes 196616 | tf_op jit(solution)/shard_map/ppermute | solution.py:61
Sparse Core Ops, SparseCore 0:
  9.4 131.1 all-gather.2

commit v10 on v8

--- a/solution.py
+++ b/solution.py
@@ -23,14 +23,15 @@
     sel = lax.dynamic_slice_in_dim(theta, mm * per, per, axis=2)
     spread = jnp.broadcast_to(sel[:, None], (sectors, G, rows_local, per)).reshape(sectors * G, rows_local, per)
     part = lax.all_to_all(spread, ("sg", "k"), 0, 0, tiled=True).reshape(width, per)
-    everyone = jnp.broadcast_to(part[None], (n_mpo,) + part.shape)
-    block = lax.all_to_all(everyone, "mpo", 0, 2, tiled=True).reshape(width, width)
+    part_t = part.T
+    everyone = jnp.broadcast_to(part_t[None], (n_mpo,) + part_t.shape)
+    block_t = lax.all_to_all(everyone, "mpo", 0, 0, tiled=True).reshape(width, width)
     positions = jnp.arange(width, dtype=jnp.int32)
     keep = positions < live_size
-    block = jnp.where(keep[:, None] & keep[None, :], block, jnp.zeros_like(block))
+    block_t = jnp.where(keep[:, None] & keep[None, :], block_t, jnp.zeros_like(block_t))
 
     product = jnp.einsum(
-        "akm,mn->akn", env_left, block, preferred_element_type=jnp.float32
+        "akm,nm->akn", env_left, block_t, preferred_element_type=jnp.float32
     ).astype(jnp.bfloat16)
     sub = slab // n_mpo
     product = product.reshape(local_w, n_mpo, sub, width)

time: 186 us -> 183 us (0.984)
  local copies, waits for them, and re-layouts: 9.25 us -> 5.47 us
    all_to_all x1 -> x0, local copies, waits for them, and re-layouts: 3.91 us -> none  [on_device(): lax.all_to_all(everyone, 'mpo', 0, 2, tiled=True).reshape(width, width)]
  transfers between devices with their start and end apart: 4 -> 4, of which waited for: 3 -> 3; matrix products, arithmetic and copies ran while one was open for 9% -> 7% of each run, Pallas kernels for 0% -> 0%
where the time goes in v10:
time: 183 us
  blocking collectives  86.3 us (47%)
  waiting for transfers between devices  54.4 us (30%)
  between operations  13.5 us (7%)
  starting transfers between devices  10.1 us (6%)
  matrix products  10.1 us (6%)
  local copies, waits for them, and re-layouts  5.47 us (3%)
  other arithmetic  2.84 us (2%)
    all_to_all x1, blocking collectives, on_device(): lax.all_to_all(spread, ('sg', 'k'), 0, 0, tiled=True).reshape(width, per)  42.6 us
    all_to_all x1, waiting for transfers between devices, on_device(): lax.all_to_all(everyone, 'mpo', 0, 0, tiled=True).reshape(width, width)  26 us
    all_to_all x1, blocking collectives, on_device(): lax.all_to_all(product, 'mpo', 1, 0, tiled=True)  24 us
    all_to_all x1, waiting for transfers between devices, on_device(): own_b = lax.all_to_all(mixed, 'mpo', 0, 0, tiled=False)  20.1 us
    all_to_all x1, blocking collectives, on_device(): lax.all_to_all(term, 'mpo', 0, 0, tiled=False)  19.6 us
    ppermute x1, waiting for transfers between devices, on_device(): return lax.ppermute(result, ('mpo', 'sg', 'k'), pairs)  7.53 us
    all_to_all x1, starting transfers between devices, on_device(): lax.all_to_all(everyone, 'mpo', 0, 0, tiled=True).reshape(width, width)  4.64 us
    dot_general x1, matrix products, on_device(): jnp.einsum('mbil,qbjl->miqj', own_b, right_all, preferred_element_type=jn...  4.6 us
  transfers between devices with their start and end apart: 4, of which 3 were waited for; matrix products, arithmetic and copies ran while one was open for 7% of the time, Pallas kernels for 0%

profile of v10, /device:TPU:70, one launch (start us, length us, event | category | flops | bytes accessed | tf_op | source)
XLA Modules:
  0.0 182.7 jit_solution(17920566921717629497)
XLA Ops:
  6.5 0.7 all-gather.3.cloned.1.call-update
  7.3 0.8 constant_dynamic-slice_fusion
  8.2 42.6 %all_to_all.35 = bf16[64,16,128]{2,1,0:T(8,128)(2,1)S(1)} all-to-all(bf16[64,16,128]{2,1,0:T(8,128)(2,1)S(1)} %bitcast.43), channel_id=1, replica_groups=mesh['mpo'=8,'sg'=16,'k'=4] {'sg','k'}, dimensions={0} | all-to-all | bytes 524288 | tf_op jit(solution)/shard_map/all_to_all | solution.py:25
  50.8 0.1 copy.16
  50.9 1.6 broadcast_in_dim.14
  52.5 4.6 %all-to-all-start.1 = ((bf16[8,128,1024]{2,1,0:T(8,128)(2,1)}), bf16[8,128,1024]{2,1,0:T(8,128)(2,1)}, u32[]{:S(2)}, u32[]{:S(2)}) async-start(bf16[8,128,1024]{2,1,0:T(8,128)(2,1)} %broadcast_in_dim.14), calls=%async_computation.1 | async-start | bytes 4194304 | tf_op jit(solution)/shard_map/all_to_all | solution.py:28
  57.2 0.6 fusion.16
  57.8 0.6 iota_compare_fusion
  58.5 26.0 %all-to-all-done.1 = bf16[8,128,1024]{2,1,0:T(8,128)(2,1)} async-done(((bf16[8,128,1024]{2,1,0:T(8,128)(2,1)}), bf16[8,128,1024]{2,1,0:T(8,128)(2,1)}, u32[]{:S(2)}, u32[]{:S(2)}) %all-to-all-start.1) | async-done | bytes 2097184 | tf_op jit(solution)/shard_map/all_to_all | solution.py:28
  84.5 3.5 %fusion.5 = bf16[1024,3,256]{0,2,1:T(8,128)(2,1)S(1)} fusion(bf16[3,256,1024]{2,1,0:T(8,128)(2,1)S(1)} %copy-done, bf16[1024,1024]{1,0:T(8,128)(2,1)} %bitcast.3, pred[1024]{0:T(1024)(128)(4,1)S(1)} %iota_compare_fusion), kind=kOutput, calls=%fused_computation.5 | convolution fusion | flops 1613496320 | bytes 5243904 | tf_op jit(solution)/shard_map/akm,nm->akn/dot_general | solution.py:33
  88.0 0.2 copy.17
  88.2 24.0 %all_to_all.36 = bf16[3,8,32,1024]{3,2,0,1:T(8,128)(2,1)S(1)} all-to-all(bf16[3,8,32,1024]{3,2,0,1:T(8,128)(2,1)S(1)} %copy.17), channel_id=1, replica_groups=mesh['mpo'=8,'sg'=16,'k'=4] {'mpo'}, dimensions={1} | all-to-all | bytes 3145728 | tf_op jit(solution)/shard_map/all_to_all | solution.py:38
  112.2 2.0 %fusion.11 = bf16[24,32,1024]{2,0,1:T(8,128)(2,1)S(1)} fusion(bf16[24,32,1024]{2,1,0:T(8,128)(2,1)S(1)} %bitcast.40, f32[24,24]{1,0:T(8,128)S(1)} %copy-done.1), kind=kOutput, calls=%fused_computation.10 | convolution fusion | flops 227278848 | bytes 3148032 | tf_op jit(solution)/shard_map/ab,akn->bkn/dot_general | solution.py:39
  114.1 2.0 %copy.20 = bf16[24,32,1024]{2,1,0:T(8,128)(2,1)} copy(bf16[24,32,1024]{2,0,1:T(8,128)(2,1)S(1)} %fusion.11) | data formatting | bytes 3145728 | tf_op jit(solution)/shard_map/convert_element_type | solution.py:41
  116.2 3.6 %all-to-all-start.3 = ((bf16[8,3,32,1024]{3,2,1,0:T(8,128)(2,1)}), bf16[8,3,32,1024]{3,2,1,0:T(8,128)(2,1)S(1)}, u32[]{:S(2)}, u32[]{:S(2)}) async-start(bf16[8,3,32,1024]{3,2,1,0:T(8,128)(2,1)} %bitcast.12), calls=%async_computation.3 | async-start | bytes 3145728 | tf_op jit(solution)/shard_map/all_to_all | solution.py:43
  119.8 0.7 add_compare_fusion.1
  120.4 0.7 add_compare_fusion
  121.1 20.1 %all-to-all-done.3 = bf16[8,3,32,1024]{3,2,1,0:T(8,128)(2,1)S(1)} async-done(((bf16[8,3,32,1024]{3,2,1,0:T(8,128)(2,1)}), bf16[8,3,32,1024]{3,2,1,0:T(8,128)(2,1)S(1)}, u32[]{:S(2)}, u32[]{:S(2)}) %all-to-all-start.3) | async-done | bytes 1572896 | tf_op jit(solution)/shard_map/all_to_all | solution.py:43
  141.2 4.6 %fusion.8 = f32[8,32,4,256,1]{3,1,4,0,2:T(8,128)S(1)} fusion(bf16[4,3,256,1024,1]{3,2,1,4,0:T(8,128)(2,1)} %bitcast.46, bf16[8,3,32,1024]{3,2,1,0:T(8,128)(2,1)S(1)} %all-to-all-done.3), kind=kOutput, calls=%fused_computation.7 | convolution fusion | flops 1610612736 | bytes 8912896 | tf_op jit(solution)/shard_map/mbil,qbjl->miqj/dot_general | solution.py:45
  145.8 0.2 and_select_fusion.1
  146.0 19.6 %all_to_all.37 = f32[8,128,256]{2,1,0:T(8,128)S(1)} all-to-all(f32[8,128,256]{2,1,0:T(8,128)S(1)} %bitcast.41), channel_id=1, replica_groups=mesh['mpo'=8,'sg'=16,'k'=4] {'mpo'}, dimensions={0} | all-to-all | bytes 2097152 | tf_op jit(solution)/shard_map/all_to_all | solution.py:53
  165.7 1.9 %collective-permute-start = (bf16[128,256]{1,0:T(8,128)(2,1)S(1)}, bf16[128,256]{1,0:T(8,128)(2,1)S(1)}, u32[]{:S(2)}, u32[]{:S(2)}) collective-permute-start(bf16[128,256]{1,0:T(8,128)(2,1)S(1)} %reduce_sum.19), channel_id=1, source_target_pairs={{0,0},{1,128},{2,256},{3,384},{4,4},{5,132},{6,260},{7,388},{8,8},... | collective-permute-start | bytes 196616 | tf_op jit(solution)/shard_map/ppermute | solution.py:62
  167.6 7.5 %collective-permute-done = bf16[128,256]{1,0:T(8,128)(2,1)S(1)} collective-permute-done((bf16[128,256]{1,0:T(8,128)(2,1)S(1)}, bf16[128,256]{1,0:T(8,128)(2,1)S(1)}, u32[]{:S(2)}, u32[]{:S(2)}) %collective-permute-start) | collective-permute-done | bytes 65568 | tf_op jit(solution)/shard_map/ppermute | solution.py:62
  175.2 0.6 copy.32
  (10 shorter events, 0.1 us)
Async XLA Ops:
  6.5 77.9 %copy-start = (bf16[3,256,1024]{2,1,0:T(8,128)(2,1)S(1)}, bf16[3,256,1024]{2,1,0:T(8,128)(2,1)}, u32[]{:S(2)}) copy-start(bf16[3,256,1024]{2,1,0:T(8,128)(2,1)} %param.6) | copy-start | bytes 4718596
  6.5 134.7 %all-gather.3.cloned.1.call-start = ((), (), s32[]{:S(2)}) async-start(), calls=%async_computation.5 | async-start | bytes 7864320 | tf_op jit(solution)/shard_map/all_gather | solution.py:20
  52.5 4.6 %copy-start.2 = (s32[16]{0:T(128)S(1)}, s32[16]{0:T(128)}, u32[]{:S(2)}) copy-start(s32[16]{0:T(128)} %param.9) | copy-start | bytes 196
  52.5 31.9 %all-to-all-start.1 = ((bf16[8,128,1024]{2,1,0:T(8,128)(2,1)}), bf16[8,128,1024]{2,1,0:T(8,128)(2,1)}, u32[]{:S(2)}, u32[]{:S(2)}) async-start(bf16[8,128,1024]{2,1,0:T(8,128)(2,1)} %broadcast_in_dim.14), calls=%async_computation.1 | async-start | bytes 4194304 | tf_op jit(solution)/shard_map/all_to_all | solution.py:28
  88.1 24.0 %copy-start.1 = (f32[24,24]{1,0:T(8,128)S(1)}, f32[24,24]{1,0:T(8,128)}, u32[]{:S(2)}) copy-start(f32[24,24]{1,0:T(8,128)} %param.8) | copy-start | bytes 6916
  116.2 25.1 %all-to-all-start.3 = ((bf16[8,3,32,1024]{3,2,1,0:T(8,128)(2,1)}), bf16[8,3,32,1024]{3,2,1,0:T(8,128)(2,1)S(1)}, u32[]{:S(2)}, u32[]{:S(2)}) async-start(bf16[8,3,32,1024]{3,2,1,0:T(8,128)(2,1)} %bitcast.12), calls=%async_computation.3 | async-start | bytes 3145728 | tf_op jit(solution)/shard_map/all_to_all | solution.py:43
  165.7 9.5 %collective-permute-start = (bf16[128,256]{1,0:T(8,128)(2,1)S(1)}, bf16[128,256]{1,0:T(8,128)(2,1)S(1)}, u32[]{:S(2)}, u32[]{:S(2)}) collective-permute-start(bf16[128,256]{1,0:T(8,128)(2,1)S(1)} %reduce_sum.19), channel_id=1, source_target_pairs={{0,0},{1,128},{2,256},{3,384},{4,4},{5,132},{6,260},{7,388},{8,8},... | collective-permute-start | bytes 196616 | tf_op jit(solution)/shard_map/ppermute | solution.py:62
Sparse Core Ops, SparseCore 0:
  9.4 131.1 all-gather.2

commit v11 on v10

--- a/solution.py
+++ b/solution.py
@@ -45,12 +45,15 @@
     term = jnp.einsum(
         "mbil,qbjl->miqj", own_b, right_all, preferred_element_type=jnp.float32
     ).reshape(slab, width)
-    row_keep = k * slab + jnp.arange(slab, dtype=jnp.int32) < live_size
-    term = jnp.where(row_keep[:, None] & keep[None, :], term, jnp.zeros_like(term))
     halves = n_mpo // G
     term = term.reshape(halves, slab // halves, G, slab)
     term = jnp.transpose(term, (2, 0, 1, 3)).reshape(n_mpo, slab // halves, slab)
-    result = jnp.sum(lax.all_to_all(term, "mpo", 0, 0, tiled=False), axis=0).astype(jnp.bfloat16)
+    summed = jnp.sum(lax.all_to_all(term, "mpo", 0, 0, tiled=False), axis=0)
+    rows_out = slab // halves
+    out_rows = k * slab + (mm % halves) * rows_out + jnp.arange(rows_out, dtype=jnp.int32)
+    out_cols = (mm // halves) * slab + jnp.arange(slab, dtype=jnp.int32)
+    out_keep = (out_rows < live_size)[:, None] & (out_cols < live_size)[None, :]
+    result = jnp.where(out_keep, summed, jnp.zeros_like(summed)).astype(jnp.bfloat16)
 
     pairs = []
     for src_m in range(n_mpo):

time: 183 us -> 184 us (level)
  blocking collectives: 86.3 us -> 90.7 us
  waiting for transfers between devices: 54.4 us -> 50.5 us
    all_to_all x1, waiting for transfers between devices: 20.1 us -> 14.6 us  [on_device(): summed = jnp.sum(lax.all_to_all(term, 'mpo', 0, 0, tiled=False), axis=0)]
    all_to_all x1, blocking collectives: 19.6 us -> 24 us  [on_device(): own_b = lax.all_to_all(mixed, 'mpo', 0, 0, tiled=False)]
  transfers between devices with their start and end apart: 4 -> 4, of which waited for: 3 -> 4; matrix products, arithmetic and copies ran while one was open for 7% -> 6% of each run, Pallas kernels for 0% -> 0%
where the time goes in v11:
time: 184 us
  blocking collectives  90.7 us (49%)
  waiting for transfers between devices  50.5 us (27%)
  between operations  13.5 us (7%)
  matrix products  11.1 us (6%)
  starting transfers between devices  11 us (6%)
  local copies, waits for them, and re-layouts  4.32 us (2%)
  other arithmetic  2.74 us (1%)
    all_to_all x1, blocking collectives, on_device(): lax.all_to_all(spread, ('sg', 'k'), 0, 0, tiled=True).reshape(width, per)  42.6 us
    all_to_all x1, waiting for transfers between devices, on_device(): lax.all_to_all(everyone, 'mpo', 0, 0, tiled=True).reshape(width, width)  26 us
    all_to_all x1, blocking collectives, on_device(): lax.all_to_all(product, 'mpo', 1, 0, tiled=True)  24 us
    all_to_all x1, blocking collectives, on_device(): own_b = lax.all_to_all(mixed, 'mpo', 0, 0, tiled=False)  24 us
    all_to_all x1, waiting for transfers between devices, on_device(): summed = jnp.sum(lax.all_to_all(term, 'mpo', 0, 0, tiled=False), axis=0)  14.6 us
    ppermute x1, waiting for transfers between devices, on_device(): return lax.ppermute(result, ('mpo', 'sg', 'k'), pairs)  7.53 us
    dot_general x1, matrix products, on_device(): jnp.einsum('mbil,qbjl->miqj', own_b, right_all, preferred_element_type=jn...  5.6 us
    all_to_all x1, starting transfers between devices, on_device(): lax.all_to_all(everyone, 'mpo', 0, 0, tiled=True).reshape(width, width)  4.64 us
  transfers between devices with their start and end apart: 4, of which 4 were waited for; matrix products, arithmetic and copies ran while one was open for 6% of the time, Pallas kernels for 0%

profile of v11, /device:TPU:70, one launch (start us, length us, event | category | flops | bytes accessed | tf_op | source)
XLA Modules:
  0.0 183.7 jit_solution(7945980880319958057)
XLA Ops:
  6.5 0.7 all-gather.3.cloned.1.call-update
  7.3 0.8 constant_dynamic-slice_fusion
  8.2 42.6 %all_to_all.35 = bf16[64,16,128]{2,1,0:T(8,128)(2,1)S(1)} all-to-all(bf16[64,16,128]{2,1,0:T(8,128)(2,1)S(1)} %bitcast.44), channel_id=1, replica_groups=mesh['mpo'=8,'sg'=16,'k'=4] {'sg','k'}, dimensions={0} | all-to-all | bytes 524288 | tf_op jit(solution)/shard_map/all_to_all | solution.py:25
  50.8 0.1 copy.16
  50.9 1.6 broadcast_in_dim.14
  52.5 4.6 %all-to-all-start.1 = ((bf16[8,128,1024]{2,1,0:T(8,128)(2,1)}), bf16[8,128,1024]{2,1,0:T(8,128)(2,1)}, u32[]{:S(2)}, u32[]{:S(2)}) async-start(bf16[8,128,1024]{2,1,0:T(8,128)(2,1)} %broadcast_in_dim.14), calls=%async_computation.1 | async-start | bytes 4194304 | tf_op jit(solution)/shard_map/all_to_all | solution.py:28
  57.2 0.6 fusion.16
  57.8 0.6 iota_compare_fusion
  58.5 26.0 %all-to-all-done.1 = bf16[8,128,1024]{2,1,0:T(8,128)(2,1)} async-done(((bf16[8,128,1024]{2,1,0:T(8,128)(2,1)}), bf16[8,128,1024]{2,1,0:T(8,128)(2,1)}, u32[]{:S(2)}, u32[]{:S(2)}) %all-to-all-start.1) | async-done | bytes 2097184 | tf_op jit(solution)/shard_map/all_to_all | solution.py:28
  84.5 3.5 %fusion.5 = bf16[1024,3,256]{0,2,1:T(8,128)(2,1)S(1)} fusion(bf16[3,256,1024]{2,1,0:T(8,128)(2,1)S(1)} %copy-done, bf16[1024,1024]{1,0:T(8,128)(2,1)} %bitcast.3, pred[1024]{0:T(1024)(128)(4,1)S(1)} %iota_compare_fusion), kind=kOutput, calls=%fused_computation.5 | convolution fusion | flops 1613496320 | bytes 5243904 | tf_op jit(solution)/shard_map/akm,nm->akn/dot_general | solution.py:33
  88.0 0.2 copy.17
  88.2 24.0 %all_to_all.36 = bf16[3,8,32,1024]{3,2,0,1:T(8,128)(2,1)S(1)} all-to-all(bf16[3,8,32,1024]{3,2,0,1:T(8,128)(2,1)S(1)} %copy.17), channel_id=1, replica_groups=mesh['mpo'=8,'sg'=16,'k'=4] {'mpo'}, dimensions={1} | all-to-all | bytes 3145728 | tf_op jit(solution)/shard_map/all_to_all | solution.py:38
  112.2 2.0 %fusion.11 = bf16[24,32,1024]{2,0,1:T(8,128)(2,1)S(1)} fusion(bf16[24,32,1024]{2,1,0:T(8,128)(2,1)S(1)} %bitcast.41, f32[24,24]{1,0:T(8,128)S(1)} %copy-done.1), kind=kOutput, calls=%fused_computation.10 | convolution fusion | flops 227278848 | bytes 3148032 | tf_op jit(solution)/shard_map/ab,akn->bkn/dot_general | solution.py:39
  114.1 0.9 copy.20
  115.0 24.0 %all_to_all.37 = bf16[8,3,32,1024]{3,2,1,0:T(8,128)(2,1)S(1)} all-to-all(bf16[8,3,32,1024]{3,2,1,0:T(8,128)(2,1)S(1)} %bitcast.42), channel_id=1, replica_groups=mesh['mpo'=8,'sg'=16,'k'=4] {'mpo'}, dimensions={0} | all-to-all | bytes 3145728 | tf_op jit(solution)/shard_map/all_to_all | solution.py:43
  139.0 1.6 all-gather.3.cloned.1.call-done
  140.7 5.6 %fusion.8 = f32[8,32,4,256,1]{3,1,4,0,2:T(8,128)} fusion(bf16[4,3,256,1024,1]{3,2,1,4,0:T(8,128)(2,1)} %bitcast.47, bf16[8,3,32,1024]{3,2,1,0:T(8,128)(2,1)S(1)} %all_to_all.37), kind=kOutput, calls=%fused_computation.7 | convolution fusion | flops 1610612736 | bytes 8912896 | tf_op jit(solution)/shard_map/mbil,qbjl->miqj/dot_general | solution.py:45
  146.3 4.4 %all-to-all-start.4 = ((f32[8,128,256]{2,1,0:T(8,128)}), f32[8,128,256]{2,1,0:T(8,128)S(1)}, u32[]{:S(2)}, u32[]{:S(2)}) async-start(f32[8,128,256]{2,1,0:T(8,128)} %bitcast.45), calls=%async_computation.4 | async-start | bytes 2097152 | tf_op jit(solution)/shard_map/all_to_all | solution.py:51
  150.7 0.7 add_compare_fusion.1
  151.3 0.7 add_compare_fusion
  152.0 14.6 %all-to-all-done.4 = f32[8,128,256]{2,1,0:T(8,128)S(1)} async-done(((f32[8,128,256]{2,1,0:T(8,128)}), f32[8,128,256]{2,1,0:T(8,128)S(1)}, u32[]{:S(2)}, u32[]{:S(2)}) %all-to-all-start.4) | async-done | bytes 1048608 | tf_op jit(solution)/shard_map/all_to_all | solution.py:51
  166.8 1.9 %collective-permute-start = (bf16[128,256]{1,0:T(8,128)(2,1)S(1)}, bf16[128,256]{1,0:T(8,128)(2,1)S(1)}, u32[]{:S(2)}, u32[]{:S(2)}) collective-permute-start(bf16[128,256]{1,0:T(8,128)(2,1)S(1)} %select_convert_fusion), channel_id=1, source_target_pairs={{0,0},{1,128},{2,256},{3,384},{4,4},{5,132},{6,260},{7,388},{8,8},... | collective-permute-start | bytes 196616 | tf_op jit(solution)/shard_map/ppermute | solution.py:65
  168.7 7.5 %collective-permute-done = bf16[128,256]{1,0:T(8,128)(2,1)S(1)} collective-permute-done((bf16[128,256]{1,0:T(8,128)(2,1)S(1)}, bf16[128,256]{1,0:T(8,128)(2,1)S(1)}, u32[]{:S(2)}, u32[]{:S(2)}) %collective-permute-start) | collective-permute-done | bytes 65568 | tf_op jit(solution)/shard_map/ppermute | solution.py:65
  176.2 0.6 copy.32
  (10 shorter events, 0.2 us)
Async XLA Ops:
  6.5 77.9 %copy-start = (bf16[3,256,1024]{2,1,0:T(8,128)(2,1)S(1)}, bf16[3,256,1024]{2,1,0:T(8,128)(2,1)}, u32[]{:S(2)}) copy-start(bf16[3,256,1024]{2,1,0:T(8,128)(2,1)} %param.6) | copy-start | bytes 4718596
  6.5 134.1 %all-gather.3.cloned.1.call-start = ((), (), s32[]{:S(2)}) async-start(), calls=%async_computation.5 | async-start | bytes 7864320 | tf_op jit(solution)/shard_map/all_gather | solution.py:20
  52.5 4.6 %copy-start.2 = (s32[16]{0:T(128)S(1)}, s32[16]{0:T(128)}, u32[]{:S(2)}) copy-start(s32[16]{0:T(128)} %param.9) | copy-start | bytes 196
  52.5 31.9 %all-to-all-start.1 = ((bf16[8,128,1024]{2,1,0:T(8,128)(2,1)}), bf16[8,128,1024]{2,1,0:T(8,128)(2,1)}, u32[]{:S(2)}, u32[]{:S(2)}) async-start(bf16[8,128,1024]{2,1,0:T(8,128)(2,1)} %broadcast_in_dim.14), calls=%async_computation.1 | async-start | bytes 4194304 | tf_op jit(solution)/shard_map/all_to_all | solution.py:28
  88.1 24.0 %copy-start.1 = (f32[24,24]{1,0:T(8,128)S(1)}, f32[24,24]{1,0:T(8,128)}, u32[]{:S(2)}) copy-start(f32[24,24]{1,0:T(8,128)} %param.8) | copy-start | bytes 6916
  146.3 20.3 %all-to-all-start.4 = ((f32[8,128,256]{2,1,0:T(8,128)}), f32[8,128,256]{2,1,0:T(8,128)S(1)}, u32[]{:S(2)}, u32[]{:S(2)}) async-start(f32[8,128,256]{2,1,0:T(8,128)} %bitcast.45), calls=%async_computation.4 | async-start | bytes 2097152 | tf_op jit(solution)/shard_map/all_to_all | solution.py:51
  166.8 9.5 %collective-permute-start = (bf16[128,256]{1,0:T(8,128)(2,1)S(1)}, bf16[128,256]{1,0:T(8,128)(2,1)S(1)}, u32[]{:S(2)}, u32[]{:S(2)}) collective-permute-start(bf16[128,256]{1,0:T(8,128)(2,1)S(1)} %select_convert_fusion), channel_id=1, source_target_pairs={{0,0},{1,128},{2,256},{3,384},{4,4},{5,132},{6,260},{7,388},{8,8},... | collective-permute-start | bytes 196616 | tf_op jit(solution)/shard_map/ppermute | solution.py:65
Sparse Core Ops, SparseCore 0:
  9.4 131.1 all-gather.2

commit v12 on v10

--- a/solution.py
+++ b/solution.py
@@ -17,7 +17,10 @@
     k = lax.axis_index("k")
     live_size = jnp.sum(jnp.where(jnp.arange(sectors, dtype=jnp.int32) == sector, sector_sizes, 0))
 
-    right_all = lax.all_gather(env_right, "k", axis=0, tiled=False)
+    right_keep = k * slab + jnp.arange(slab, dtype=jnp.int32) < live_size
+    right_all = lax.all_gather(
+        jnp.where(right_keep[None, :, None], env_right, jnp.zeros_like(env_right)), "k", axis=0, tiled=False
+    )
 
     per = width // n_mpo
     sel = lax.dynamic_slice_in_dim(theta, mm * per, per, axis=2)
@@ -39,14 +42,14 @@
     mixed = jnp.einsum(
         "ab,akn->bkn", mpo_core, all_a.astype(jnp.float32), precision=lax.Precision.HIGHEST
     ).astype(jnp.bfloat16)
+    mixed_keep = k * slab + mm * sub + jnp.arange(sub, dtype=jnp.int32) < live_size
+    mixed = jnp.where(mixed_keep[None, :, None], mixed, jnp.zeros_like(mixed))
     mixed = mixed.reshape(n_mpo, local_w, sub, width)
     own_b = lax.all_to_all(mixed, "mpo", 0, 0, tiled=False)
 
     term = jnp.einsum(
         "mbil,qbjl->miqj", own_b, right_all, preferred_element_type=jnp.float32
     ).reshape(slab, width)
-    row_keep = k * slab + jnp.arange(slab, dtype=jnp.int32) < live_size
-    term = jnp.where(row_keep[:, None] & keep[None, :], term, jnp.zeros_like(term))
     halves = n_mpo // G
     term = term.reshape(halves, slab // halves, G, slab)
     term = jnp.transpose(term, (2, 0, 1, 3)).reshape(n_mpo, slab // halves, slab)

time: 183 us -> 187 us (1.022)
  other arithmetic: 2.84 us -> 6.16 us
    select_n x1, other arithmetic: 0.18 us -> 2.73 us  [on_device(): jnp.where(right_keep[None, :, None], env_right, jnp.zeros_like(env_right))]
    convert_element_type x1 -> x0, local copies, waits for them, and re-layouts: 2.02 us -> none  [on_device(): mixed = jnp.einsum('ab,akn->bkn', mpo_core, all_a.astype(jnp.float32), pr...]
  transfers between devices with their start and end apart: 4 -> 4, of which waited for: 3 -> 3; matrix products, arithmetic and copies ran while one was open for 7% -> 6% of each run, Pallas kernels for 0% -> 0%
where the time goes in v12:
time: 187 us; the launch traced here: 186 us
  blocking collectives  86.1 us (46%)
  waiting for transfers between devices  55 us (29%)
  between operations  13.5 us (7%)
  starting transfers between devices  10.2 us (5%)
  matrix products  10.1 us (5%)
  other arithmetic  6.16 us (3%)
  local copies, waits for them, and re-layouts  5.41 us (3%)
    all_to_all x1, blocking collectives, on_device(): lax.all_to_all(spread, ('sg', 'k'), 0, 0, tiled=True).reshape(width, per)  43.1 us
    all_to_all x1, waiting for transfers between devices, on_device(): lax.all_to_all(everyone, 'mpo', 0, 0, tiled=True).reshape(width, width)  26.6 us
    all_to_all x1, blocking collectives, on_device(): own_b = lax.all_to_all(mixed, 'mpo', 0, 0, tiled=False)  24 us
    all_to_all x1, waiting for transfers between devices, on_device(): lax.all_to_all(product, 'mpo', 1, 0, tiled=True)  20.8 us
    all_to_all x1, blocking collectives, on_device(): lax.all_to_all(term, 'mpo', 0, 0, tiled=False)  19 us
    ppermute x1, waiting for transfers between devices, on_device(): return lax.ppermute(result, ('mpo', 'sg', 'k'), pairs)  7.53 us
    dot_general x1, matrix products, on_device(): jnp.einsum('mbil,qbjl->miqj', own_b, right_all, preferred_element_type=jn...  4.6 us
    all_to_all x1, starting transfers between devices, on_device(): lax.all_to_all(everyone, 'mpo', 0, 0, tiled=True).reshape(width, width)  4.52 us
  transfers between devices with their start and end apart: 4, of which 3 were waited for; matrix products, arithmetic and copies ran while one was open for 6% of the time, Pallas kernels for 0%

profile of v12, /device:TPU:70, one launch (start us, length us, event | category | flops | bytes accessed | tf_op | source)
XLA Modules:
  0.0 186.4 jit_solution(11075225449568460428)
XLA Ops:
  6.5 1.4 fusion.15
  8.0 0.7 add_compare_fusion
  8.6 2.7 %broadcast_select_fusion = bf16[3,256,1024]{2,1,0:T(8,128)(2,1)} fusion(bf16[3,256,1024]{2,1,0:T(8,128)(2,1)} %param.7, pred[256]{0:T(512)(128)(4,1)S(1)} %add_compare_fusion), kind=kLoop, calls=%fused_computation.11 | loop fusion | flops 786432 | bytes 3145984 | tf_op jit(solution)/shard_map/jit(_where)/select_n | solution.py:22
  11.4 0.8 constant_dynamic-slice_fusion
  12.3 43.1 %all_to_all.35 = bf16[64,16,128]{2,1,0:T(8,128)(2,1)S(1)} all-to-all(bf16[64,16,128]{2,1,0:T(8,128)(2,1)S(1)} %bitcast.44), channel_id=1, replica_groups=mesh['mpo'=8,'sg'=16,'k'=4] {'sg','k'}, dimensions={0} | all-to-all | bytes 524288 | tf_op jit(solution)/shard_map/all_to_all | solution.py:28
  55.4 0.1 copy.16
  55.5 1.6 broadcast_in_dim.48
  57.1 4.5 %all-to-all-start.1 = ((bf16[8,128,1024]{2,1,0:T(8,128)(2,1)}), bf16[8,128,1024]{2,1,0:T(8,128)(2,1)}, u32[]{:S(2)}, u32[]{:S(2)}) async-start(bf16[8,128,1024]{2,1,0:T(8,128)(2,1)} %broadcast_in_dim.48), calls=%async_computation.1 | async-start | bytes 4194304 | tf_op jit(solution)/shard_map/all_to_all | solution.py:31
  61.7 0.6 iota_compare_fusion
  62.3 26.6 %all-to-all-done.1 = bf16[8,128,1024]{2,1,0:T(8,128)(2,1)} async-done(((bf16[8,128,1024]{2,1,0:T(8,128)(2,1)}), bf16[8,128,1024]{2,1,0:T(8,128)(2,1)}, u32[]{:S(2)}, u32[]{:S(2)}) %all-to-all-start.1) | async-done | bytes 2097184 | tf_op jit(solution)/shard_map/all_to_all | solution.py:31
  88.9 3.5 %fusion.5 = bf16[1024,3,256]{0,2,1:T(8,128)(2,1)S(1)} fusion(bf16[3,256,1024]{2,1,0:T(8,128)(2,1)S(1)} %copy-done, bf16[1024,1024]{1,0:T(8,128)(2,1)} %bitcast.3, pred[1024]{0:T(1024)(128)(4,1)S(1)} %iota_compare_fusion), kind=kOutput, calls=%fused_computation.5 | convolution fusion | flops 1613496320 | bytes 5243904 | tf_op jit(solution)/shard_map/akm,nm->akn/dot_general | solution.py:36
  92.5 1.3 copy.17
  93.7 3.7 %all-to-all-start.2 = ((bf16[3,8,32,1024]{3,2,0,1:T(8,128)(2,1)}), bf16[3,8,32,1024]{3,2,0,1:T(8,128)(2,1)S(1)}, u32[]{:S(2)}, u32[]{:S(2)}) async-start(bf16[3,8,32,1024]{3,2,0,1:T(8,128)(2,1)} %copy.17), calls=%async_computation.2 | async-start | bytes 3145728 | tf_op jit(solution)/shard_map/all_to_all | solution.py:41
  97.4 0.7 add_compare_fusion.1
  98.1 20.8 %all-to-all-done.2 = bf16[3,8,32,1024]{3,2,0,1:T(8,128)(2,1)S(1)} async-done(((bf16[3,8,32,1024]{3,2,0,1:T(8,128)(2,1)}), bf16[3,8,32,1024]{3,2,0,1:T(8,128)(2,1)S(1)}, u32[]{:S(2)}, u32[]{:S(2)}) %all-to-all-start.2) | async-done | bytes 1572896 | tf_op jit(solution)/shard_map/all_to_all | solution.py:41
  118.9 2.0 %select_bitcast_fusion = bf16[24,32,1024]{2,0,1:T(8,128)(2,1)S(1)} fusion(pred[32]{0:T(512)(128)(4,1)S(1)} %add_compare_fusion.1, bf16[24,32,1024]{2,1,0:T(8,128)(2,1)S(1)} %bitcast.42, f32[24,24]{1,0:T(8,128)S(1)} %copy-done.1), kind=kOutput, calls=%fused_computation.10 | convolution fusion | flops 228065280 | bytes 3148064 | tf_op jit(solution)/shard_map/ab,akn->bkn/dot_general | solution.py:42
  120.9 0.9 copy.20
  121.8 24.0 %all_to_all.36 = bf16[8,3,32,1024]{3,2,1,0:T(8,128)(2,1)S(1)} all-to-all(bf16[8,3,32,1024]{3,2,1,0:T(8,128)(2,1)S(1)} %bitcast.41), channel_id=1, replica_groups=mesh['mpo'=8,'sg'=16,'k'=4] {'mpo'}, dimensions={0} | all-to-all | bytes 3145728 | tf_op jit(solution)/shard_map/all_to_all | solution.py:48
  145.8 4.6 %fusion.8 = f32[8,32,4,256,1]{3,1,4,0,2:T(8,128)S(1)} fusion(bf16[4,3,256,1024,1]{3,2,1,4,0:T(8,128)(2,1)} %bitcast.47, bf16[8,3,32,1024]{3,2,1,0:T(8,128)(2,1)S(1)} %all_to_all.36), kind=kOutput, calls=%fused_computation.7 | convolution fusion | flops 1610612736 | bytes 8912896 | tf_op jit(solution)/shard_map/mbil,qbjl->miqj/dot_general | solution.py:50
  150.4 19.0 %all_to_all.37 = f32[8,128,256]{2,1,0:T(8,128)S(1)} all-to-all(f32[8,128,256]{2,1,0:T(8,128)S(1)} %bitcast.45), channel_id=1, replica_groups=mesh['mpo'=8,'sg'=16,'k'=4] {'mpo'}, dimensions={0} | all-to-all | bytes 2097152 | tf_op jit(solution)/shard_map/all_to_all | solution.py:56
  169.4 0.1 reduce_sum.19
  169.5 1.9 %collective-permute-start = (bf16[128,256]{1,0:T(8,128)(2,1)S(1)}, bf16[128,256]{1,0:T(8,128)(2,1)S(1)}, u32[]{:S(2)}, u32[]{:S(2)}) collective-permute-start(bf16[128,256]{1,0:T(8,128)(2,1)S(1)} %reduce_sum.19), channel_id=1, source_target_pairs={{0,0},{1,128},{2,256},{3,384},{4,4},{5,132},{6,260},{7,388},{8,8},... | collective-permute-start | bytes 196616 | tf_op jit(solution)/shard_map/ppermute | solution.py:65
  171.4 7.5 %collective-permute-done = bf16[128,256]{1,0:T(8,128)(2,1)S(1)} collective-permute-done((bf16[128,256]{1,0:T(8,128)(2,1)S(1)}, bf16[128,256]{1,0:T(8,128)(2,1)S(1)}, u32[]{:S(2)}, u32[]{:S(2)}) %collective-permute-start) | collective-permute-done | bytes 65568 | tf_op jit(solution)/shard_map/ppermute | solution.py:65
  178.9 0.6 copy.32
  (8 shorter events, 0.1 us)
Async XLA Ops:
  6.5 82.4 %copy-start = (bf16[3,256,1024]{2,1,0:T(8,128)(2,1)S(1)}, bf16[3,256,1024]{2,1,0:T(8,128)(2,1)}, u32[]{:S(2)}) copy-start(bf16[3,256,1024]{2,1,0:T(8,128)(2,1)} %param.6) | copy-start | bytes 4718596
  6.5 139.3 %all-gather.3.cloned.1.call-start = ((), (), s32[]{:S(2)}) async-start(), calls=%async_computation.5 | async-start | bytes 7864320 | tf_op jit(solution)/shard_map/all_gather | solution.py:21
  57.1 31.8 %all-to-all-start.1 = ((bf16[8,128,1024]{2,1,0:T(8,128)(2,1)}), bf16[8,128,1024]{2,1,0:T(8,128)(2,1)}, u32[]{:S(2)}, u32[]{:S(2)}) async-start(bf16[8,128,1024]{2,1,0:T(8,128)(2,1)} %broadcast_in_dim.48), calls=%async_computation.1 | async-start | bytes 4194304 | tf_op jit(solution)/shard_map/all_to_all | solution.py:31
  93.7 25.2 %copy-start.1 = (f32[24,24]{1,0:T(8,128)S(1)}, f32[24,24]{1,0:T(8,128)}, u32[]{:S(2)}) copy-start(f32[24,24]{1,0:T(8,128)} %param.8) | copy-start | bytes 6916
  93.7 25.2 %all-to-all-start.2 = ((bf16[3,8,32,1024]{3,2,0,1:T(8,128)(2,1)}), bf16[3,8,32,1024]{3,2,0,1:T(8,128)(2,1)S(1)}, u32[]{:S(2)}, u32[]{:S(2)}) async-start(bf16[3,8,32,1024]{3,2,0,1:T(8,128)(2,1)} %copy.17), calls=%async_computation.2 | async-start | bytes 3145728 | tf_op jit(solution)/shard_map/all_to_all | solution.py:41
  169.5 9.5 %collective-permute-start = (bf16[128,256]{1,0:T(8,128)(2,1)S(1)}, bf16[128,256]{1,0:T(8,128)(2,1)S(1)}, u32[]{:S(2)}, u32[]{:S(2)}) collective-permute-start(bf16[128,256]{1,0:T(8,128)(2,1)S(1)} %reduce_sum.19), channel_id=1, source_target_pairs={{0,0},{1,128},{2,256},{3,384},{4,4},{5,132},{6,260},{7,388},{8,8},... | collective-permute-start | bytes 196616 | tf_op jit(solution)/shard_map/ppermute | solution.py:65
Sparse Core Ops, SparseCore 0:
  11.5 133.0 all-gather.2
